TPU v7x, 256 devices: a whole 4x4x8 slice. The times are simulated.
256 devices in a mesh: section: 4 (over z_hi, core), ep: 64 (over y, x, z_lo).
Axes of the slice: x: 4, y: 4, z: 8 (z_hi: 2, z_lo: 4; z = z_hi * 4 + z_lo), core: 2. Of those that a mesh axis runs over, the one named last changes fastest.
Arguments:
- tokens: bfloat16 [4, 8192, 4096], P('section', 'ep'), may hold values from -6 to 6
- routes: int32 [4, 8192, 8], P('section', 'ep'), may hold values from 0 to 127, as said below
- router_weights: float32 [4, 8192, 8], P('section', 'ep'), may hold values from 0.25 to 1
- w_gate: bfloat16 [4, 64, 4096, 384], P('section', 'ep'), may hold values from -0.09375 to 0.09375
- w_up: bfloat16 [4, 64, 4096, 384], P('section', 'ep'), may hold values from -0.09375 to 0.09375
- w_down: bfloat16 [4, 64, 384, 4096], P('section', 'ep'), may hold values from -0.15625 to 0.15625
- w_query: bfloat16 [4, 4096, 1024], P('section', 'ep'), may hold values from -0.09375 to 0.09375
- w_keyval: bfloat16 [4, 4096, 256], P('section', 'ep'), may hold values from -0.09375 to 0.09375
- gain_query: float32 [4, 128], P('section'), may hold values from 0.8 to 2
- gain_key: float32 [4, 128], P('section'), may hold values from 0.8 to 2
- segment_ids: int32 [4, 8192], P('section', 'ep'), may hold values from 0 to 31, never falling along the last dimension, each value on 1 to 512 neighbouring positions
Outputs:
- layer_out: bfloat16 [4, 8192, 4096], P('section', 'ep')
- attended: bfloat16 [4, 8192, 1024], P('section', 'ep')
Inputs may be any that keep to these rules, and one draw needn't show every extreme that they name: `routes`: each token names 8 different experts, at most one of them below 16. Among the tokens of one device (aligned blocks of 128 rows in each section) no expert below 16 is named by more than 8 of them, and in each section one expert below 16 is named by exactly 8 tokens of every block. `segment_ids`: along each section's tokens the reaction numbers never fall; each reaction spans 1 to 512 tokens and one spans exactly 512.
All inputs are finite; a program needn't handle non-finite values.
Results may differ from a plain program's by a relative error of at most 0.018.
Values may be sent and summed in bfloat16 or wider, within the bound.
No kernel may reach another device: no remote copies, remote signals or barrier semaphores. Data moves between devices by JAX's collectives and lax.ppermute only.
A program may use at most 128 MiB of HBM per device.

v0:
```python
import math

import jax
import jax.numpy as jnp
from jax import lax
from jax.sharding import PartitionSpec as P

OWNERS = 4
SEG_MOST = 512


EPSILON = 1e-06
ROPE_BASE = 1000000.0
FAR_INDEX = 1073741824


def passed_along(block, axis, distance):
    devices = range(lax.axis_size(axis))
    route = [((i - distance) % len(devices), i) for i in devices]
    return lax.ppermute(block, axis, route)


def prefix(shard, axis, combine, identity):
    length, mine = (lax.axis_size(axis), lax.axis_index(axis))
    everything = jax.tree.map(lambda part: lax.all_gather(part, axis), shard)
    start = jax.tree.map(
        lambda part, zero: jnp.broadcast_to(jnp.asarray(zero, part.dtype), part.shape),
        shard,
        identity,
    )

    def step(k, before):
        reached = k < mine
        new = combine(before, jax.tree.map(lambda part: part[k], everything))
        return jax.tree.map(lambda a, b: jnp.where(reached, a, b), new, before)

    return lax.fori_loop(0, length, step, start)


def passed_along_2(value, axis, steps):
    count = lax.axis_size(axis)
    leading, last = (max(0, -steps), min(count, count - steps))
    return lax.ppermute(value, axis, [(source, source + steps) for source in range(leading, last)])


def rms_rows(values):
    return values * lax.rsqrt(jnp.mean(values * values, axis=-1, keepdims=True) + EPSILON)


def rotary(values, position):
    half_count = values.shape[-1] // 2
    frequency = ROPE_BASE ** (-(jnp.arange(half_count, dtype=jnp.float32) * 2.0) / values.shape[-1])
    angles = position.astype(jnp.float32)[:, None] * frequency[None, :]
    cosine = jnp.concatenate([jnp.cos(angles), jnp.cos(angles)], axis=-1)[:, None, :]
    sine = jnp.concatenate([jnp.sin(angles), jnp.sin(angles)], axis=-1)[:, None, :]
    turned = jnp.concatenate([-values[..., half_count:], values[..., :half_count]], axis=-1)
    return values * cosine + turned * sine


def feed_forward(row_block, gate_part, up_part, down_part):
    gate_proj = jnp.dot(row_block, gate_part, preferred_element_type=jnp.float32)
    up_proj = jnp.dot(row_block, up_part, preferred_element_type=jnp.float32)
    activated = (jax.nn.silu(gate_proj) * up_proj).astype(jnp.bfloat16)
    return jnp.dot(activated, down_part, preferred_element_type=jnp.float32)


def keep_later(earlier, later):
    same_id = earlier[0] == later[0]
    newer_id = later[0] > earlier[0]
    start_at = jnp.where(
        same_id, jnp.minimum(earlier[1], later[1]), jnp.where(newer_id, later[1], earlier[1])
    )
    return (jnp.maximum(earlier[0], later[0]), start_at)


def on_device(
    tokens,
    routes,
    router_weights,
    w_gate,
    w_up,
    w_down,
    w_query,
    w_keyval,
    gain_query,
    gain_key,
    segment_ids,
):
    device_count = lax.axis_size("ep")
    expert_count = device_count // OWNERS
    token_count = tokens.shape[1]
    model_width = tokens.shape[2]
    capacity = OWNERS * max(1, token_count // device_count)
    wide_tokens = tokens[0].astype(jnp.float32)
    normed = rms_rows(wide_tokens).astype(jnp.bfloat16)
    inside = routes[0] < expert_count
    has_route = jnp.any(inside, axis=-1)
    chosen = jnp.sum(jnp.where(inside, routes[0], 0), axis=-1)
    weight_kept = jnp.sum(jnp.where(inside, router_weights[0], 0.0), axis=-1)
    expert_ids = jnp.arange(expert_count, dtype=jnp.int32)
    member = ((chosen[:, None] == expert_ids[None, :]) & has_route[:, None]).astype(jnp.int32)
    rank_within = jnp.sum((jnp.cumsum(member, axis=0) - member) * member, axis=-1)
    slot_index = jnp.where(has_route, chosen * capacity + rank_within, -1)
    slot_ids = jnp.arange(expert_count * capacity, dtype=jnp.int32)
    placing = (slot_ids[:, None] == slot_index[None, :]).astype(jnp.bfloat16)
    packed = jnp.dot(placing, normed, preferred_element_type=jnp.float32).astype(jnp.bfloat16)
    gate_part = w_gate[0, 0]
    up_part = w_up[0, 0]
    down_part = w_down[0, 0]
    spread = jnp.broadcast_to(
        packed.reshape(expert_count, 1, capacity, model_width),
        (expert_count, OWNERS, capacity, model_width),
    ).reshape(device_count, capacity, model_width)
    received = lax.all_to_all(spread, "ep", split_axis=0, concat_axis=0, tiled=True)
    partial_out = feed_forward(
        received.reshape(-1, model_width), gate_part, up_part, down_part
    ).reshape(received.shape)
    returned_rows = lax.all_to_all(
        partial_out.astype(jnp.bfloat16), "ep", split_axis=0, concat_axis=0, tiled=True
    ).astype(partial_out.dtype)
    merged = jnp.sum(
        returned_rows.reshape(expert_count, OWNERS, capacity, model_width), axis=1
    ).reshape(expert_count * capacity, model_width)
    fetched_rows = jnp.take(merged, jnp.maximum(slot_index, 0), axis=0)
    expert_out = jnp.where(has_route[:, None], fetched_rows, 0.0)
    layer_out = (wide_tokens + weight_kept[:, None] * expert_out).astype(jnp.bfloat16)
    arrived = passed_along(layer_out, "section", 1)
    lifted = rms_rows(arrived.astype(jnp.float32)).astype(jnp.bfloat16)
    head_dim = gain_query.shape[-1]
    query_width = w_query.shape[-1]
    head_count = query_width // head_dim
    query_raw = jnp.dot(
        lifted,
        lax.all_gather(w_query[0], "ep", axis=0, tiled=True),
        preferred_element_type=jnp.float32,
    )
    keyval_raw = jnp.dot(
        lifted,
        lax.all_gather(w_keyval[0], "ep", axis=0, tiled=True),
        preferred_element_type=jnp.float32,
    )
    segment_row = segment_ids[0]
    first_index = lax.axis_index("ep") * token_count
    global_index = first_index + jnp.arange(token_count, dtype=jnp.int32)
    change = jnp.concatenate([jnp.ones((1,), dtype=bool), segment_row[1:] != segment_row[:-1]])
    local_start = lax.cummax(jnp.where(change, global_index, 0), axis=0)
    empty_prior = (jnp.full((1,), -1, jnp.int32), jnp.full((1,), FAR_INDEX, jnp.int32))
    prior_id, prior_start = prefix(
        (segment_row[-1:], local_start[-1:]), "ep", keep_later, empty_prior
    )
    start_index = jnp.where(segment_row == prior_id[0], prior_start[0], local_start).astype(
        jnp.int32
    )
    position = global_index - start_index
    query = rotary(
        rms_rows(query_raw.reshape(token_count, head_count, head_dim)) * gain_query[0], position
    ).astype(jnp.bfloat16)
    key_part = rotary(rms_rows(keyval_raw[:, None, :head_dim]) * gain_key[0], position)[
        :, 0
    ].astype(jnp.bfloat16)
    value_part = keyval_raw[:, head_dim:].astype(jnp.bfloat16)
    key_value = jnp.concatenate([key_part, value_part], axis=-1)
    reach = (SEG_MOST - 1) // token_count + 1
    earlier_pieces = []
    for distance in range(1, reach + 1):
        earlier_pieces.append(passed_along_2(key_value, "ep", distance))
    window = jnp.concatenate(earlier_pieces[::-1] + [key_value], axis=0)
    key_index = (
        first_index - reach * token_count + jnp.arange((reach + 1) * token_count, dtype=jnp.int32)
    )
    query_rows = query.reshape(token_count * head_count, head_dim)
    query_index = jnp.repeat(global_index, head_count)
    query_start = jnp.repeat(start_index, head_count)
    score_scale = 1.0 / math.sqrt(head_dim)
    scores = (
        jnp.einsum(
            "qd,kd->qk", query_rows, window[:, :head_dim], preferred_element_type=jnp.float32
        )
        * score_scale
    )
    allowed = (key_index[None, :] <= query_index[:, None]) & (
        key_index[None, :] >= query_start[:, None]
    )
    probabilities = jnp.where(allowed, jnp.exp(scores), 0.0)
    total_mass = jnp.sum(probabilities, axis=-1)
    mixed = jnp.dot(
        probabilities.astype(jnp.bfloat16), window[:, head_dim:], preferred_element_type=jnp.float32
    )
    attended = (mixed / total_mass[:, None]).astype(jnp.bfloat16).reshape(token_count, query_width)
    return (layer_out[None], attended[None])


def solution(mesh):
    in_specs = (
        P("section", "ep", None),
        P("section", "ep", None),
        P("section", "ep", None),
        P("section", "ep", None, None),
        P("section", "ep", None, None),
        P("section", "ep", None, None),
        P("section", "ep", None),
        P("section", "ep", None),
        P("section", None),
        P("section", None),
        P("section", "ep"),
    )
    out_specs = (P("section", "ep", None), P("section", "ep", None))
    return jax.shard_map(
        on_device, mesh=mesh, in_specs=in_specs, out_specs=out_specs, check_vma=False
    )
```

profile of v0, /device:TPU:32, one launch (start us, length us, event | category | flops | bytes accessed | tf_op | source)
XLA Modules:
  0.0 793.2 jit_solution(10381463069038364061)
XLA Ops:
  7.2 0.9 fusion.79
  8.0 0.8 fusion.76
  8.8 1.5 fusion.13
  10.8 1.7 fusion.2
  12.6 2.5 broadcast_in_dim.94
  15.0 11.8 %all-to-all-start = ((bf16[64,8,4096]{2,1,0:T(8,128)(2,1)}), bf16[64,8,4096]{2,1,0:T(8,128)(2,1)}, u32[]{:S(2)}, u32[]{:S(2)}) async-start(bf16[64,8,4096]{2,1,0:T(8,128)(2,1)} %bitcast.139), calls=%async_computation | async-start | bytes 8388608 | tf_op jit(solution)/shard_map/all_to_all | solution.py:114
  26.9 0.7 all-gather.7.cloned.1.call-update
  27.7 0.7 all-gather.5.cloned.1.call-update
  28.4 108.3 %all-to-all-done = bf16[64,8,4096]{2,1,0:T(8,128)(2,1)} async-done(((bf16[64,8,4096]{2,1,0:T(8,128)(2,1)}), bf16[64,8,4096]{2,1,0:T(8,128)(2,1)}, u32[]{:S(2)}, u32[]{:S(2)}) %all-to-all-start) | async-done | bytes 4194336 | tf_op jit(solution)/shard_map/all_to_all | solution.py:114
  136.7 6.4 fusion.5
  143.1 9.7 %convolution_convert_fusion = bf16[64,8,4096]{2,1,0:T(8,128)(2,1)} fusion(bf16[1,1,384,4096]{3,2,1,0:T(8,128)(2,1)S(1)} %copy-done, bf16[1,1,4096,384]{3,2,1,0:T(8,128)(2,1)} %param.17, bf16[64,8,4096]{2,1,0:T(8,128)(2,1)} %all-to-all-done, f32[512,384]{1,0:T(8,128)} %fusion.5), kind=kOutput, calls=%fused_computation.6 | convolution fusion | flops 3224502272 | bytes 15466496 | tf_op jit(solution)/shard_map/dot_general | solution.py:64
  152.8 6.9 all-to-all-start.1
  159.7 0.6 slice.41
  162.0 1.3 bitcast_dynamic-update-slice_fusion.1
  163.3 1.3 bitcast_dynamic-update-slice_fusion
  164.6 97.9 %all-reduce.2 = (s32[64]{0:T(128)S(1)}, s32[64]{0:T(128)S(1)}) all-reduce(s32[64]{0:T(128)S(1)} %bitcast_dynamic-update-slice_fusion.1, s32[64]{0:T(128)S(1)} %bitcast_dynamic-update-slice_fusion), channel_id=1, replica_groups=mesh['section'=4,'ep'=64] {'ep'}, use_global_device_ids=true, to_apply=%add | all-reduce | flops 128 | bytes 1024
  262.4 239.9 %while.15 = (s32[]{:T(128)}, s32[1]{0:T(128)}, s32[1]{0:T(128)}, s32[]{:T(128)}, s32[64,1]{0,1:T(1,128)S(1)}, /*index=5*/s32[64,1]{0,1:T(1,128)S(1)}, s32[]{:T(128)}) while((s32[]{:T(128)}, s32[1]{0:T(128)}, s32[1]{0:T(128)}, s32[]{:T(128)}, s32[64,1]{0,1:T(1,128)S(1)}, /*index=5*/s32[64,1]{0,1:T(1,128)S(1)}, s32[]{:T(128)}) %tuple.53), condition=%wide.region_9.10_spmd, body=%wide.region_8.9_spmd.sunk | while | flops 11 | bytes 216 | solution.py:37
  269.9 0.6 constant_dynamic-slice_fusion.3
  273.7 0.6 constant_dynamic-slice_fusion.3
  281.2 0.6 constant_dynamic-slice_fusion.3
  284.9 0.6 constant_dynamic-slice_fusion.3
  292.4 0.6 constant_dynamic-slice_fusion.3
  303.7 0.6 constant_dynamic-slice_fusion.3
  311.2 0.6 constant_dynamic-slice_fusion.3
  314.9 0.6 constant_dynamic-slice_fusion.3
  322.4 0.6 constant_dynamic-slice_fusion.3
  329.9 0.6 constant_dynamic-slice_fusion.3
  341.1 0.6 constant_dynamic-slice_fusion.3
  348.6 0.6 constant_dynamic-slice_fusion.3
  356.1 0.6 constant_dynamic-slice_fusion.3
  359.9 0.6 constant_dynamic-slice_fusion.3
  367.4 0.6 constant_dynamic-slice_fusion.3
  374.9 0.6 constant_dynamic-slice_fusion.3
  382.4 0.6 constant_dynamic-slice_fusion.3
  386.1 0.6 constant_dynamic-slice_fusion.3
  393.6 0.6 constant_dynamic-slice_fusion.3
  397.4 0.6 constant_dynamic-slice_fusion.3
  404.9 0.6 constant_dynamic-slice_fusion.3
  412.4 0.6 constant_dynamic-slice_fusion.3
  419.9 0.6 constant_dynamic-slice_fusion.3
  427.4 0.6 constant_dynamic-slice_fusion.3
  431.1 0.6 constant_dynamic-slice_fusion.3
  502.8 4.5 convert_reduce_fusion
  507.3 5.1 gather_fusion
  512.4 3.4 fusion.15
  516.2 3.4 fusion.16
  519.6 21.7 %collective-permute-done = bf16[128,4096]{1,0:T(8,128)(2,1)} collective-permute-done((bf16[128,4096]{1,0:T(8,128)(2,1)}, bf16[128,4096]{1,0:T(8,128)(2,1)}, u32[]{:S(2)}, u32[]{:S(2)}) %collective-permute-start) | collective-permute-done | bytes 1048608 | tf_op jit(solution)/shard_map/ppermute | solution.py:20
  541.3 1.5 fusion.17
  542.9 2.4 fusion.19
  545.8 5.1 collective-permute-start.1
  550.9 23.9 %collective-permute-start.2 = (bf16[128,256]{1,0:T(8,128)(2,1)S(1)}, bf16[128,256]{1,0:T(8,128)(2,1)}, u32[]{:S(2)}, u32[]{:S(2)}) collective-permute-start(bf16[128,256]{1,0:T(8,128)(2,1)S(1)} %pad_maximum_fusion.2), channel_id=1, source_target_pairs={{0,3},{1,4},{2,5},{3,6},{4,7},{5,8},{6,9},{7,10},{8,11},{9,12},{10... | collective-permute-start | bytes 196616 | tf_op jit(solution)/shard_map/ppermute | solution.py:43
  574.8 1.9 collective-permute-start.3
  576.7 5.3 collective-permute-start.4
  582.0 187.7 %all-gather.5.cloned.1.call-done = bf16[1,4096,1024]{2,1,0:T(8,128)(2,1)} async-done(((bf16[1,64,1024]{2,1,0:T(8,128)(2,1)}), bf16[1,4096,1024]{2,1,0:T(8,128)(2,1)}) %all-gather.5.cloned.1.call-update) | async-done | bytes 8388624 | tf_op jit(solution)/shard_map/all_gather | solution.py:134
  769.7 5.0 fusion
  774.7 0.8 copy-done.1
  775.9 0.9 multiply_multiply_fusion
  776.8 1.1 fusion.55
  777.9 1.9 reshape.297
  779.9 0.8 constant_dynamic-update-slice_fusion.4
  780.8 0.8 constant_dynamic-update-slice_fusion.3
  781.6 0.8 constant_dynamic-update-slice_fusion.2
  782.5 2.5 fusion.80
  785.6 0.8 broadcast_in_dim_reshape.2
  (101 shorter events, 27.9 us)
Async XLA Ops:
  7.2 135.9 %copy-start = (bf16[1,1,384,4096]{3,2,1,0:T(8,128)(2,1)S(1)}, bf16[1,1,384,4096]{3,2,1,0:T(8,128)(2,1)}, u32[]{:S(2)}) copy-start(bf16[1,1,384,4096]{3,2,1,0:T(8,128)(2,1)} %param.18) | copy-start | bytes 9437188
  15.0 121.6 %all-to-all-start = ((bf16[64,8,4096]{2,1,0:T(8,128)(2,1)}), bf16[64,8,4096]{2,1,0:T(8,128)(2,1)}, u32[]{:S(2)}, u32[]{:S(2)}) async-start(bf16[64,8,4096]{2,1,0:T(8,128)(2,1)} %bitcast.139), calls=%async_computation | async-start | bytes 8388608 | tf_op jit(solution)/shard_map/all_to_all | solution.py:114
  26.9 516.0 %all-gather.7.cloned.1.call-start = ((), (), s32[]{:S(2)}) async-start(), calls=%async_computation.3 | async-start | bytes 2129920 | tf_op jit(solution)/shard_map/all_gather | solution.py:139
  27.6 742.1 %all-gather.5.cloned.1.call-start = ((), (), s32[]{:S(2)}) async-start(), calls=%async_computation.2 | async-start | bytes 8519680 | tf_op jit(solution)/shard_map/all_gather | solution.py:134
  152.8 6.9 copy-start.5
  152.8 8.6 %copy-start.6 = (u32[256]{0:T(256)S(1)}, u32[256]{0:T(256)}, u32[]{:S(2)}) copy-start(u32[256]{0:T(256)} %constant.111) | copy-start | bytes 3076
  152.8 349.6 %copy-start.2 = (s32[1,128,8]{1,2,0:T(8,128)S(1)}, s32[1,128,8]{1,2,0:T(8,128)}, u32[]{:S(2)}) copy-start(s32[1,128,8]{1,2,0:T(8,128)} %param.14) | copy-start | bytes 12292
  152.8 349.6 %copy-start.3 = (f32[1,128,8]{1,2,0:T(8,128)S(1)}, f32[1,128,8]{1,2,0:T(8,128)}, u32[]{:S(2)}) copy-start(f32[1,128,8]{1,2,0:T(8,128)} %param.15) | copy-start | bytes 12292
  152.8 349.9 %all-to-all-start.1 = ((bf16[64,8,4096]{2,1,0:T(8,128)(2,1)}), bf16[64,8,4096]{2,1,0:T(8,128)(2,1)}, u32[]{:S(2)}, u32[]{:S(2)}) async-start(bf16[64,8,4096]{2,1,0:T(8,128)(2,1)} %convolution_convert_fusion), calls=%async_computation.1 | async-start | bytes 8388608 | tf_op jit(solution)/shard_map/all_to_all | solution.py:118
  515.8 25.5 %collective-permute-start = (bf16[128,4096]{1,0:T(8,128)(2,1)}, bf16[128,4096]{1,0:T(8,128)(2,1)}, u32[]{:S(2)}, u32[]{:S(2)}) collective-permute-start(bf16[128,4096]{1,0:T(8,128)(2,1)} %fusion.15), channel_id=1, source_target_pairs={{192,0},{0,64},{64,128},{128,192},{193,1},{1,65},{65,129},{129,193... | collective-permute-start | bytes 3145736 | tf_op jit(solution)/shard_map/ppermute | solution.py:20
  519.6 25.8 %copy-start.4 = (f32[1,128]{1,0:T(1,128)S(1)}, f32[1,128]{1,0:T(1,128)}, u32[]{:S(2)}) copy-start(f32[1,128]{1,0:T(1,128)} %param.22) | copy-start | bytes 1540
  545.8 234.1 %collective-permute-start.1 = (bf16[128,256]{1,0:T(8,128)(2,1)S(1)}, bf16[128,256]{1,0:T(8,128)(2,1)}, u32[]{:S(2)}, u32[]{:S(2)}) collective-permute-start(bf16[128,256]{1,0:T(8,128)(2,1)S(1)} %pad_maximum_fusion.2), channel_id=1, source_target_pairs={{0,4},{1,5},{2,6},{3,7},{4,8},{5,9},{6,10},{7,11},{8,12},{9,13},{1... | collective-permute-start | bytes 196616 | tf_op jit(solution)/shard_map/ppermute | solution.py:43
  550.9 229.9 %collective-permute-start.2 = (bf16[128,256]{1,0:T(8,128)(2,1)S(1)}, bf16[128,256]{1,0:T(8,128)(2,1)}, u32[]{:S(2)}, u32[]{:S(2)}) collective-permute-start(bf16[128,256]{1,0:T(8,128)(2,1)S(1)} %pad_maximum_fusion.2), channel_id=1, source_target_pairs={{0,3},{1,4},{2,5},{3,6},{4,7},{5,8},{6,9},{7,10},{8,11},{9,12},{10... | collective-permute-start | bytes 196616 | tf_op jit(solution)/shard_map/ppermute | solution.py:43
  574.8 206.8 %collective-permute-start.3 = (bf16[128,256]{1,0:T(8,128)(2,1)S(1)}, bf16[128,256]{1,0:T(8,128)(2,1)}, u32[]{:S(2)}, u32[]{:S(2)}) collective-permute-start(bf16[128,256]{1,0:T(8,128)(2,1)S(1)} %pad_maximum_fusion.2), channel_id=1, source_target_pairs={{0,2},{1,3},{2,4},{3,5},{4,6},{5,7},{6,8},{7,9},{8,10},{9,11},{10,... | collective-permute-start | bytes 196616 | tf_op jit(solution)/shard_map/ppermute | solution.py:43
  576.7 205.8 %collective-permute-start.4 = (bf16[128,256]{1,0:T(8,128)(2,1)S(1)}, bf16[128,256]{1,0:T(8,128)(2,1)S(1)}, u32[]{:S(2)}, u32[]{:S(2)}) collective-permute-start(bf16[128,256]{1,0:T(8,128)(2,1)S(1)} %pad_maximum_fusion.2), channel_id=1, source_target_pairs={{0,1},{1,2},{2,3},{3,4},{4,5},{5,6},{6,7},{7,8},{8,9},{9,10},{10,1... | collective-permute-start | bytes 196616 | tf_op jit(solution)/shard_map/ppermute | solution.py:43
  774.7 0.8 copy-start.1
Sparse Core Ops, SparseCore 0:
  29.5 355.1 all-gather.6
  386.5 383.1 all-gather.4
where the time goes:
time: 803 us; the launch traced here: 793 us
  waiting for transfers between devices  319 us (40%)
  loops' own time  201 us (25%)
  blocking collectives  97.9 us (12%)
  local copies, waits for them, and re-layouts  57.2 us (7%)
  starting transfers between devices  55 us (7%)
  matrix products  28.3 us (4%)
  other arithmetic  20 us (2%)
  between operations  14.4 us (2%)
    another operation x1, loops' own time, prefix(): return lax.fori_loop(0, length, step, start)  201 us
    all_gather x1, waiting for transfers between devices, on_device(): lax.all_gather(w_query[0], 'ep', axis=0, tiled=True)  188 us
    all_to_all x1, waiting for transfers between devices, on_device(): lax.all_to_all(spread, 'ep', split_axis=0, concat_axis=0, tiled=True)  108 us
    unnamed x1, blocking collectives  97.9 us
    dynamic_slice x64, local copies, waits for them, and re-layouts, step(): new = combine(before, jax.tree.map(lambda part: part[k], everything))  38.6 us
    ppermute x4, starting transfers between devices, passed_along_2(): lax.ppermute(value, axis, [(source, source + steps) for source in range(l...  36.2 us
    ppermute x1, waiting for transfers between devices, passed_along(): return lax.ppermute(block, axis, route)  21.7 us
  transfers between devices with their start and end apart: 9, of which 3 were waited for; matrix products, arithmetic and copies ran while one was open for 12% of the time, Pallas kernels for 0%

commit v1 on v0

--- a/solution.py
+++ b/solution.py
@@ -142,15 +142,17 @@
     segment_row = segment_ids[0]
     first_index = lax.axis_index("ep") * token_count
     global_index = first_index + jnp.arange(token_count, dtype=jnp.int32)
-    change = jnp.concatenate([jnp.ones((1,), dtype=bool), segment_row[1:] != segment_row[:-1]])
-    local_start = lax.cummax(jnp.where(change, global_index, 0), axis=0)
-    empty_prior = (jnp.full((1,), -1, jnp.int32), jnp.full((1,), FAR_INDEX, jnp.int32))
-    prior_id, prior_start = prefix(
-        (segment_row[-1:], local_start[-1:]), "ep", keep_later, empty_prior
-    )
-    start_index = jnp.where(segment_row == prior_id[0], prior_start[0], local_start).astype(
-        jnp.int32
-    )
+    reach = (SEG_MOST - 1) // token_count + 1
+    key_index = (
+        first_index - reach * token_count + jnp.arange((reach + 1) * token_count, dtype=jnp.int32)
+    )
+    segment_pieces = []
+    for distance in range(1, reach + 1):
+        segment_pieces.append(passed_along_2(segment_row, "ep", distance))
+    window_segment = jnp.concatenate(segment_pieces[::-1] + [segment_row], axis=0)
+    window_segment = jnp.where(key_index >= 0, window_segment, -1)
+    same_segment = window_segment[None, :] == segment_row[:, None]
+    start_index = jnp.min(jnp.where(same_segment, key_index[None, :], FAR_INDEX), axis=1)
     position = global_index - start_index
     query = rotary(
         rms_rows(query_raw.reshape(token_count, head_count, head_dim)) * gain_query[0], position
@@ -160,33 +162,27 @@
     ].astype(jnp.bfloat16)
     value_part = keyval_raw[:, head_dim:].astype(jnp.bfloat16)
     key_value = jnp.concatenate([key_part, value_part], axis=-1)
-    reach = (SEG_MOST - 1) // token_count + 1
     earlier_pieces = []
     for distance in range(1, reach + 1):
         earlier_pieces.append(passed_along_2(key_value, "ep", distance))
     window = jnp.concatenate(earlier_pieces[::-1] + [key_value], axis=0)
-    key_index = (
-        first_index - reach * token_count + jnp.arange((reach + 1) * token_count, dtype=jnp.int32)
-    )
-    query_rows = query.reshape(token_count * head_count, head_dim)
-    query_index = jnp.repeat(global_index, head_count)
-    query_start = jnp.repeat(start_index, head_count)
     score_scale = 1.0 / math.sqrt(head_dim)
     scores = (
         jnp.einsum(
-            "qd,kd->qk", query_rows, window[:, :head_dim], preferred_element_type=jnp.float32
+            "thd,kd->thk", query, window[:, :head_dim], preferred_element_type=jnp.float32
         )
         * score_scale
     )
-    allowed = (key_index[None, :] <= query_index[:, None]) & (
-        key_index[None, :] >= query_start[:, None]
-    )
+    allowed = (same_segment & (key_index[None, :] <= global_index[:, None]))[:, None, :]
     probabilities = jnp.where(allowed, jnp.exp(scores), 0.0)
     total_mass = jnp.sum(probabilities, axis=-1)
-    mixed = jnp.dot(
-        probabilities.astype(jnp.bfloat16), window[:, head_dim:], preferred_element_type=jnp.float32
-    )
-    attended = (mixed / total_mass[:, None]).astype(jnp.bfloat16).reshape(token_count, query_width)
+    mixed = jnp.einsum(
+        "thk,kd->thd",
+        probabilities.astype(jnp.bfloat16),
+        window[:, head_dim:],
+        preferred_element_type=jnp.float32,
+    )
+    attended = (mixed / total_mass[..., None]).astype(jnp.bfloat16).reshape(token_count, query_width)
     return (layer_out[None], attended[None])
 
 

time: 803 us -> 804 us (level); the launches traced: 793 us -> 803 us
  waiting for transfers between devices: 319 us -> 684 us
  loops' own time: 201 us -> 0 us
  blocking collectives: 97.9 us -> 0 us
  local copies, waits for them, and re-layouts: 57.2 us -> 15.2 us
  starting transfers between devices: 55 us -> 45.3 us
    another operation x1 -> x0, loops' own time: 201 us -> none  [prefix(): return lax.fori_loop(0, length, step, start)]
    all_gather x1, waiting for transfers between devices: 188 us -> 373 us  [on_device(): lax.all_gather(w_query[0], 'ep', axis=0, tiled=True)]
    unnamed x1 -> x0, blocking collectives: 97.9 us -> none
    ppermute x4 -> x8, waiting for transfers between devices: 0.01 us -> 87.2 us  [passed_along_2(): lax.ppermute(value, axis, [(source, source + steps) for source in range(l...]
    all_gather x1, waiting for transfers between devices: 0.02 us -> 78.5 us  [on_device(): lax.all_gather(w_keyval[0], 'ep', axis=0, tiled=True)]
    dynamic_slice x64 -> x0, local copies, waits for them, and re-layouts: 38.6 us -> none  [step(): new = combine(before, jax.tree.map(lambda part: part[k], everything))]
    ppermute x4 -> x8, starting transfers between devices: 36.2 us -> 26.2 us  [passed_along_2(): lax.ppermute(value, axis, [(source, source + steps) for source in range(l...]
  transfers between devices with their start and end apart: 9 -> 13, of which waited for: 3 -> 8; matrix products, arithmetic and copies ran while one was open for 12% -> 6% of each run, Pallas kernels for 0% -> 0%
where the time goes in v1:
time: 804 us; the launch traced here: 803 us
  waiting for transfers between devices  684 us (85%)
  starting transfers between devices  45.3 us (6%)
  matrix products  26.7 us (3%)
  other arithmetic  17.7 us (2%)
  local copies, waits for them, and re-layouts  15.2 us (2%)
  between operations  14.4 us (2%)
    all_gather x1, waiting for transfers between devices, on_device(): lax.all_gather(w_query[0], 'ep', axis=0, tiled=True)  373 us
    all_to_all x1, waiting for transfers between devices, on_device(): lax.all_to_all(spread, 'ep', split_axis=0, concat_axis=0, tiled=True)  108 us
    ppermute x8, waiting for transfers between devices, passed_along_2(): lax.ppermute(value, axis, [(source, source + steps) for source in range(l...  87.2 us
    all_gather x1, waiting for transfers between devices, on_device(): lax.all_gather(w_keyval[0], 'ep', axis=0, tiled=True)  78.5 us
    ppermute x1, waiting for transfers between devices, passed_along(): return lax.ppermute(block, axis, route)  27.8 us
    ppermute x8, starting transfers between devices, passed_along_2(): lax.ppermute(value, axis, [(source, source + steps) for source in range(l...  26.2 us
  transfers between devices with their start and end apart: 13, of which 8 were waited for; matrix products, arithmetic and copies ran while one was open for 6% of the time, Pallas kernels for 0%

profile of v1, /device:TPU:32, one launch (start us, length us, event | category | flops | bytes accessed | tf_op | source)
XLA Modules:
  0.0 803.5 jit_solution(15481423913225358977)
XLA Ops:
  7.2 0.9 fusion.83
  8.0 0.8 fusion.79
  8.8 1.5 fusion.15
  10.4 0.1 fusion.75
  10.5 0.2 reduce_window_sum.11
  10.6 0.2 select_reduce_fusion
  10.8 1.7 fusion.2
  12.6 2.5 broadcast_in_dim.108
  15.0 11.8 %all-to-all-start = ((bf16[64,8,4096]{2,1,0:T(8,128)(2,1)}), bf16[64,8,4096]{2,1,0:T(8,128)(2,1)}, u32[]{:S(2)}, u32[]{:S(2)}) async-start(bf16[64,8,4096]{2,1,0:T(8,128)(2,1)} %bitcast.115), calls=%async_computation | async-start | bytes 8388608 | tf_op jit(solution)/shard_map/all_to_all | solution.py:114
  26.9 0.0 all-gather.7.cloned.1.call-start
  26.9 0.7 all-gather.7.cloned.1.call-update
  27.6 0.0 all-gather.5.cloned.1.call-start
  27.7 0.7 all-gather.5.cloned.1.call-update
  28.4 108.3 %all-to-all-done = bf16[64,8,4096]{2,1,0:T(8,128)(2,1)} async-done(((bf16[64,8,4096]{2,1,0:T(8,128)(2,1)}), bf16[64,8,4096]{2,1,0:T(8,128)(2,1)}, u32[]{:S(2)}, u32[]{:S(2)}) %all-to-all-start) | async-done | bytes 4194336 | tf_op jit(solution)/shard_map/all_to_all | solution.py:114
  136.7 6.4 fusion.5
  143.0 9.7 %convolution_convert_fusion = bf16[64,8,4096]{2,1,0:T(8,128)(2,1)} fusion(bf16[1,1,384,4096]{3,2,1,0:T(8,128)(2,1)S(1)} %copy-done, bf16[1,1,4096,384]{3,2,1,0:T(8,128)(2,1)} %param.15, bf16[64,8,4096]{2,1,0:T(8,128)(2,1)} %all-to-all-done, f32[512,384]{1,0:T(8,128)} %fusion.5), kind=kOutput, calls=%fused_computation.4 | convolution fusion | flops 3224502272 | bytes 15466496 | tf_op jit(solution)/shard_map/dot_general | solution.py:64
  152.8 6.9 all-to-all-start.1
  159.7 3.4 collective-permute-start
  163.0 3.4 collective-permute-start.1
  166.4 4.3 collective-permute-start.2
  170.7 4.3 collective-permute-start.3
  175.1 1.2 collective-permute-done
  176.3 32.1 %collective-permute-done.1 = s32[128]{0:T(128)S(1)} collective-permute-done((s32[128]{0:T(128)S(1)}, s32[128]{0:T(128)S(1)}, u32[]{:S(2)}, u32[]{:S(2)}) %collective-permute-start.1) | collective-permute-done | bytes 544 | tf_op jit(solution)/shard_map/ppermute | solution.py:43
  208.4 53.8 %collective-permute-done.2 = s32[128]{0:T(128)S(1)} collective-permute-done((s32[128]{0:T(128)S(1)}, s32[128]{0:T(128)S(1)}, u32[]{:S(2)}, u32[]{:S(2)}) %collective-permute-start.2) | collective-permute-done | bytes 544 | tf_op jit(solution)/shard_map/ppermute | solution.py:43
  262.3 0.2 fusion.68
  262.5 0.3 multiply_cosine_fusion
  262.8 7.9 all-to-all-done.1
  270.7 4.5 convert_reduce_fusion
  275.1 5.0 gather_fusion
  280.2 2.6 fusion.17
  282.8 0.3 collective-permute-start.4
  283.0 0.1 compare_and_fusion
  283.2 1.6 fusion.18
  284.8 27.8 %collective-permute-done.4 = bf16[128,4096]{1,0:T(8,128)(2,1)S(1)} collective-permute-done((bf16[128,4096]{1,0:T(8,128)(2,1)S(1)}, bf16[128,4096]{1,0:T(8,128)(2,1)S(1)}, u32[]{:S(2)}, u32[]{:S(2)}) %collective-permute-start.4) | collective-permute-done | bytes 1048608 | tf_op jit(solution)/shard_map/ppermute | solution.py:20
  312.5 1.1 copy-done.3
  313.6 0.3 fusion.19
  313.9 78.5 %all-gather.7.cloned.1.call-done = bf16[1,4096,256]{2,1,0:T(8,128)(2,1)} async-done(((bf16[1,64,256]{2,1,0:T(8,128)(2,1)}), bf16[1,4096,256]{2,1,0:T(8,128)(2,1)}) %all-gather.7.cloned.1.call-update) | async-done | bytes 2097168 | tf_op jit(solution)/shard_map/all_gather | solution.py:139
  392.4 2.4 fusion.21
  394.9 0.1 multiply_reduce_fusion.1
  395.0 0.1 fusion.76
  395.1 0.1 fusion.71
  395.2 0.8 fusion.73
  396.0 1.9 collective-permute-start.5
  397.9 1.9 collective-permute-start.6
  399.8 1.9 collective-permute-start.7
  401.7 5.2 collective-permute-start.8
  406.9 373.2 %all-gather.5.cloned.1.call-done = bf16[1,4096,1024]{2,1,0:T(8,128)(2,1)} async-done(((bf16[1,64,1024]{2,1,0:T(8,128)(2,1)}), bf16[1,4096,1024]{2,1,0:T(8,128)(2,1)}) %all-gather.5.cloned.1.call-update) | async-done | bytes 8388624 | tf_op jit(solution)/shard_map/all_gather | solution.py:134
  780.1 5.0 fusion.43
  785.1 0.1 copy.26
  785.3 0.8 copy-done.4
  786.0 0.2 multiply_reduce_fusion
  786.3 0.7 copy.19
  786.9 1.3 add_rsqrt_fusion
  788.2 0.8 copy.20
  789.0 1.3 multiply_multiply_fusion
  790.3 0.2 slice_negate_fusion
  790.6 0.3 fusion.64
  790.9 0.8 constant_dynamic-update-slice_fusion.5
  791.8 0.8 constant_dynamic-update-slice_fusion.4
  792.6 0.8 constant_dynamic-update-slice_fusion.3
  793.5 0.8 constant_dynamic-update-slice_fusion.2
  794.3 0.8 fusion.13
  795.2 0.6 fusion.46
  795.8 0.9 copy.23
  (47 shorter events, 0.2 us)
Async XLA Ops:
  7.2 135.9 %copy-start = (bf16[1,1,384,4096]{3,2,1,0:T(8,128)(2,1)S(1)}, bf16[1,1,384,4096]{3,2,1,0:T(8,128)(2,1)}, u32[]{:S(2)}) copy-start(bf16[1,1,384,4096]{3,2,1,0:T(8,128)(2,1)} %param.16) | copy-start | bytes 9437188
  15.0 121.6 %all-to-all-start = ((bf16[64,8,4096]{2,1,0:T(8,128)(2,1)}), bf16[64,8,4096]{2,1,0:T(8,128)(2,1)}, u32[]{:S(2)}, u32[]{:S(2)}) async-start(bf16[64,8,4096]{2,1,0:T(8,128)(2,1)} %bitcast.115), calls=%async_computation | async-start | bytes 8388608 | tf_op jit(solution)/shard_map/all_to_all | solution.py:114
  26.9 365.5 %all-gather.7.cloned.1.call-start = ((), (), s32[]{:S(2)}) async-start(), calls=%async_computation.3 | async-start | bytes 2129920 | tf_op jit(solution)/shard_map/all_gather | solution.py:139
  27.6 752.5 %all-gather.5.cloned.1.call-start = ((), (), s32[]{:S(2)}) async-start(), calls=%async_computation.2 | async-start | bytes 8519680 | tf_op jit(solution)/shard_map/all_gather | solution.py:134
  152.8 6.9 copy-start.10
  152.8 22.3 %copy-start.6 = (s32[1,128,8]{1,2,0:T(8,128)S(1)}, s32[1,128,8]{1,2,0:T(8,128)}, u32[]{:S(2)}) copy-start(s32[1,128,8]{1,2,0:T(8,128)} %param.12) | copy-start | bytes 12292
  152.8 22.3 %copy-start.8 = (f32[1,128,8]{1,2,0:T(8,128)S(1)}, f32[1,128,8]{1,2,0:T(8,128)}, u32[]{:S(2)}) copy-start(f32[1,128,8]{1,2,0:T(8,128)} %param.13) | copy-start | bytes 12292
  152.8 117.9 %all-to-all-start.1 = ((bf16[64,8,4096]{2,1,0:T(8,128)(2,1)}), bf16[64,8,4096]{2,1,0:T(8,128)(2,1)}, u32[]{:S(2)}, u32[]{:S(2)}) async-start(bf16[64,8,4096]{2,1,0:T(8,128)(2,1)} %convolution_convert_fusion), calls=%async_computation.1 | async-start | bytes 8388608 | tf_op jit(solution)/shard_map/all_to_all | solution.py:118
  159.7 16.6 %collective-permute-start = (s32[128]{0:T(128)S(1)}, s32[128]{0:T(128)S(1)}, u32[]{:S(2)}, u32[]{:S(2)}) collective-permute-start(s32[128]{0:T(128)S(1)} %bitcast.120), channel_id=1, source_target_pairs={{0,4},{1,5},{2,6},{3,7},{4,8},{5,9},{6,10},{7,11},{8,12},{9,13},{1... | collective-permute-start | bytes 1544 | tf_op jit(solution)/shard_map/ppermute | solution.py:43
  163.0 45.4 %collective-permute-start.1 = (s32[128]{0:T(128)S(1)}, s32[128]{0:T(128)S(1)}, u32[]{:S(2)}, u32[]{:S(2)}) collective-permute-start(s32[128]{0:T(128)S(1)} %bitcast.121), channel_id=1, source_target_pairs={{0,3},{1,4},{2,5},{3,6},{4,7},{5,8},{6,9},{7,10},{8,11},{9,12},{10... | collective-permute-start | bytes 1544 | tf_op jit(solution)/shard_map/ppermute | solution.py:43
  166.4 95.8 %collective-permute-start.2 = (s32[128]{0:T(128)S(1)}, s32[128]{0:T(128)S(1)}, u32[]{:S(2)}, u32[]{:S(2)}) collective-permute-start(s32[128]{0:T(128)S(1)} %bitcast.122), channel_id=1, source_target_pairs={{0,2},{1,3},{2,4},{3,5},{4,6},{5,7},{6,8},{7,9},{8,10},{9,11},{10,... | collective-permute-start | bytes 1544 | tf_op jit(solution)/shard_map/ppermute | solution.py:43
  170.7 91.6 %collective-permute-start.3 = (s32[128]{0:T(128)S(1)}, s32[128]{0:T(128)S(1)}, u32[]{:S(2)}, u32[]{:S(2)}) collective-permute-start(s32[128]{0:T(128)S(1)} %bitcast.123), channel_id=1, source_target_pairs={{0,1},{1,2},{2,3},{3,4},{4,5},{5,6},{6,7},{7,8},{8,9},{9,10},{10,1... | collective-permute-start | bytes 1544 | tf_op jit(solution)/shard_map/ppermute | solution.py:43
  280.2 3.0 copy-start.1
  280.2 3.0 copy-start.2
  282.8 29.8 %collective-permute-start.4 = (bf16[128,4096]{1,0:T(8,128)(2,1)S(1)}, bf16[128,4096]{1,0:T(8,128)(2,1)S(1)}, u32[]{:S(2)}, u32[]{:S(2)}) collective-permute-start(bf16[128,4096]{1,0:T(8,128)(2,1)S(1)} %fusion.17), channel_id=1, source_target_pairs={{192,0},{0,64},{64,128},{128,192},{193,1},{1,65},{65,129},{129,193... | collective-permute-start | bytes 3145736 | tf_op jit(solution)/shard_map/ppermute | solution.py:20
  284.8 110.2 %copy-start.11 = (f32[1,128]{1,0:T(1,128)S(1)}, f32[1,128]{1,0:T(1,128)}, u32[]{:S(2)}) copy-start(f32[1,128]{1,0:T(1,128)} %param.20) | copy-start | bytes 1540
  312.5 1.1 copy-start.3
  313.9 78.5 %copy-start.7 = (f32[128]{0:T(128)}, f32[128]{0:T(128)S(1)}, u32[]{:S(2)}) copy-start(f32[128]{0:T(128)S(1)} %add_rsqrt_fusion.2) | copy-start | bytes 1540
  396.0 394.9 %collective-permute-start.5 = (bf16[128,256]{1,0:T(8,128)(2,1)S(1)}, bf16[128,256]{1,0:T(8,128)(2,1)}, u32[]{:S(2)}, u32[]{:S(2)}) collective-permute-start(bf16[128,256]{1,0:T(8,128)(2,1)S(1)} %pad_maximum_fusion.2), channel_id=1, source_target_pairs={{0,4},{1,5},{2,6},{3,7},{4,8},{5,9},{6,10},{7,11},{8,12},{9,13},{1... | collective-permute-start | bytes 196616 | tf_op jit(solution)/shard_map/ppermute | solution.py:43
  397.9 393.9 %collective-permute-start.6 = (bf16[128,256]{1,0:T(8,128)(2,1)S(1)}, bf16[128,256]{1,0:T(8,128)(2,1)}, u32[]{:S(2)}, u32[]{:S(2)}) collective-permute-start(bf16[128,256]{1,0:T(8,128)(2,1)S(1)} %pad_maximum_fusion.2), channel_id=1, source_target_pairs={{0,3},{1,4},{2,5},{3,6},{4,7},{5,8},{6,9},{7,10},{8,11},{9,12},{10... | collective-permute-start | bytes 196616 | tf_op jit(solution)/shard_map/ppermute | solution.py:43
  399.8 392.8 %collective-permute-start.7 = (bf16[128,256]{1,0:T(8,128)(2,1)S(1)}, bf16[128,256]{1,0:T(8,128)(2,1)}, u32[]{:S(2)}, u32[]{:S(2)}) collective-permute-start(bf16[128,256]{1,0:T(8,128)(2,1)S(1)} %pad_maximum_fusion.2), channel_id=1, source_target_pairs={{0,2},{1,3},{2,4},{3,5},{4,6},{5,7},{6,8},{7,9},{8,10},{9,11},{10,... | collective-permute-start | bytes 196616 | tf_op jit(solution)/shard_map/ppermute | solution.py:43
  401.7 391.7 %collective-permute-start.8 = (bf16[128,256]{1,0:T(8,128)(2,1)S(1)}, bf16[128,256]{1,0:T(8,128)(2,1)}, u32[]{:S(2)}, u32[]{:S(2)}) collective-permute-start(bf16[128,256]{1,0:T(8,128)(2,1)S(1)} %pad_maximum_fusion.2), channel_id=1, source_target_pairs={{0,1},{1,2},{2,3},{3,4},{4,5},{5,6},{6,7},{7,8},{8,9},{9,10},{10,1... | collective-permute-start | bytes 196616 | tf_op jit(solution)/shard_map/ppermute | solution.py:43
  785.2 0.8 copy-start.4
  789.0 1.5 copy-start.5
  789.0 1.5 copy-start.9
Sparse Core Ops, SparseCore 0:
  29.5 362.8 all-gather.6
  394.2 385.8 all-gather.4

commit v2 on v1

--- a/solution.py
+++ b/solution.py
@@ -12,6 +12,7 @@
 EPSILON = 1e-06
 ROPE_BASE = 1000000.0
 FAR_INDEX = 1073741824
+EP = ("ep_y", "ep_x", "ep_z")
 
 
 def passed_along(block, axis, distance):
@@ -86,7 +87,7 @@
     gain_key,
     segment_ids,
 ):
-    device_count = lax.axis_size("ep")
+    device_count = lax.axis_size(EP)
     expert_count = device_count // OWNERS
     token_count = tokens.shape[1]
     model_width = tokens.shape[2]
@@ -111,12 +112,12 @@
         packed.reshape(expert_count, 1, capacity, model_width),
         (expert_count, OWNERS, capacity, model_width),
     ).reshape(device_count, capacity, model_width)
-    received = lax.all_to_all(spread, "ep", split_axis=0, concat_axis=0, tiled=True)
+    received = lax.all_to_all(spread, EP, split_axis=0, concat_axis=0, tiled=True)
     partial_out = feed_forward(
         received.reshape(-1, model_width), gate_part, up_part, down_part
     ).reshape(received.shape)
     returned_rows = lax.all_to_all(
-        partial_out.astype(jnp.bfloat16), "ep", split_axis=0, concat_axis=0, tiled=True
+        partial_out.astype(jnp.bfloat16), EP, split_axis=0, concat_axis=0, tiled=True
     ).astype(partial_out.dtype)
     merged = jnp.sum(
         returned_rows.reshape(expert_count, OWNERS, capacity, model_width), axis=1
@@ -129,18 +130,14 @@
     head_dim = gain_query.shape[-1]
     query_width = w_query.shape[-1]
     head_count = query_width // head_dim
-    query_raw = jnp.dot(
-        lifted,
-        lax.all_gather(w_query[0], "ep", axis=0, tiled=True),
-        preferred_element_type=jnp.float32,
-    )
-    keyval_raw = jnp.dot(
-        lifted,
-        lax.all_gather(w_keyval[0], "ep", axis=0, tiled=True),
-        preferred_element_type=jnp.float32,
-    )
+    projection = jnp.concatenate([w_query[0], w_keyval[0]], axis=-1)
+    for axis in EP[::-1]:
+        projection = lax.all_gather(projection, axis, axis=0, tiled=True)
+    projected = jnp.dot(lifted, projection, preferred_element_type=jnp.float32)
+    query_raw = projected[:, :query_width]
+    keyval_raw = projected[:, query_width:]
     segment_row = segment_ids[0]
-    first_index = lax.axis_index("ep") * token_count
+    first_index = lax.axis_index(EP) * token_count
     global_index = first_index + jnp.arange(token_count, dtype=jnp.int32)
     reach = (SEG_MOST - 1) // token_count + 1
     key_index = (
@@ -148,7 +145,7 @@
     )
     segment_pieces = []
     for distance in range(1, reach + 1):
-        segment_pieces.append(passed_along_2(segment_row, "ep", distance))
+        segment_pieces.append(passed_along_2(segment_row, EP, distance))
     window_segment = jnp.concatenate(segment_pieces[::-1] + [segment_row], axis=0)
     window_segment = jnp.where(key_index >= 0, window_segment, -1)
     same_segment = window_segment[None, :] == segment_row[:, None]
@@ -164,7 +161,7 @@
     key_value = jnp.concatenate([key_part, value_part], axis=-1)
     earlier_pieces = []
     for distance in range(1, reach + 1):
-        earlier_pieces.append(passed_along_2(key_value, "ep", distance))
+        earlier_pieces.append(passed_along_2(key_value, EP, distance))
     window = jnp.concatenate(earlier_pieces[::-1] + [key_value], axis=0)
     score_scale = 1.0 / math.sqrt(head_dim)
     scores = (
@@ -187,20 +184,29 @@
 
 
 def solution(mesh):
+    ep_size = mesh.shape["ep"]
+    z_size = 4 if ep_size % 4 == 0 else 1
+    x_size = 4 if ep_size % (z_size * 4) == 0 else 1
+    split_mesh = jax.sharding.Mesh(
+        mesh.devices.reshape(
+            mesh.shape["section"], ep_size // (x_size * z_size), x_size, z_size
+        ),
+        ("section",) + EP,
+    )
     in_specs = (
-        P("section", "ep", None),
-        P("section", "ep", None),
-        P("section", "ep", None),
-        P("section", "ep", None, None),
-        P("section", "ep", None, None),
-        P("section", "ep", None, None),
-        P("section", "ep", None),
-        P("section", "ep", None),
+        P("section", EP, None),
+        P("section", EP, None),
+        P("section", EP, None),
+        P("section", EP, None, None),
+        P("section", EP, None, None),
+        P("section", EP, None, None),
+        P("section", EP, None),
+        P("section", EP, None),
         P("section", None),
         P("section", None),
-        P("section", "ep"),
-    )
-    out_specs = (P("section", "ep", None), P("section", "ep", None))
+        P("section", EP),
+    )
+    out_specs = (P("section", EP, None), P("section", EP, None))
     return jax.shard_map(
-        on_device, mesh=mesh, in_specs=in_specs, out_specs=out_specs, check_vma=False
-    )
+        on_device, mesh=split_mesh, in_specs=in_specs, out_specs=out_specs, check_vma=False
+    )

time: 804 us -> 373 us (0.46)
  waiting for transfers between devices: 684 us -> 147 us
  blocking collectives: 0 us -> 104 us
    all_gather x2, waiting for transfers between devices: 452 us -> 39.4 us  [on_device(): projection = lax.all_gather(projection, axis, axis=0, tiled=True)]
    all_to_all x2, waiting for transfers between devices: 116 us -> 5.98 us  [the longest x1 5.98 us: on_device(): lax.all_to_all(partial_out.astype(jnp.bfloat16), EP, split_axis=0, concat...]
    all_gather x0 -> x1, blocking collectives: none -> 104 us  [on_device(): projection = lax.all_gather(projection, axis, axis=0, tiled=True)]
    ppermute x8, waiting for transfers between devices: 87.2 us -> 73.8 us  [passed_along_2(): lax.ppermute(value, axis, [(source, source + steps) for source in range(l...]
  transfers between devices with their start and end apart: 13 -> 13, of which waited for: 8 -> 6; matrix products, arithmetic and copies ran while one was open for 6% -> 10% of each run, Pallas kernels for 0% -> 0%
where the time goes in v2:
time: 373 us; the launch traced here: 370 us
  waiting for transfers between devices  147 us (39%)
  blocking collectives  104 us (28%)
  starting transfers between devices  46.6 us (12%)
  matrix products  25.4 us (7%)
  other arithmetic  17.1 us (5%)
  local copies, waits for them, and re-layouts  15.2 us (4%)
  between operations  14.5 us (4%)
    all_gather x1, blocking collectives, on_device(): projection = lax.all_gather(projection, axis, axis=0, tiled=True)  104 us
    ppermute x8, waiting for transfers between devices, passed_along_2(): lax.ppermute(value, axis, [(source, source + steps) for source in range(l...  73.8 us
    all_gather x2, waiting for transfers between devices, on_device(): projection = lax.all_gather(projection, axis, axis=0, tiled=True)  39.4 us
    ppermute x1, waiting for transfers between devices, passed_along(): return lax.ppermute(block, axis, route)  27.6 us
    ppermute x8, starting transfers between devices, passed_along_2(): lax.ppermute(value, axis, [(source, source + steps) for source in range(l...  24.7 us
    all_to_all x1, starting transfers between devices, on_device(): lax.all_to_all(spread, EP, split_axis=0, concat_axis=0, tiled=True)  12 us
    dot_general x1, matrix products, feed_forward(): return jnp.dot(activated, down_part, preferred_element_type=jnp.float32)  9.92 us
    all_to_all x1, starting transfers between devices, on_device(): lax.all_to_all(partial_out.astype(jnp.bfloat16), EP, split_axis=0, concat...  9.78 us
  transfers between devices with their start and end apart: 13, of which 6 were waited for; matrix products, arithmetic and copies ran while one was open for 10% of the time, Pallas kernels for 0%

profile of v2, /device:TPU:32, one launch (start us, length us, event | category | flops | bytes accessed | tf_op | source)
XLA Modules:
  0.0 369.9 jit_solution(9271736330934015404)
XLA Ops:
  7.2 0.0 copy-start
  7.2 0.9 fusion.77
  8.0 0.8 fusion.73
  8.8 0.1 fusion.69
  8.9 0.2 reduce_window_sum.11
  9.1 0.2 select_reduce_fusion
  9.3 1.5 fusion.13
  10.8 1.7 fusion
  12.6 2.5 broadcast_in_dim.108
  15.0 12.0 %all-to-all-start = ((bf16[64,8,4096]{2,1,0:T(8,128)(2,1)}), bf16[64,8,4096]{2,1,0:T(8,128)(2,1)}, u32[]{:S(2)}, u32[]{:S(2)}) async-start(bf16[64,8,4096]{2,1,0:T(8,128)(2,1)} %bitcast.110), calls=%async_computation | async-start | bytes 8388608 | tf_op jit(solution)/shard_map/all_to_all | solution.py:115
  27.0 0.0 all-gather.3.cloned.1.call-start
  27.1 104.3 %all_gather.9 = bf16[256,1280]{1,0:T(8,128)(2,1)} all-gather(bf16[64,1280]{1,0:T(8,128)(2,1)S(1)} %pad_maximum_fusion), channel_id=1, replica_groups=mesh['section'=4,'ep_y'=4,'ep_x'=4,'ep_z'=4] {'ep_z'}, dimensions={0}, use_global_device_ids=true | all-gather | bytes 819200 | tf_op jit(solution)/shard_map/all_gather | solution.py:135
  131.4 0.0 all-gather.3.cloned.1.call-update
  131.5 0.0 all-gather.5.cloned.1.call-start
  131.5 39.4 %all-gather.3.cloned.1.call-done = bf16[1024,1280]{1,0:T(8,128)(2,1)} async-done(((bf16[256,1280]{1,0:T(8,128)(2,1)}), bf16[1024,1280]{1,0:T(8,128)(2,1)}) %all-gather.3.cloned.1.call-update) | async-done | bytes 2621456 | tf_op jit(solution)/shard_map/all_gather | solution.py:135
  170.9 0.0 all-gather.5.cloned.1.call-update
  171.0 6.4 %fusion.3 = f32[512,384]{1,0:T(8,128)} fusion(bf16[64,8,4096]{2,1,0:T(8,128)(2,1)} %all-to-all-done, bf16[1,1,4096,384]{3,2,1,0:T(8,128)(2,1)} %param.14), kind=kOutput, calls=%fused_computation.7 | convolution fusion | flops 1610612736 | bytes 8126464 | tf_op jit(solution)/shard_map/dot_general | solution.py:62
  177.3 9.9 %convolution_convert_fusion = bf16[64,8,4096]{2,1,0:T(8,128)(2,1)} fusion(bf16[1,1,384,4096]{3,2,1,0:T(8,128)(2,1)S(1)} %copy-done, bf16[1,1,4096,384]{3,2,1,0:T(8,128)(2,1)} %param.15, bf16[64,8,4096]{2,1,0:T(8,128)(2,1)} %all-to-all-done, f32[512,384]{1,0:T(8,128)} %fusion.3), kind=kOutput, calls=%fused_computation.2 | convolution fusion | flops 3224502272 | bytes 15466496 | tf_op jit(solution)/shard_map/dot_general | solution.py:65
  187.3 9.8 %all-to-all-start.1 = ((bf16[64,8,4096]{2,1,0:T(8,128)(2,1)}), bf16[64,8,4096]{2,1,0:T(8,128)(2,1)}, u32[]{:S(2)}, u32[]{:S(2)}) async-start(bf16[64,8,4096]{2,1,0:T(8,128)(2,1)} %convolution_convert_fusion), calls=%async_computation.1 | async-start | bytes 8388608 | tf_op jit(solution)/shard_map/all_to_all | solution.py:119
  197.1 3.4 collective-permute-start
  200.4 3.4 collective-permute-start.1
  203.8 4.3 %collective-permute-start.2 = (s32[128]{0:T(128)S(1)}, s32[128]{0:T(128)S(1)}, u32[]{:S(2)}, u32[]{:S(2)}) collective-permute-start(s32[128]{0:T(128)S(1)} %bitcast.119), channel_id=1, source_target_pairs={{0,2},{1,3},{2,4},{3,5},{4,6},{5,7},{6,8},{7,9},{8,10},{9,11},{10,... | collective-permute-start | bytes 1544 | tf_op jit(solution)/shard_map/ppermute | solution.py:44
  208.1 4.5 %collective-permute-start.3 = (s32[128]{0:T(128)S(1)}, s32[128]{0:T(128)S(1)}, u32[]{:S(2)}, u32[]{:S(2)}) collective-permute-start(s32[128]{0:T(128)S(1)} %bitcast.120), channel_id=1, source_target_pairs={{0,1},{1,2},{2,3},{3,4},{4,5},{5,6},{6,7},{7,8},{8,9},{9,10},{10,1... | collective-permute-start | bytes 1544 | tf_op jit(solution)/shard_map/ppermute | solution.py:44
  212.7 1.4 collective-permute-done
  214.1 26.1 %collective-permute-done.1 = s32[128]{0:T(128)S(1)} collective-permute-done((s32[128]{0:T(128)S(1)}, s32[128]{0:T(128)S(1)}, u32[]{:S(2)}, u32[]{:S(2)}) %collective-permute-start.1) | collective-permute-done | bytes 544 | tf_op jit(solution)/shard_map/ppermute | solution.py:44
  240.2 46.3 %collective-permute-done.2 = s32[128]{0:T(128)S(1)} collective-permute-done((s32[128]{0:T(128)S(1)}, s32[128]{0:T(128)S(1)}, u32[]{:S(2)}, u32[]{:S(2)}) %collective-permute-start.2) | collective-permute-done | bytes 544 | tf_op jit(solution)/shard_map/ppermute | solution.py:44
  286.5 0.2 fusion.62
  286.7 0.3 multiply_cosine_fusion
  287.0 6.0 %all-to-all-done.1 = bf16[64,8,4096]{2,1,0:T(8,128)(2,1)} async-done(((bf16[64,8,4096]{2,1,0:T(8,128)(2,1)}), bf16[64,8,4096]{2,1,0:T(8,128)(2,1)}, u32[]{:S(2)}, u32[]{:S(2)}) %all-to-all-start.1) | async-done | bytes 4194336 | tf_op jit(solution)/shard_map/all_to_all | solution.py:119
  293.0 4.5 %convert_reduce_fusion = f32[16,8,4096]{2,1,0:T(8,128)} fusion(bf16[64,8,4096]{2,1,0:T(8,128)(2,1)} %all-to-all-done.1), kind=kLoop, calls=%fused_computation.1 | loop fusion | flops 3670016 | bytes 6291456 | tf_op jit(solution)/shard_map/reduce_sum | solution.py:122
  297.5 5.0 %gather_fusion = f32[128,4096]{1,0:T(8,128)} fusion(f32[128,4096]{1,0:T(8,128)} %bitcast.109, s32[1024]{0:T(1024)S(1)} %pad_clamp_fusion), kind=kCustom, calls=%fused_computation | custom fusion | bytes 4194816 | tf_op jit(solution)/shard_map/jit(_take)/gather | solution.py:125
  302.5 2.6 fusion.15
  305.1 0.1 collective-permute-start.4
  305.2 0.1 compare_and_fusion
  305.4 1.6 fusion.16
  306.9 27.6 %collective-permute-done.4 = bf16[128,4096]{1,0:T(8,128)(2,1)S(1)} collective-permute-done((bf16[128,4096]{1,0:T(8,128)(2,1)S(1)}, bf16[128,4096]{1,0:T(8,128)(2,1)S(1)}, u32[]{:S(2)}, u32[]{:S(2)}) %collective-permute-start.4) | collective-permute-done | bytes 1048608 | tf_op jit(solution)/shard_map/ppermute | solution.py:21
  334.6 1.0 copy-done.5
  335.6 0.3 fusion.17
  335.9 0.0 all-gather.5.cloned.1.call-done
  335.9 5.9 %fusion.47 = f32[128,1280]{1,0:T(8,128)S(1)} fusion(bf16[4096,1280]{1,0:T(8,128)(2,1)} %all-gather.5.cloned.1.call-done, bf16[128,4096]{1,0:T(8,128)(2,1)} %copy-done.5, f32[128]{0:T(128)S(1)} %add_rsqrt_fusion.2), kind=kOutput, calls=%fused_computation.40 | convolution fusion | flops 1343750144 | bytes 12190208 | tf_op jit(solution)/shard_map/dot_general | solution.py:136
  341.9 0.1 multiply_reduce_fusion.1
  342.0 0.1 fusion.70
  342.1 0.1 fusion.65
  342.2 0.1 fusion.67
  342.4 1.9 collective-permute-start.5
  344.3 2.3 collective-permute-start.6
  346.6 1.9 collective-permute-start.7
  348.5 3.1 collective-permute-start.8
  351.6 0.1 copy.26
  351.7 0.8 copy-done.3
  352.5 0.2 multiply_reduce_fusion
  352.7 0.7 copy.19
  353.3 1.3 add_rsqrt_fusion
  354.6 0.8 copy.20
  355.4 1.3 multiply_multiply_fusion
  356.7 0.2 slice_negate_fusion
  357.0 0.3 fusion.60
  357.3 0.8 constant_dynamic-update-slice_fusion.5
  358.2 0.8 constant_dynamic-update-slice_fusion.4
  359.0 0.8 constant_dynamic-update-slice_fusion.3
  359.9 0.8 constant_dynamic-update-slice_fusion.2
  360.7 0.8 fusion.11
  361.6 0.6 fusion.39
  362.2 0.9 copy.23
  (53 shorter events, 0.3 us)
Async XLA Ops:
  7.2 170.2 %copy-start = (bf16[1,1,384,4096]{3,2,1,0:T(8,128)(2,1)S(1)}, bf16[1,1,384,4096]{3,2,1,0:T(8,128)(2,1)}, u32[]{:S(2)}) copy-start(bf16[1,1,384,4096]{3,2,1,0:T(8,128)(2,1)} %param.16) | copy-start | bytes 9437188
  15.0 12.0 %copy-start.6 = (bf16[1,64,1024]{2,1,0:T(8,128)(2,1)S(1)}, bf16[1,64,1024]{2,1,0:T(8,128)(2,1)}, u32[]{:S(2)}) copy-start(bf16[1,64,1024]{2,1,0:T(8,128)(2,1)} %param.17) | copy-start | bytes 393220
  15.0 12.0 %copy-start.8 = (bf16[1,64,256]{2,1,0:T(8,128)(2,1)S(1)}, bf16[1,64,256]{2,1,0:T(8,128)(2,1)}, u32[]{:S(2)}) copy-start(bf16[1,64,256]{2,1,0:T(8,128)(2,1)} %param.18) | copy-start | bytes 98308
  15.0 155.9 %all-to-all-start = ((bf16[64,8,4096]{2,1,0:T(8,128)(2,1)}), bf16[64,8,4096]{2,1,0:T(8,128)(2,1)}, u32[]{:S(2)}, u32[]{:S(2)}) async-start(bf16[64,8,4096]{2,1,0:T(8,128)(2,1)} %bitcast.110), calls=%async_computation | async-start | bytes 8388608 | tf_op jit(solution)/shard_map/all_to_all | solution.py:115
  27.0 143.9 %all-gather.3.cloned.1.call-start = ((), (), s32[]{:S(2)}) async-start(), calls=%async_computation.2 | async-start | bytes 3276800 | tf_op jit(solution)/shard_map/all_gather | solution.py:135
  131.5 204.4 %all-gather.5.cloned.1.call-start = ((), (), s32[]{:S(2)}) async-start(), calls=%async_computation.3 | async-start | bytes 13107200 | tf_op jit(solution)/shard_map/all_gather | solution.py:135
  187.3 9.8 %copy-start.11 = (s32[1,128]{1,0:T(1,128)S(1)}, s32[1,128]{1,0:T(1,128)}, u32[]{:S(2)}) copy-start(s32[1,128]{1,0:T(1,128)} %param.21) | copy-start | bytes 1540
  187.3 25.4 %copy-start.7 = (s32[1,128,8]{1,2,0:T(8,128)S(1)}, s32[1,128,8]{1,2,0:T(8,128)}, u32[]{:S(2)}) copy-start(s32[1,128,8]{1,2,0:T(8,128)} %param.12) | copy-start | bytes 12292
  187.3 25.4 %copy-start.9 = (f32[1,128,8]{1,2,0:T(8,128)S(1)}, f32[1,128,8]{1,2,0:T(8,128)}, u32[]{:S(2)}) copy-start(f32[1,128,8]{1,2,0:T(8,128)} %param.13) | copy-start | bytes 12292
  187.3 105.7 %all-to-all-start.1 = ((bf16[64,8,4096]{2,1,0:T(8,128)(2,1)}), bf16[64,8,4096]{2,1,0:T(8,128)(2,1)}, u32[]{:S(2)}, u32[]{:S(2)}) async-start(bf16[64,8,4096]{2,1,0:T(8,128)(2,1)} %convolution_convert_fusion), calls=%async_computation.1 | async-start | bytes 8388608 | tf_op jit(solution)/shard_map/all_to_all | solution.py:119
  197.1 17.0 %collective-permute-start = (s32[128]{0:T(128)S(1)}, s32[128]{0:T(128)S(1)}, u32[]{:S(2)}, u32[]{:S(2)}) collective-permute-start(s32[128]{0:T(128)S(1)} %bitcast.117), channel_id=1, source_target_pairs={{0,4},{1,5},{2,6},{3,7},{4,8},{5,9},{6,10},{7,11},{8,12},{9,13},{1... | collective-permute-start | bytes 1544 | tf_op jit(solution)/shard_map/ppermute | solution.py:44
  200.4 39.7 %collective-permute-start.1 = (s32[128]{0:T(128)S(1)}, s32[128]{0:T(128)S(1)}, u32[]{:S(2)}, u32[]{:S(2)}) collective-permute-start(s32[128]{0:T(128)S(1)} %bitcast.118), channel_id=1, source_target_pairs={{0,3},{1,4},{2,5},{3,6},{4,7},{5,8},{6,9},{7,10},{8,11},{9,12},{10... | collective-permute-start | bytes 1544 | tf_op jit(solution)/shard_map/ppermute | solution.py:44
  203.8 82.6 %collective-permute-start.2 = (s32[128]{0:T(128)S(1)}, s32[128]{0:T(128)S(1)}, u32[]{:S(2)}, u32[]{:S(2)}) collective-permute-start(s32[128]{0:T(128)S(1)} %bitcast.119), channel_id=1, source_target_pairs={{0,2},{1,3},{2,4},{3,5},{4,6},{5,7},{6,8},{7,9},{8,10},{9,11},{10,... | collective-permute-start | bytes 1544 | tf_op jit(solution)/shard_map/ppermute | solution.py:44
  208.1 78.4 %collective-permute-start.3 = (s32[128]{0:T(128)S(1)}, s32[128]{0:T(128)S(1)}, u32[]{:S(2)}, u32[]{:S(2)}) collective-permute-start(s32[128]{0:T(128)S(1)} %bitcast.120), channel_id=1, source_target_pairs={{0,1},{1,2},{2,3},{3,4},{4,5},{5,6},{6,7},{7,8},{8,9},{9,10},{10,1... | collective-permute-start | bytes 1544 | tf_op jit(solution)/shard_map/ppermute | solution.py:44
  302.5 2.8 copy-start.1
  302.5 2.8 copy-start.2
  305.1 29.4 %collective-permute-start.4 = (bf16[128,4096]{1,0:T(8,128)(2,1)S(1)}, bf16[128,4096]{1,0:T(8,128)(2,1)S(1)}, u32[]{:S(2)}, u32[]{:S(2)}) collective-permute-start(bf16[128,4096]{1,0:T(8,128)(2,1)S(1)} %fusion.15), channel_id=1, source_target_pairs={{192,0},{0,64},{64,128},{128,192},{193,1},{1,65},{65,129},{129,193... | collective-permute-start | bytes 3145736 | tf_op jit(solution)/shard_map/ppermute | solution.py:21
  334.6 1.0 copy-start.5
  335.9 6.1 %copy-start.12 = (f32[1,128]{1,0:T(1,128)S(1)}, f32[1,128]{1,0:T(1,128)}, u32[]{:S(2)}) copy-start(f32[1,128]{1,0:T(1,128)} %param.20) | copy-start | bytes 1540
  335.9 6.3 %copy-start.13 = (f32[1,128]{1,0:T(1,128)S(1)}, f32[1,128]{1,0:T(1,128)}, u32[]{:S(2)}) copy-start(f32[1,128]{1,0:T(1,128)} %param.20) | copy-start | bytes 1540
  342.4 15.0 %collective-permute-start.5 = (bf16[128,256]{1,0:T(8,128)(2,1)S(1)}, bf16[128,256]{1,0:T(8,128)(2,1)}, u32[]{:S(2)}, u32[]{:S(2)}) collective-permute-start(bf16[128,256]{1,0:T(8,128)(2,1)S(1)} %pad_maximum_fusion.3), channel_id=1, source_target_pairs={{0,4},{1,5},{2,6},{3,7},{4,8},{5,9},{6,10},{7,11},{8,12},{9,13},{1... | collective-permute-start | bytes 196616 | tf_op jit(solution)/shard_map/ppermute | solution.py:44
  344.3 13.9 %collective-permute-start.6 = (bf16[128,256]{1,0:T(8,128)(2,1)S(1)}, bf16[128,256]{1,0:T(8,128)(2,1)}, u32[]{:S(2)}, u32[]{:S(2)}) collective-permute-start(bf16[128,256]{1,0:T(8,128)(2,1)S(1)} %pad_maximum_fusion.3), channel_id=1, source_target_pairs={{0,3},{1,4},{2,5},{3,6},{4,7},{5,8},{6,9},{7,10},{8,11},{9,12},{10... | collective-permute-start | bytes 196616 | tf_op jit(solution)/shard_map/ppermute | solution.py:44
  346.6 12.5 %collective-permute-start.7 = (bf16[128,256]{1,0:T(8,128)(2,1)S(1)}, bf16[128,256]{1,0:T(8,128)(2,1)}, u32[]{:S(2)}, u32[]{:S(2)}) collective-permute-start(bf16[128,256]{1,0:T(8,128)(2,1)S(1)} %pad_maximum_fusion.3), channel_id=1, source_target_pairs={{0,2},{1,3},{2,4},{3,5},{4,6},{5,7},{6,8},{7,9},{8,10},{9,11},{10,... | collective-permute-start | bytes 196616 | tf_op jit(solution)/shard_map/ppermute | solution.py:44
  348.5 11.4 %collective-permute-start.8 = (bf16[128,256]{1,0:T(8,128)(2,1)S(1)}, bf16[128,256]{1,0:T(8,128)(2,1)}, u32[]{:S(2)}, u32[]{:S(2)}) collective-permute-start(bf16[128,256]{1,0:T(8,128)(2,1)S(1)} %pad_maximum_fusion.3), channel_id=1, source_target_pairs={{0,1},{1,2},{2,3},{3,4},{4,5},{5,6},{6,7},{7,8},{8,9},{9,10},{10,1... | collective-permute-start | bytes 196616 | tf_op jit(solution)/shard_map/ppermute | solution.py:44
  351.7 0.8 copy-start.3
  355.4 1.5 copy-start.4
  355.4 1.5 copy-start.10
Sparse Core Ops, SparseCore 0:
  131.6 39.2 all-gather.2
  172.7 148.4 all-gather.4

commit v3 on v2

--- a/solution.py
+++ b/solution.py
@@ -112,6 +112,18 @@
         packed.reshape(expert_count, 1, capacity, model_width),
         (expert_count, OWNERS, capacity, model_width),
     ).reshape(device_count, capacity, model_width)
+    segment_row = segment_ids[0]
+    first_index = lax.axis_index(EP) * token_count
+    reach = (SEG_MOST - 1) // token_count + 1
+    segment_pieces = []
+    for distance in range(1, reach + 1):
+        segment_pieces.append(passed_along_2(segment_row, EP, distance))
+    projection = jnp.concatenate([w_query[0], w_keyval[0]], axis=-1)
+    projection = lax.all_gather(projection, EP[-1], axis=0, tiled=True)
+    spread, projection, segment_pieces = lax.optimization_barrier(
+        (spread, projection, segment_pieces)
+    )
+    projection = lax.all_gather(projection, EP[:-1], axis=0, tiled=True)
     received = lax.all_to_all(spread, EP, split_axis=0, concat_axis=0, tiled=True)
     partial_out = feed_forward(
         received.reshape(-1, model_width), gate_part, up_part, down_part
@@ -130,22 +142,13 @@
     head_dim = gain_query.shape[-1]
     query_width = w_query.shape[-1]
     head_count = query_width // head_dim
-    projection = jnp.concatenate([w_query[0], w_keyval[0]], axis=-1)
-    for axis in EP[::-1]:
-        projection = lax.all_gather(projection, axis, axis=0, tiled=True)
     projected = jnp.dot(lifted, projection, preferred_element_type=jnp.float32)
     query_raw = projected[:, :query_width]
     keyval_raw = projected[:, query_width:]
-    segment_row = segment_ids[0]
-    first_index = lax.axis_index(EP) * token_count
     global_index = first_index + jnp.arange(token_count, dtype=jnp.int32)
-    reach = (SEG_MOST - 1) // token_count + 1
     key_index = (
         first_index - reach * token_count + jnp.arange((reach + 1) * token_count, dtype=jnp.int32)
     )
-    segment_pieces = []
-    for distance in range(1, reach + 1):
-        segment_pieces.append(passed_along_2(segment_row, EP, distance))
     window_segment = jnp.concatenate(segment_pieces[::-1] + [segment_row], axis=0)
     window_segment = jnp.where(key_index >= 0, window_segment, -1)
     same_segment = window_segment[None, :] == segment_row[:, None]

time: 373 us -> 348 us (0.933)
  blocking collectives: 104 us -> 15.1 us
  waiting for transfers between devices: 147 us -> 215 us
    all_to_all x1, waiting for transfers between devices: 0.01 us -> 92.7 us  [on_device(): lax.all_to_all(spread, EP, split_axis=0, concat_axis=0, tiled=True)]
    all_gather x1, blocking collectives: 104 us -> 15.1 us  [on_device(): projection = lax.all_gather(projection, EP[-1], axis=0, tiled=True)]
    all_to_all x1, waiting for transfers between devices: 5.98 us -> 93.6 us  [on_device(): lax.all_to_all(partial_out.astype(jnp.bfloat16), EP, split_axis=0, concat...]
    ppermute x8, waiting for transfers between devices: 73.8 us -> 0.02 us  [passed_along_2(): lax.ppermute(value, axis, [(source, source + steps) for source in range(l...]
    all_gather x2 -> x1, waiting for transfers between devices: 39.4 us -> 0.02 us  [on_device(): projection = lax.all_gather(projection, EP[:-1], axis=0, tiled=True)]
  transfers between devices with their start and end apart: 13 -> 12, of which waited for: 6 -> 3; matrix products, arithmetic and copies ran while one was open for 10% -> 13% of each run, Pallas kernels for 0% -> 0%
where the time goes in v3:
time: 348 us; the launch traced here: 346 us
  waiting for transfers between devices  215 us (62%)
  starting transfers between devices  43.3 us (12%)
  matrix products  25.5 us (7%)
  other arithmetic  17.7 us (5%)
  local copies, waits for them, and re-layouts  15.1 us (4%)
  blocking collectives  15.1 us (4%)
  between operations  14.5 us (4%)
    all_to_all x1, waiting for transfers between devices, on_device(): lax.all_to_all(partial_out.astype(jnp.bfloat16), EP, split_axis=0, concat...  93.6 us
    all_to_all x1, waiting for transfers between devices, on_device(): lax.all_to_all(spread, EP, split_axis=0, concat_axis=0, tiled=True)  92.7 us
    ppermute x1, waiting for transfers between devices, passed_along(): return lax.ppermute(block, axis, route)  27.6 us
    ppermute x8, starting transfers between devices, passed_along_2(): lax.ppermute(value, axis, [(source, source + steps) for source in range(l...  25.8 us
    all_gather x1, blocking collectives, on_device(): projection = lax.all_gather(projection, EP[-1], axis=0, tiled=True)  15.1 us
    all_to_all x1, starting transfers between devices, on_device(): lax.all_to_all(spread, EP, split_axis=0, concat_axis=0, tiled=True)  10.9 us
    dot_general x1, matrix products, feed_forward(): return jnp.dot(activated, down_part, preferred_element_type=jnp.float32)  9.96 us
  transfers between devices with their start and end apart: 12, of which 3 were waited for; matrix products, arithmetic and copies ran while one was open for 13% of the time, Pallas kernels for 0%

profile of v3, /device:TPU:32, one launch (start us, length us, event | category | flops | bytes accessed | tf_op | source)
XLA Modules:
  0.0 345.8 jit_solution(1427781803277047902)
XLA Ops:
  7.2 0.0 copy-start
  7.2 4.1 %collective-permute-start = (s32[128]{0:T(128)}, s32[128]{0:T(128)S(1)}, u32[]{:S(2)}, u32[]{:S(2)}) collective-permute-start(s32[128]{0:T(128)} %bitcast.117), channel_id=1, source_target_pairs={{0,1},{1,2},{2,3},{3,4},{4,5},{5,6},{6,7},{7,8},{8,9},{9,10},{10,1... | collective-permute-start | bytes 1544 | tf_op jit(solution)/shard_map/ppermute | solution.py:44
  11.3 3.4 collective-permute-start.1
  14.7 4.7 %collective-permute-start.2 = (s32[128]{0:T(128)}, s32[128]{0:T(128)S(1)}, u32[]{:S(2)}, u32[]{:S(2)}) collective-permute-start(s32[128]{0:T(128)} %bitcast.119), channel_id=1, source_target_pairs={{0,3},{1,4},{2,5},{3,6},{4,7},{5,8},{6,9},{7,10},{8,11},{9,12},{10... | collective-permute-start | bytes 1544 | tf_op jit(solution)/shard_map/ppermute | solution.py:44
  19.4 3.4 collective-permute-start.3
  22.8 0.7 fusion.77
  23.5 0.7 fusion.73
  24.2 0.1 fusion.69
  24.3 0.2 reduce_window_sum.11
  24.5 0.2 select_reduce_fusion
  24.7 1.5 fusion.13
  26.2 0.9 pad_maximum_fusion
  27.2 15.1 %all_gather.6 = bf16[256,1280]{1,0:T(8,128)(2,1)} all-gather(bf16[64,1280]{1,0:T(8,128)(2,1)S(1)} %pad_maximum_fusion), channel_id=1, replica_groups=mesh['section'=4,'ep_y'=4,'ep_x'=4,'ep_z'=4] {'ep_z'}, dimensions={0}, use_global_device_ids=true | all-gather | bytes 819200 | tf_op jit(solution)/shard_map/all_gather | solution.py:122
  42.3 1.7 fusion
  44.0 0.0 collective-permute-done
  44.0 0.0 collective-permute-done.2
  44.1 2.5 broadcast_in_dim.108
  46.5 10.9 %all-to-all-start = ((bf16[64,8,4096]{2,1,0:T(8,128)(2,1)}), bf16[64,8,4096]{2,1,0:T(8,128)(2,1)}, u32[]{:S(2)}, u32[]{:S(2)}) async-start(bf16[64,8,4096]{2,1,0:T(8,128)(2,1)} %bitcast.110), calls=%async_computation | async-start | bytes 8388608 | tf_op jit(solution)/shard_map/all_to_all | solution.py:127
  57.5 0.0 all-gather.2.cloned.1.call-start
  57.5 0.7 all-gather.2.cloned.1.call-update
  58.2 92.7 %all-to-all-done = bf16[64,8,4096]{2,1,0:T(8,128)(2,1)} async-done(((bf16[64,8,4096]{2,1,0:T(8,128)(2,1)}), bf16[64,8,4096]{2,1,0:T(8,128)(2,1)}, u32[]{:S(2)}, u32[]{:S(2)}) %all-to-all-start) | async-done | bytes 4194336 | tf_op jit(solution)/shard_map/all_to_all | solution.py:127
  150.9 6.5 %fusion.3 = f32[512,384]{1,0:T(8,128)} fusion(bf16[64,8,4096]{2,1,0:T(8,128)(2,1)} %all-to-all-done, bf16[1,1,4096,384]{3,2,1,0:T(8,128)(2,1)} %param.14), kind=kOutput, calls=%fused_computation.7 | convolution fusion | flops 1610612736 | bytes 8126464 | tf_op jit(solution)/shard_map/dot_general | solution.py:62
  157.4 10.0 %convolution_convert_fusion = bf16[64,8,4096]{2,1,0:T(8,128)(2,1)} fusion(bf16[1,1,384,4096]{3,2,1,0:T(8,128)(2,1)S(1)} %copy-done, bf16[1,1,4096,384]{3,2,1,0:T(8,128)(2,1)} %param.15, bf16[64,8,4096]{2,1,0:T(8,128)(2,1)} %all-to-all-done, f32[512,384]{1,0:T(8,128)} %fusion.3), kind=kOutput, calls=%fused_computation.2 | convolution fusion | flops 3224502272 | bytes 15466496 | tf_op jit(solution)/shard_map/dot_general | solution.py:65
  167.4 6.3 %all-to-all-start.1 = ((bf16[64,8,4096]{2,1,0:T(8,128)(2,1)}), bf16[64,8,4096]{2,1,0:T(8,128)(2,1)}, u32[]{:S(2)}, u32[]{:S(2)}) async-start(bf16[64,8,4096]{2,1,0:T(8,128)(2,1)} %convolution_convert_fusion), calls=%async_computation.1 | async-start | bytes 8388608 | tf_op jit(solution)/shard_map/all_to_all | solution.py:131
  173.9 0.2 fusion.62
  174.1 0.3 multiply_cosine_fusion
  174.4 93.6 %all-to-all-done.1 = bf16[64,8,4096]{2,1,0:T(8,128)(2,1)} async-done(((bf16[64,8,4096]{2,1,0:T(8,128)(2,1)}), bf16[64,8,4096]{2,1,0:T(8,128)(2,1)}, u32[]{:S(2)}, u32[]{:S(2)}) %all-to-all-start.1) | async-done | bytes 4194336 | tf_op jit(solution)/shard_map/all_to_all | solution.py:131
  267.9 4.5 %convert_reduce_fusion = f32[16,8,4096]{2,1,0:T(8,128)} fusion(bf16[64,8,4096]{2,1,0:T(8,128)(2,1)} %all-to-all-done.1), kind=kLoop, calls=%fused_computation.1 | loop fusion | flops 3670016 | bytes 6291456 | tf_op jit(solution)/shard_map/reduce_sum | solution.py:134
  272.4 5.0 %gather_fusion = f32[128,4096]{1,0:T(8,128)} fusion(f32[128,4096]{1,0:T(8,128)} %bitcast.109, s32[1024]{0:T(1024)S(1)} %pad_clamp_fusion), kind=kCustom, calls=%fused_computation | custom fusion | bytes 4194816 | tf_op jit(solution)/shard_map/jit(_take)/gather | solution.py:137
  277.4 2.6 fusion.15
  280.0 0.3 collective-permute-start.4
  280.3 0.1 compare_and_fusion
  280.5 1.6 fusion.16
  282.0 27.6 %collective-permute-done.4 = bf16[128,4096]{1,0:T(8,128)(2,1)S(1)} collective-permute-done((bf16[128,4096]{1,0:T(8,128)(2,1)S(1)}, bf16[128,4096]{1,0:T(8,128)(2,1)S(1)}, u32[]{:S(2)}, u32[]{:S(2)}) %collective-permute-start.4) | collective-permute-done | bytes 1048608 | tf_op jit(solution)/shard_map/ppermute | solution.py:21
  309.6 1.0 copy-done.5
  310.6 0.3 fusion.17
  310.9 0.0 copy-start.10
  310.9 0.0 all-gather.2.cloned.1.call-done
  310.9 5.9 %fusion.47 = f32[128,1280]{1,0:T(8,128)S(1)} fusion(bf16[4096,1280]{1,0:T(8,128)(2,1)} %all-gather.2.cloned.1.call-done, bf16[128,4096]{1,0:T(8,128)(2,1)} %copy-done.5, f32[128]{0:T(128)S(1)} %add_rsqrt_fusion.2), kind=kOutput, calls=%fused_computation.40 | convolution fusion | flops 1343750144 | bytes 12190208 | tf_op jit(solution)/shard_map/dot_general | solution.py:145
  316.9 0.1 multiply_reduce_fusion.1
  317.0 0.1 fusion.70
  317.1 0.1 fusion.65
  317.2 0.1 fusion.67
  317.4 1.9 collective-permute-start.5
  319.3 3.5 %collective-permute-start.6 = (bf16[128,256]{1,0:T(8,128)(2,1)S(1)}, bf16[128,256]{1,0:T(8,128)(2,1)}, u32[]{:S(2)}, u32[]{:S(2)}) collective-permute-start(bf16[128,256]{1,0:T(8,128)(2,1)S(1)} %pad_maximum_fusion.3), channel_id=1, source_target_pairs={{0,3},{1,4},{2,5},{3,6},{4,7},{5,8},{6,9},{7,10},{8,11},{9,12},{10... | collective-permute-start | bytes 196616 | tf_op jit(solution)/shard_map/ppermute | solution.py:44
  322.8 1.9 collective-permute-start.7
  324.7 2.8 collective-permute-start.8
  327.5 0.1 copy.26
  327.6 0.8 copy-done.3
  328.4 0.2 multiply_reduce_fusion
  328.6 0.7 copy.19
  329.3 1.3 add_rsqrt_fusion
  330.6 0.8 copy.20
  331.4 0.0 copy-start.8
  331.4 1.3 multiply_multiply_fusion
  332.7 0.2 slice_negate_fusion
  332.9 0.3 fusion.60
  333.3 0.8 constant_dynamic-update-slice_fusion.5
  334.1 0.8 constant_dynamic-update-slice_fusion.4
  335.0 0.8 constant_dynamic-update-slice_fusion.3
  335.8 0.8 constant_dynamic-update-slice_fusion.2
  336.7 0.8 fusion.11
  337.5 0.6 fusion.39
  338.1 0.9 copy.23
  (46 shorter events, 0.2 us)
Async XLA Ops:
  7.2 150.2 %copy-start = (bf16[1,1,384,4096]{3,2,1,0:T(8,128)(2,1)S(1)}, bf16[1,1,384,4096]{3,2,1,0:T(8,128)(2,1)}, u32[]{:S(2)}) copy-start(bf16[1,1,384,4096]{3,2,1,0:T(8,128)(2,1)} %param.16) | copy-start | bytes 9437188
  7.2 36.8 %collective-permute-start = (s32[128]{0:T(128)}, s32[128]{0:T(128)S(1)}, u32[]{:S(2)}, u32[]{:S(2)}) collective-permute-start(s32[128]{0:T(128)} %bitcast.117), channel_id=1, source_target_pairs={{0,1},{1,2},{2,3},{3,4},{4,5},{5,6},{6,7},{7,8},{8,9},{9,10},{10,1... | collective-permute-start | bytes 1544 | tf_op jit(solution)/shard_map/ppermute | solution.py:44
  11.3 32.7 %collective-permute-start.1 = (s32[128]{0:T(128)}, s32[128]{0:T(128)S(1)}, u32[]{:S(2)}, u32[]{:S(2)}) collective-permute-start(s32[128]{0:T(128)} %bitcast.118), channel_id=1, source_target_pairs={{0,2},{1,3},{2,4},{3,5},{4,6},{5,7},{6,8},{7,9},{8,10},{9,11},{10,... | collective-permute-start | bytes 1544 | tf_op jit(solution)/shard_map/ppermute | solution.py:44
  14.7 29.4 %collective-permute-start.2 = (s32[128]{0:T(128)}, s32[128]{0:T(128)S(1)}, u32[]{:S(2)}, u32[]{:S(2)}) collective-permute-start(s32[128]{0:T(128)} %bitcast.119), channel_id=1, source_target_pairs={{0,3},{1,4},{2,5},{3,6},{4,7},{5,8},{6,9},{7,10},{8,11},{9,12},{10... | collective-permute-start | bytes 1544 | tf_op jit(solution)/shard_map/ppermute | solution.py:44
  19.4 24.6 %collective-permute-start.3 = (s32[128]{0:T(128)}, s32[128]{0:T(128)S(1)}, u32[]{:S(2)}, u32[]{:S(2)}) collective-permute-start(s32[128]{0:T(128)} %bitcast.120), channel_id=1, source_target_pairs={{0,4},{1,5},{2,6},{3,7},{4,8},{5,9},{6,10},{7,11},{8,12},{9,13},{1... | collective-permute-start | bytes 1544 | tf_op jit(solution)/shard_map/ppermute | solution.py:44
  46.5 104.4 %all-to-all-start = ((bf16[64,8,4096]{2,1,0:T(8,128)(2,1)}), bf16[64,8,4096]{2,1,0:T(8,128)(2,1)}, u32[]{:S(2)}, u32[]{:S(2)}) async-start(bf16[64,8,4096]{2,1,0:T(8,128)(2,1)} %bitcast.110), calls=%async_computation | async-start | bytes 8388608 | tf_op jit(solution)/shard_map/all_to_all | solution.py:127
  57.5 253.4 %all-gather.2.cloned.1.call-start = ((), (), s32[]{:S(2)}) async-start(), calls=%async_computation.2 | async-start | bytes 11141120 | tf_op jit(solution)/shard_map/all_gather | solution.py:126
  167.3 6.4 %copy-start.6 = (s32[1,128,8]{1,2,0:T(8,128)S(1)}, s32[1,128,8]{1,2,0:T(8,128)}, u32[]{:S(2)}) copy-start(s32[1,128,8]{1,2,0:T(8,128)} %param.12) | copy-start | bytes 12292
  167.3 6.4 %copy-start.7 = (f32[1,128,8]{1,2,0:T(8,128)S(1)}, f32[1,128,8]{1,2,0:T(8,128)}, u32[]{:S(2)}) copy-start(f32[1,128,8]{1,2,0:T(8,128)} %param.13) | copy-start | bytes 12292
  167.3 6.5 %copy-start.9 = (s32[1,128]{1,0:T(1,128)S(1)}, s32[1,128]{1,0:T(1,128)}, u32[]{:S(2)}) copy-start(s32[1,128]{1,0:T(1,128)} %param.21) | copy-start | bytes 1540
  167.4 100.6 %all-to-all-start.1 = ((bf16[64,8,4096]{2,1,0:T(8,128)(2,1)}), bf16[64,8,4096]{2,1,0:T(8,128)(2,1)}, u32[]{:S(2)}, u32[]{:S(2)}) async-start(bf16[64,8,4096]{2,1,0:T(8,128)(2,1)} %convolution_convert_fusion), calls=%async_computation.1 | async-start | bytes 8388608 | tf_op jit(solution)/shard_map/all_to_all | solution.py:131
  277.4 3.0 copy-start.1
  277.4 3.0 copy-start.2
  280.0 29.6 %collective-permute-start.4 = (bf16[128,4096]{1,0:T(8,128)(2,1)S(1)}, bf16[128,4096]{1,0:T(8,128)(2,1)S(1)}, u32[]{:S(2)}, u32[]{:S(2)}) collective-permute-start(bf16[128,4096]{1,0:T(8,128)(2,1)S(1)} %fusion.15), channel_id=1, source_target_pairs={{192,0},{0,64},{64,128},{128,192},{193,1},{1,65},{65,129},{129,193... | collective-permute-start | bytes 3145736 | tf_op jit(solution)/shard_map/ppermute | solution.py:21
  309.6 1.0 copy-start.5
  310.9 6.1 %copy-start.10 = (f32[1,128]{1,0:T(1,128)S(1)}, f32[1,128]{1,0:T(1,128)}, u32[]{:S(2)}) copy-start(f32[1,128]{1,0:T(1,128)} %param.20) | copy-start | bytes 1540
  310.9 6.3 %copy-start.11 = (f32[1,128]{1,0:T(1,128)S(1)}, f32[1,128]{1,0:T(1,128)}, u32[]{:S(2)}) copy-start(f32[1,128]{1,0:T(1,128)} %param.20) | copy-start | bytes 1540
  317.4 15.9 %collective-permute-start.5 = (bf16[128,256]{1,0:T(8,128)(2,1)S(1)}, bf16[128,256]{1,0:T(8,128)(2,1)}, u32[]{:S(2)}, u32[]{:S(2)}) collective-permute-start(bf16[128,256]{1,0:T(8,128)(2,1)S(1)} %pad_maximum_fusion.3), channel_id=1, source_target_pairs={{0,4},{1,5},{2,6},{3,7},{4,8},{5,9},{6,10},{7,11},{8,12},{9,13},{1... | collective-permute-start | bytes 196616 | tf_op jit(solution)/shard_map/ppermute | solution.py:44
  319.3 14.8 %collective-permute-start.6 = (bf16[128,256]{1,0:T(8,128)(2,1)S(1)}, bf16[128,256]{1,0:T(8,128)(2,1)}, u32[]{:S(2)}, u32[]{:S(2)}) collective-permute-start(bf16[128,256]{1,0:T(8,128)(2,1)S(1)} %pad_maximum_fusion.3), channel_id=1, source_target_pairs={{0,3},{1,4},{2,5},{3,6},{4,7},{5,8},{6,9},{7,10},{8,11},{9,12},{10... | collective-permute-start | bytes 196616 | tf_op jit(solution)/shard_map/ppermute | solution.py:44
  322.8 12.2 %collective-permute-start.7 = (bf16[128,256]{1,0:T(8,128)(2,1)S(1)}, bf16[128,256]{1,0:T(8,128)(2,1)}, u32[]{:S(2)}, u32[]{:S(2)}) collective-permute-start(bf16[128,256]{1,0:T(8,128)(2,1)S(1)} %pad_maximum_fusion.3), channel_id=1, source_target_pairs={{0,2},{1,3},{2,4},{3,5},{4,6},{5,7},{6,8},{7,9},{8,10},{9,11},{10,... | collective-permute-start | bytes 196616 | tf_op jit(solution)/shard_map/ppermute | solution.py:44
  324.7 11.1 %collective-permute-start.8 = (bf16[128,256]{1,0:T(8,128)(2,1)S(1)}, bf16[128,256]{1,0:T(8,128)(2,1)}, u32[]{:S(2)}, u32[]{:S(2)}) collective-permute-start(bf16[128,256]{1,0:T(8,128)(2,1)S(1)} %pad_maximum_fusion.3), channel_id=1, source_target_pairs={{0,1},{1,2},{2,3},{3,4},{4,5},{5,6},{6,7},{7,8},{8,9},{9,10},{10,1... | collective-permute-start | bytes 196616 | tf_op jit(solution)/shard_map/ppermute | solution.py:44
  327.6 0.8 copy-start.3
  331.4 1.5 copy-start.4
  331.4 1.5 copy-start.8
Sparse Core Ops, SparseCore 0:
  60.7 110.5 all-gather.1

commit v4 on v3

--- a/solution.py
+++ b/solution.py
@@ -108,10 +108,6 @@
     gate_part = w_gate[0, 0]
     up_part = w_up[0, 0]
     down_part = w_down[0, 0]
-    spread = jnp.broadcast_to(
-        packed.reshape(expert_count, 1, capacity, model_width),
-        (expert_count, OWNERS, capacity, model_width),
-    ).reshape(device_count, capacity, model_width)
     segment_row = segment_ids[0]
     first_index = lax.axis_index(EP) * token_count
     reach = (SEG_MOST - 1) // token_count + 1
@@ -120,20 +116,30 @@
         segment_pieces.append(passed_along_2(segment_row, EP, distance))
     projection = jnp.concatenate([w_query[0], w_keyval[0]], axis=-1)
     projection = lax.all_gather(projection, EP[-1], axis=0, tiled=True)
-    spread, projection, segment_pieces = lax.optimization_barrier(
-        (spread, projection, segment_pieces)
+    packed, projection, segment_pieces = lax.optimization_barrier(
+        (packed, projection, segment_pieces)
     )
     projection = lax.all_gather(projection, EP[:-1], axis=0, tiled=True)
-    received = lax.all_to_all(spread, EP, split_axis=0, concat_axis=0, tiled=True)
-    partial_out = feed_forward(
-        received.reshape(-1, model_width), gate_part, up_part, down_part
-    ).reshape(received.shape)
-    returned_rows = lax.all_to_all(
-        partial_out.astype(jnp.bfloat16), EP, split_axis=0, concat_axis=0, tiled=True
-    ).astype(partial_out.dtype)
-    merged = jnp.sum(
-        returned_rows.reshape(expert_count, OWNERS, capacity, model_width), axis=1
-    ).reshape(expert_count * capacity, model_width)
+    group_axes, owner_axis = EP[:-1], EP[-1]
+    crossed = lax.all_to_all(
+        packed.reshape(expert_count, capacity, model_width),
+        group_axes,
+        split_axis=0,
+        concat_axis=0,
+        tiled=True,
+    )
+    received = lax.all_gather(crossed, owner_axis, axis=0, tiled=True)
+    partial_out = feed_forward(received, gate_part, up_part, down_part)
+    reduced = lax.psum_scatter(
+        partial_out.astype(jnp.bfloat16), owner_axis, scatter_dimension=0, tiled=True
+    )
+    merged = lax.all_to_all(
+        reduced.reshape(expert_count, capacity, model_width),
+        group_axes,
+        split_axis=0,
+        concat_axis=0,
+        tiled=True,
+    ).astype(jnp.float32).reshape(expert_count * capacity, model_width)
     fetched_rows = jnp.take(merged, jnp.maximum(slot_index, 0), axis=0)
     expert_out = jnp.where(has_route[:, None], fetched_rows, 0.0)
     layer_out = (wide_tokens + weight_kept[:, None] * expert_out).astype(jnp.bfloat16)

time: 348 us -> 352 us (1.011)
  blocking collectives: 15.1 us -> 36.3 us
  waiting for transfers between devices: 215 us -> 207 us
  starting transfers between devices: 43.3 us -> 36.9 us
    all_to_all x2 -> x1, waiting for transfers between devices: 186 us -> 17.1 us  [on_device(): lax.all_to_all(reduced.reshape(expert_count, capacity, model_width), grou...]
    all_gather x0 -> x1, waiting for transfers between devices: none -> 83 us  [on_device(): received = lax.all_gather(crossed, owner_axis, axis=0, tiled=True)]
    reduce_scatter x0 -> x1, waiting for transfers between devices: none -> 81.5 us  [on_device(): lax.psum_scatter(partial_out.astype(jnp.bfloat16), owner_axis, scatter_di...]
    all_to_all x0 -> x1, blocking collectives: none -> 21.2 us  [on_device(): lax.all_to_all(packed.reshape(expert_count, capacity, model_width), group...]
    all_to_all x2 -> x1, starting transfers between devices: 17.2 us -> 6.85 us  [on_device(): lax.all_to_all(reduced.reshape(expert_count, capacity, model_width), grou...]
    reduce_sum x1 -> x0, other arithmetic: 4.48 us -> none  [on_device(): jnp.sum(returned_rows.reshape(expert_count, OWNERS, capacity, model_width...]
    ppermute x8, starting transfers between devices: 25.8 us -> 29.6 us  [passed_along_2(): lax.ppermute(value, axis, [(source, source + steps) for source in range(l...]
  transfers between devices with their start and end apart: 12 -> 13, of which waited for: 3 -> 4; matrix products, arithmetic and copies ran while one was open for 13% -> 8% of each run, Pallas kernels for 0% -> 0%
where the time goes in v4:
time: 352 us; the launch traced here: 351 us
  waiting for transfers between devices  207 us (59%)
  starting transfers between devices  36.9 us (10%)
  blocking collectives  36.3 us (10%)
  matrix products  26.3 us (7%)
  between operations  16 us (5%)
  other arithmetic  15.8 us (4%)
  local copies, waits for them, and re-layouts  12.7 us (4%)
    all_gather x1, waiting for transfers between devices, on_device(): received = lax.all_gather(crossed, owner_axis, axis=0, tiled=True)  83 us
    reduce_scatter x1, waiting for transfers between devices, on_device(): lax.psum_scatter(partial_out.astype(jnp.bfloat16), owner_axis, scatter_di...  81.5 us
    ppermute x8, starting transfers between devices, passed_along_2(): lax.ppermute(value, axis, [(source, source + steps) for source in range(l...  29.6 us
    ppermute x1, waiting for transfers between devices, passed_along(): return lax.ppermute(block, axis, route)  25.2 us
    all_to_all x1, blocking collectives, on_device(): lax.all_to_all(packed.reshape(expert_count, capacity, model_width), group...  21.2 us
    all_to_all x1, waiting for transfers between devices, on_device(): lax.all_to_all(reduced.reshape(expert_count, capacity, model_width), grou...  17.1 us
    all_gather x1, blocking collectives, on_device(): projection = lax.all_gather(projection, EP[-1], axis=0, tiled=True)  15.1 us
    dot_general x1, matrix products, feed_forward(): return jnp.dot(activated, down_part, preferred_element_type=jnp.float32)  9.84 us
  transfers between devices with their start and end apart: 13, of which 4 were waited for; matrix products, arithmetic and copies ran while one was open for 8% of the time, Pallas kernels for 0%

profile of v4, /device:TPU:32, one launch (start us, length us, event | category | flops | bytes accessed | tf_op | source)
XLA Modules:
  0.0 351.3 jit_solution(4174123503561676189)
XLA Ops:
  8.0 0.0 copy-start
  8.0 0.0 all-gather.3.cloned.1.call-start
  8.1 4.1 %collective-permute-start = (s32[128]{0:T(128)}, s32[128]{0:T(128)S(1)}, u32[]{:S(2)}, u32[]{:S(2)}) collective-permute-start(s32[128]{0:T(128)} %bitcast.100), channel_id=1, source_target_pairs={{0,1},{1,2},{2,3},{3,4},{4,5},{5,6},{6,7},{7,8},{8,9},{9,10},{10,1... | collective-permute-start | bytes 1544 | tf_op jit(solution)/shard_map/ppermute | solution.py:44
  12.2 3.4 collective-permute-start.1
  15.6 4.7 %collective-permute-start.2 = (s32[128]{0:T(128)}, s32[128]{0:T(128)S(1)}, u32[]{:S(2)}, u32[]{:S(2)}) collective-permute-start(s32[128]{0:T(128)} %bitcast.102), channel_id=1, source_target_pairs={{0,3},{1,4},{2,5},{3,6},{4,7},{5,8},{6,9},{7,10},{8,11},{9,12},{10... | collective-permute-start | bytes 1544 | tf_op jit(solution)/shard_map/ppermute | solution.py:44
  20.3 3.4 collective-permute-start.3
  23.7 0.7 fusion.60
  24.4 0.7 fusion.56
  25.1 0.1 fusion.52
  25.2 0.2 reduce_window_sum.11
  25.4 0.2 select_reduce_fusion
  25.6 1.5 fusion.10
  27.1 2.7 convolution_convert_fusion.1
  29.9 15.1 %all_gather.9 = bf16[256,1280]{1,0:T(8,128)(2,1)} all-gather(bf16[64,1280]{1,0:T(8,128)(2,1)S(1)} %pad_maximum_fusion), channel_id=1, replica_groups=mesh['section'=4,'ep_y'=4,'ep_x'=4,'ep_z'=4] {'ep_z'}, dimensions={0}, use_global_device_ids=true | all-gather | bytes 819200 | tf_op jit(solution)/shard_map/all_gather | solution.py:118
  45.0 21.2 %all_to_all.10 = bf16[16,8,4096]{2,1,0:T(8,128)(2,1)} all-to-all(bf16[16,8,4096]{2,1,0:T(8,128)(2,1)} %bitcast.94), channel_id=1, replica_groups=mesh['section'=4,'ep_y'=4,'ep_x'=4,'ep_z'=4] {'ep_y','ep_x'}, dimensions={0} | all-to-all | bytes 2097152 | tf_op jit(solution)/shard_map/all_to_all | solution.py:124
  66.2 0.0 all-gather.3.cloned.1.call-update
  66.2 0.0 reduce-scatter.2.cloned.1.call-start
  66.3 83.0 %all-gather.3.cloned.1.call-done = bf16[64,8,4096]{2,1,0:T(8,128)(2,1)} async-done(((bf16[16,8,4096]{2,1,0:T(8,128)(2,1)}), bf16[64,8,4096]{2,1,0:T(8,128)(2,1)}) %all-gather.3.cloned.1.call-update) | async-done | bytes 4194320 | tf_op jit(solution)/shard_map/all_gather | solution.py:131
  149.3 6.4 %fusion.3 = f32[64,8,384]{2,1,0:T(8,128)} fusion(bf16[64,8,4096]{2,1,0:T(8,128)(2,1)} %all-gather.3.cloned.1.call-done, bf16[1,1,4096,384]{3,2,1,0:T(8,128)(2,1)} %param.14), kind=kOutput, calls=%fused_computation.6 | convolution fusion | flops 1610612736 | bytes 8126464 | tf_op jit(solution)/shard_map/dot_general | solution.py:62
  155.7 9.8 %convolution_convert_fusion = bf16[64,8,4096]{2,1,0:T(8,128)(2,1)} fusion(bf16[1,1,384,4096]{3,2,1,0:T(8,128)(2,1)S(1)} %copy-done, bf16[64,8,4096]{2,1,0:T(8,128)(2,1)} %all-gather.3.cloned.1.call-done, bf16[1,1,4096,384]{3,2,1,0:T(8,128)(2,1)} %param.15, f32[64,8,384]{2,1,0:T(8,128)} %fusion.3), kind=kOutput, calls=%fused_computation.1 | convolution fusion | flops 3224502272 | bytes 15466496 | tf_op jit(solution)/shard_map/dot_general | solution.py:65
  165.5 0.0 reduce-scatter.2.cloned.1.call-update
  165.5 0.0 all-gather.5.cloned.1.call-start
  165.6 0.5 all-gather.5.cloned.1.call-update
  166.2 0.0 copy-done.10
  166.3 81.5 %reduce-scatter.2.cloned.1.call-done = bf16[16,8,4096]{2,1,0:T(8,128)(2,1)} async-done(((bf16[64,8,4096]{2,1,0:T(8,128)(2,1)}), bf16[16,8,4096]{2,1,0:T(8,128)(2,1)}) %reduce-scatter.2.cloned.1.call-update) | async-done | bytes 1048592 | tf_op jit(solution)/shard_map/reduce_scatter | solution.py:133
  247.8 6.9 %all-to-all-start.1 = ((bf16[16,8,4096]{2,1,0:T(8,128)(2,1)}), bf16[16,8,4096]{2,1,0:T(8,128)(2,1)}, u32[]{:S(2)}, u32[]{:S(2)}) async-start(bf16[16,8,4096]{2,1,0:T(8,128)(2,1)} %reduce-scatter.2.cloned.1.call-done), calls=%async_computation.2 | async-start | bytes 2097152 | tf_op jit(solution)/shard_map/all_to_all | solution.py:136
  254.7 0.2 fusion.45
  254.9 0.3 multiply_cosine_fusion
  255.2 17.1 %all-to-all-done.1 = bf16[16,8,4096]{2,1,0:T(8,128)(2,1)} async-done(((bf16[16,8,4096]{2,1,0:T(8,128)(2,1)}), bf16[16,8,4096]{2,1,0:T(8,128)(2,1)}, u32[]{:S(2)}, u32[]{:S(2)}) %all-to-all-start.1) | async-done | bytes 1048608 | tf_op jit(solution)/shard_map/all_to_all | solution.py:136
  272.3 2.8 bitcast_convert_fusion
  275.1 5.0 %gather_fusion = f32[128,4096]{1,0:T(8,128)} fusion(f32[128,4096]{1,0:T(8,128)} %bitcast_convert_fusion, s32[1024]{0:T(1024)S(1)} %pad_clamp_fusion), kind=kCustom, calls=%fused_computation | custom fusion | bytes 4194816 | tf_op jit(solution)/shard_map/jit(_take)/gather | solution.py:143
  280.1 2.6 fusion.12
  282.7 0.3 collective-permute-start.4
  283.0 0.1 compare_and_fusion
  283.1 2.2 fusion.13
  285.4 25.2 %collective-permute-done.4 = bf16[128,4096]{1,0:T(8,128)(2,1)S(1)} collective-permute-done((bf16[128,4096]{1,0:T(8,128)(2,1)S(1)}, bf16[128,4096]{1,0:T(8,128)(2,1)S(1)}, u32[]{:S(2)}, u32[]{:S(2)}) %collective-permute-start.4) | collective-permute-done | bytes 1048608 | tf_op jit(solution)/shard_map/ppermute | solution.py:21
  310.6 1.0 copy-done.5
  311.6 0.3 fusion.14
  311.9 0.0 all-gather.5.cloned.1.call-done
  311.9 5.9 %fusion.35 = f32[128,1280]{1,0:T(8,128)S(1)} fusion(bf16[4096,1280]{1,0:T(8,128)(2,1)} %all-gather.5.cloned.1.call-done, bf16[128,4096]{1,0:T(8,128)(2,1)} %copy-done.5, f32[128]{0:T(128)S(1)} %add_rsqrt_fusion.2), kind=kOutput, calls=%fused_computation.35 | convolution fusion | flops 1343750144 | bytes 12190208 | tf_op jit(solution)/shard_map/dot_general | solution.py:151
  317.9 0.1 multiply_reduce_fusion.1
  318.0 0.1 fusion.53
  318.1 0.1 fusion.48
  318.2 0.1 fusion.50
  318.4 3.0 collective-permute-start.5
  321.4 1.9 collective-permute-start.6
  323.3 5.9 %collective-permute-start.7 = (bf16[128,256]{1,0:T(8,128)(2,1)S(1)}, bf16[128,256]{1,0:T(8,128)(2,1)}, u32[]{:S(2)}, u32[]{:S(2)}) collective-permute-start(bf16[128,256]{1,0:T(8,128)(2,1)S(1)} %pad_maximum_fusion.3), channel_id=1, source_target_pairs={{0,2},{1,3},{2,4},{3,5},{4,6},{5,7},{6,8},{7,9},{8,10},{9,11},{10,... | collective-permute-start | bytes 196616 | tf_op jit(solution)/shard_map/ppermute | solution.py:44
  329.2 3.2 collective-permute-start.8
  332.4 0.1 copy.26
  332.5 0.8 copy-done.3
  333.3 0.2 multiply_reduce_fusion
  333.5 0.7 copy.19
  334.2 1.3 add_rsqrt_fusion
  335.5 0.8 copy.20
  336.3 1.3 multiply_multiply_fusion
  337.6 0.2 slice_negate_fusion
  337.8 0.3 fusion.43
  338.2 0.8 constant_dynamic-update-slice_fusion.5
  339.0 0.8 constant_dynamic-update-slice_fusion.4
  339.9 0.8 constant_dynamic-update-slice_fusion.3
  340.7 0.8 constant_dynamic-update-slice_fusion.2
  341.6 0.8 fusion.8
  342.4 0.6 fusion.32
  343.0 0.9 copy.23
  (56 shorter events, 0.3 us)
Async XLA Ops:
  8.0 147.7 %copy-start = (bf16[1,1,384,4096]{3,2,1,0:T(8,128)(2,1)S(1)}, bf16[1,1,384,4096]{3,2,1,0:T(8,128)(2,1)}, u32[]{:S(2)}) copy-start(bf16[1,1,384,4096]{3,2,1,0:T(8,128)(2,1)} %param.16) | copy-start | bytes 9437188
  8.0 21.8 %copy-start.6 = (bf16[1,64,1024]{2,1,0:T(8,128)(2,1)S(1)}, bf16[1,64,1024]{2,1,0:T(8,128)(2,1)}, u32[]{:S(2)}) copy-start(bf16[1,64,1024]{2,1,0:T(8,128)(2,1)} %param.17) | copy-start | bytes 393220
  8.0 21.8 %copy-start.8 = (bf16[1,64,256]{2,1,0:T(8,128)(2,1)S(1)}, bf16[1,64,256]{2,1,0:T(8,128)(2,1)}, u32[]{:S(2)}) copy-start(bf16[1,64,256]{2,1,0:T(8,128)(2,1)} %param.18) | copy-start | bytes 98308
  8.0 141.3 %all-gather.3.cloned.1.call-start = ((), (), s32[]{:S(2)}) async-start(), calls=%async_computation.3 | async-start | bytes 5242880 | tf_op jit(solution)/shard_map/all_gather | solution.py:131
  8.1 36.9 %collective-permute-start = (s32[128]{0:T(128)}, s32[128]{0:T(128)S(1)}, u32[]{:S(2)}, u32[]{:S(2)}) collective-permute-start(s32[128]{0:T(128)} %bitcast.100), channel_id=1, source_target_pairs={{0,1},{1,2},{2,3},{3,4},{4,5},{5,6},{6,7},{7,8},{8,9},{9,10},{10,1... | collective-permute-start | bytes 1544 | tf_op jit(solution)/shard_map/ppermute | solution.py:44
  12.2 32.8 %collective-permute-start.1 = (s32[128]{0:T(128)}, s32[128]{0:T(128)S(1)}, u32[]{:S(2)}, u32[]{:S(2)}) collective-permute-start(s32[128]{0:T(128)} %bitcast.101), channel_id=1, source_target_pairs={{0,2},{1,3},{2,4},{3,5},{4,6},{5,7},{6,8},{7,9},{8,10},{9,11},{10,... | collective-permute-start | bytes 1544 | tf_op jit(solution)/shard_map/ppermute | solution.py:44
  15.6 29.4 %collective-permute-start.2 = (s32[128]{0:T(128)}, s32[128]{0:T(128)S(1)}, u32[]{:S(2)}, u32[]{:S(2)}) collective-permute-start(s32[128]{0:T(128)} %bitcast.102), channel_id=1, source_target_pairs={{0,3},{1,4},{2,5},{3,6},{4,7},{5,8},{6,9},{7,10},{8,11},{9,12},{10... | collective-permute-start | bytes 1544 | tf_op jit(solution)/shard_map/ppermute | solution.py:44
  20.3 24.7 %collective-permute-start.3 = (s32[128]{0:T(128)}, s32[128]{0:T(128)S(1)}, u32[]{:S(2)}, u32[]{:S(2)}) collective-permute-start(s32[128]{0:T(128)} %bitcast.103), channel_id=1, source_target_pairs={{0,4},{1,5},{2,6},{3,7},{4,8},{5,9},{6,10},{7,11},{8,12},{9,13},{1... | collective-permute-start | bytes 1544 | tf_op jit(solution)/shard_map/ppermute | solution.py:44
  24.4 255.7 %copy-start.9 = (pred[128]{0:T(512)(128)(4,1)}, pred[128]{0:T(512)(128)(4,1)S(1)}, u32[]{:S(2)}) copy-start(pred[128]{0:T(512)(128)(4,1)S(1)} %fusion.60) | copy-start | bytes 388
  66.2 181.6 %reduce-scatter.2.cloned.1.call-start = ((), (), s32[]{:S(2)}) async-start(), calls=%async_computation.4 | async-start | bytes 5242880 | tf_op jit(solution)/shard_map/reduce_scatter | solution.py:133
  165.5 0.7 copy-start.7
  165.5 0.7 copy-start.10
  165.5 89.1 %copy-start.12 = (s32[1,128]{1,0:T(1,128)S(1)}, s32[1,128]{1,0:T(1,128)}, u32[]{:S(2)}) copy-start(s32[1,128]{1,0:T(1,128)} %param.21) | copy-start | bytes 1540
  165.5 146.4 %all-gather.5.cloned.1.call-start = ((), (), s32[]{:S(2)}) async-start(), calls=%async_computation.5 | async-start | bytes 11141120 | tf_op jit(solution)/shard_map/all_gather | solution.py:122
  247.8 24.5 %all-to-all-start.1 = ((bf16[16,8,4096]{2,1,0:T(8,128)(2,1)}), bf16[16,8,4096]{2,1,0:T(8,128)(2,1)}, u32[]{:S(2)}, u32[]{:S(2)}) async-start(bf16[16,8,4096]{2,1,0:T(8,128)(2,1)} %reduce-scatter.2.cloned.1.call-done), calls=%async_computation.2 | async-start | bytes 2097152 | tf_op jit(solution)/shard_map/all_to_all | solution.py:136
  280.1 3.0 copy-start.1
  280.1 3.0 copy-start.2
  282.7 27.9 %collective-permute-start.4 = (bf16[128,4096]{1,0:T(8,128)(2,1)S(1)}, bf16[128,4096]{1,0:T(8,128)(2,1)S(1)}, u32[]{:S(2)}, u32[]{:S(2)}) collective-permute-start(bf16[128,4096]{1,0:T(8,128)(2,1)S(1)} %fusion.12), channel_id=1, source_target_pairs={{192,0},{0,64},{64,128},{128,192},{193,1},{1,65},{65,129},{129,193... | collective-permute-start | bytes 3145736 | tf_op jit(solution)/shard_map/ppermute | solution.py:21
  310.6 1.0 copy-start.5
  311.9 6.1 %copy-start.13 = (f32[1,128]{1,0:T(1,128)S(1)}, f32[1,128]{1,0:T(1,128)}, u32[]{:S(2)}) copy-start(f32[1,128]{1,0:T(1,128)} %param.20) | copy-start | bytes 1540
  311.9 6.3 %copy-start.14 = (f32[1,128]{1,0:T(1,128)S(1)}, f32[1,128]{1,0:T(1,128)}, u32[]{:S(2)}) copy-start(f32[1,128]{1,0:T(1,128)} %param.20) | copy-start | bytes 1540
  318.4 19.8 %collective-permute-start.5 = (bf16[128,256]{1,0:T(8,128)(2,1)S(1)}, bf16[128,256]{1,0:T(8,128)(2,1)}, u32[]{:S(2)}, u32[]{:S(2)}) collective-permute-start(bf16[128,256]{1,0:T(8,128)(2,1)S(1)} %pad_maximum_fusion.3), channel_id=1, source_target_pairs={{0,4},{1,5},{2,6},{3,7},{4,8},{5,9},{6,10},{7,11},{8,12},{9,13},{1... | collective-permute-start | bytes 196616 | tf_op jit(solution)/shard_map/ppermute | solution.py:44
  321.4 17.7 %collective-permute-start.6 = (bf16[128,256]{1,0:T(8,128)(2,1)S(1)}, bf16[128,256]{1,0:T(8,128)(2,1)}, u32[]{:S(2)}, u32[]{:S(2)}) collective-permute-start(bf16[128,256]{1,0:T(8,128)(2,1)S(1)} %pad_maximum_fusion.3), channel_id=1, source_target_pairs={{0,3},{1,4},{2,5},{3,6},{4,7},{5,8},{6,9},{7,10},{8,11},{9,12},{10... | collective-permute-start | bytes 196616 | tf_op jit(solution)/shard_map/ppermute | solution.py:44
  323.3 16.6 %collective-permute-start.7 = (bf16[128,256]{1,0:T(8,128)(2,1)S(1)}, bf16[128,256]{1,0:T(8,128)(2,1)}, u32[]{:S(2)}, u32[]{:S(2)}) collective-permute-start(bf16[128,256]{1,0:T(8,128)(2,1)S(1)} %pad_maximum_fusion.3), channel_id=1, source_target_pairs={{0,2},{1,3},{2,4},{3,5},{4,6},{5,7},{6,8},{7,9},{8,10},{9,11},{10,... | collective-permute-start | bytes 196616 | tf_op jit(solution)/shard_map/ppermute | solution.py:44
  329.2 11.6 %collective-permute-start.8 = (bf16[128,256]{1,0:T(8,128)(2,1)S(1)}, bf16[128,256]{1,0:T(8,128)(2,1)}, u32[]{:S(2)}, u32[]{:S(2)}) collective-permute-start(bf16[128,256]{1,0:T(8,128)(2,1)S(1)} %pad_maximum_fusion.3), channel_id=1, source_target_pairs={{0,1},{1,2},{2,3},{3,4},{4,5},{5,6},{6,7},{7,8},{8,9},{9,10},{10,1... | collective-permute-start | bytes 196616 | tf_op jit(solution)/shard_map/ppermute | solution.py:44
  332.5 0.8 copy-start.3
  336.3 1.5 copy-start.4
  336.3 1.6 copy-start.11
Sparse Core Ops, SparseCore 0:
  66.3 82.9 all-gather.2
  165.6 82.0 reduce-scatter.1
Sparse Core Ops, SparseCore 1:
  168.4 85.5 all-gather.4

commit v5 on v3

--- a/solution.py
+++ b/solution.py
@@ -115,14 +115,15 @@
     segment_row = segment_ids[0]
     first_index = lax.axis_index(EP) * token_count
     reach = (SEG_MOST - 1) // token_count + 1
-    segment_pieces = []
-    for distance in range(1, reach + 1):
-        segment_pieces.append(passed_along_2(segment_row, EP, distance))
-    projection = jnp.concatenate([w_query[0], w_keyval[0]], axis=-1)
+    shard_rows = w_query.shape[1]
+    per_row = -(-token_count // shard_rows)
+    carried = jnp.pad(segment_row, (0, shard_rows * per_row - token_count)).reshape(
+        shard_rows, per_row
+    )
+    carried = jnp.pad(carried.astype(jnp.bfloat16), ((0, 0), (0, 128 - per_row)))
+    projection = jnp.concatenate([w_query[0], w_keyval[0], carried], axis=-1)
     projection = lax.all_gather(projection, EP[-1], axis=0, tiled=True)
-    spread, projection, segment_pieces = lax.optimization_barrier(
-        (spread, projection, segment_pieces)
-    )
+    spread, projection = lax.optimization_barrier((spread, projection))
     projection = lax.all_gather(projection, EP[:-1], axis=0, tiled=True)
     received = lax.all_to_all(spread, EP, split_axis=0, concat_axis=0, tiled=True)
     partial_out = feed_forward(
@@ -144,15 +145,21 @@
     head_count = query_width // head_dim
     projected = jnp.dot(lifted, projection, preferred_element_type=jnp.float32)
     query_raw = projected[:, :query_width]
-    keyval_raw = projected[:, query_width:]
+    keyval_raw = projected[:, query_width : query_width + 2 * head_dim]
+    all_segments = (
+        projection[:, query_width + 2 * head_dim :][:, :per_row]
+        .astype(jnp.int32)
+        .reshape(-1)[: device_count * token_count]
+    )
     global_index = first_index + jnp.arange(token_count, dtype=jnp.int32)
     key_index = (
         first_index - reach * token_count + jnp.arange((reach + 1) * token_count, dtype=jnp.int32)
     )
-    window_segment = jnp.concatenate(segment_pieces[::-1] + [segment_row], axis=0)
-    window_segment = jnp.where(key_index >= 0, window_segment, -1)
-    same_segment = window_segment[None, :] == segment_row[:, None]
-    start_index = jnp.min(jnp.where(same_segment, key_index[None, :], FAR_INDEX), axis=1)
+    section_index = jnp.arange(device_count * token_count, dtype=jnp.int32)
+    start_index = jnp.min(
+        jnp.where(all_segments[None, :] == segment_row[:, None], section_index[None, :], FAR_INDEX),
+        axis=1,
+    )
     position = global_index - start_index
     query = rotary(
         rms_rows(query_raw.reshape(token_count, head_count, head_dim)) * gain_query[0], position
@@ -173,7 +180,9 @@
         )
         * score_scale
     )
-    allowed = (same_segment & (key_index[None, :] <= global_index[:, None]))[:, None, :]
+    allowed = (
+        (key_index[None, :] >= start_index[:, None]) & (key_index[None, :] <= global_index[:, None])
+    )[:, None, :]
     probabilities = jnp.where(allowed, jnp.exp(scores), 0.0)
     total_mass = jnp.sum(probabilities, axis=-1)
     mixed = jnp.einsum(

time: 348 us -> 343 us (0.986)
  blocking collectives: 15.1 us -> 123 us
  waiting for transfers between devices: 215 us -> 121 us
  starting transfers between devices: 43.3 us -> 16.7 us
  other arithmetic: 17.7 us -> 23 us
  local copies, waits for them, and re-layouts: 15.1 us -> 20 us
    all_to_all x0 -> x1, blocking collectives: none -> 104 us  [on_device(): lax.all_to_all(spread, EP, split_axis=0, concat_axis=0, tiled=True)]
    all_to_all x1 -> x0, waiting for transfers between devices: 92.7 us -> none  [on_device(): lax.all_to_all(spread, EP, split_axis=0, concat_axis=0, tiled=True)]
    ppermute x8 -> x4, starting transfers between devices: 25.8 us -> 10 us  [passed_along_2(): lax.ppermute(value, axis, [(source, source + steps) for source in range(l...]
    all_to_all x1 -> x0, starting transfers between devices: 10.9 us -> none  [on_device(): lax.all_to_all(spread, EP, split_axis=0, concat_axis=0, tiled=True)]
    all_gather x1, blocking collectives: 15.1 us -> 19.1 us  [on_device(): projection = lax.all_gather(projection, EP[-1], axis=0, tiled=True)]
    unnamed x35 -> x41, local copies, waits for them, and re-layouts: 6.2 us -> 9.26 us
  transfers between devices with their start and end apart: 12 -> 7, of which waited for: 3 -> 2; matrix products, arithmetic and copies ran while one was open for 13% -> 10% of each run, Pallas kernels for 0% -> 0%
where the time goes in v5:
time: 343 us; the launch traced here: 341 us
  blocking collectives  123 us (36%)
  waiting for transfers between devices  121 us (35%)
  other arithmetic  23 us (7%)
  matrix products  22.7 us (7%)
  local copies, waits for them, and re-layouts  20 us (6%)
  starting transfers between devices  16.7 us (5%)
  between operations  14.4 us (4%)
    all_to_all x1, blocking collectives, on_device(): lax.all_to_all(spread, EP, split_axis=0, concat_axis=0, tiled=True)  104 us
    all_to_all x1, waiting for transfers between devices, on_device(): lax.all_to_all(partial_out.astype(jnp.bfloat16), EP, split_axis=0, concat...  93.4 us
    ppermute x1, waiting for transfers between devices, passed_along(): return lax.ppermute(block, axis, route)  27.7 us
    all_gather x1, blocking collectives, on_device(): projection = lax.all_gather(projection, EP[-1], axis=0, tiled=True)  19.1 us
    ppermute x4, starting transfers between devices, passed_along_2(): lax.ppermute(value, axis, [(source, source + steps) for source in range(l...  10 us
    dot_general x1, matrix products, feed_forward(): return jnp.dot(activated, down_part, preferred_element_type=jnp.float32)  9.89 us
    unnamed x41, local copies, waits for them, and re-layouts  9.26 us
  transfers between devices with their start and end apart: 7, of which 2 were waited for; matrix products, arithmetic and copies ran while one was open for 10% of the time, Pallas kernels for 0%

profile of v5, /device:TPU:32, one launch (start us, length us, event | category | flops | bytes accessed | tf_op | source)
XLA Modules:
  0.0 341.1 jit_solution(1977430579139286616)
XLA Ops:
  7.2 0.0 copy-start
  7.2 0.0 all-gather.2.cloned.1.call-start
  7.2 0.9 fusion.78
  8.1 0.8 fusion.74
  8.8 1.5 fusion.13
  10.4 0.1 fusion.70
  10.5 0.2 reduce_window_sum.11
  10.6 0.2 select_reduce_fusion.1
  10.8 0.7 convert_reduce_fusion.1
  11.5 0.1 convert_element_type.75
  11.7 0.9 fusion.65
  12.6 19.1 %all_gather.6 = bf16[256,1408]{1,0:T(8,128)(2,1)} all-gather(bf16[64,1408]{1,0:T(8,128)(2,1)S(1)} %fusion.65), channel_id=1, replica_groups=mesh['section'=4,'ep_y'=4,'ep_x'=4,'ep_z'=4] {'ep_z'}, dimensions={0}, use_global_device_ids=true | all-gather | bytes 901120 | tf_op jit(solution)/shard_map/all_gather | solution.py:125
  31.7 1.7 fusion
  33.4 2.6 broadcast_in_dim.107
  36.0 0.0 all-gather.2.cloned.1.call-update
  36.0 0.0 copy-start.16
  36.0 104.0 %all_to_all.10 = bf16[64,8,4096]{2,1,0:T(8,128)(2,1)S(1)} all-to-all(bf16[64,8,4096]{2,1,0:T(8,128)(2,1)} %bitcast.109), channel_id=1, replica_groups=mesh['section'=4,'ep_y'=4,'ep_x'=4,'ep_z'=4] {'ep_y','ep_x','ep_z'}, dimensions={0} | all-to-all | bytes 8388608 | tf_op jit(solution)/shard_map/all_to_all | solution.py:128
  140.0 2.0 copy-done.6
  142.1 3.2 fusion.3
  145.3 9.9 %convolution_convert_fusion = bf16[64,8,4096]{2,1,0:T(8,128)(2,1)} fusion(bf16[1,1,384,4096]{3,2,1,0:T(8,128)(2,1)S(1)} %copy-done, bf16[1,1,4096,384]{3,2,1,0:T(8,128)(2,1)} %param.15, bf16[64,8,4096]{2,1,0:T(8,128)(2,1)} %copy-done.6, f32[512,384]{1,0:T(8,128)} %fusion.3), kind=kOutput, calls=%fused_computation.2 | convolution fusion | flops 3224502272 | bytes 15466496 | tf_op jit(solution)/shard_map/dot_general | solution.py:65
  155.2 6.3 %all-to-all-start.1 = ((bf16[64,8,4096]{2,1,0:T(8,128)(2,1)}), bf16[64,8,4096]{2,1,0:T(8,128)(2,1)}, u32[]{:S(2)}, u32[]{:S(2)}) async-start(bf16[64,8,4096]{2,1,0:T(8,128)(2,1)} %convolution_convert_fusion), calls=%async_computation.1 | async-start | bytes 8388608 | tf_op jit(solution)/shard_map/all_to_all | solution.py:132
  161.5 0.5 iota_add_fusion.1
  162.1 93.4 %all-to-all-done.1 = bf16[64,8,4096]{2,1,0:T(8,128)(2,1)} async-done(((bf16[64,8,4096]{2,1,0:T(8,128)(2,1)}), bf16[64,8,4096]{2,1,0:T(8,128)(2,1)}, u32[]{:S(2)}, u32[]{:S(2)}) %all-to-all-start.1) | async-done | bytes 4194336 | tf_op jit(solution)/shard_map/all_to_all | solution.py:132
  255.5 4.5 %convert_reduce_fusion = f32[16,8,4096]{2,1,0:T(8,128)} fusion(bf16[64,8,4096]{2,1,0:T(8,128)(2,1)} %all-to-all-done.1), kind=kLoop, calls=%fused_computation.1 | loop fusion | flops 3670016 | bytes 6291456 | tf_op jit(solution)/shard_map/reduce_sum | solution.py:135
  259.9 5.1 %gather_fusion = f32[128,4096]{1,0:T(8,128)} fusion(f32[128,4096]{1,0:T(8,128)} %bitcast.108, s32[1024]{0:T(1024)S(1)} %pad_clamp_fusion), kind=kCustom, calls=%fused_computation | custom fusion | bytes 4194816 | tf_op jit(solution)/shard_map/jit(_take)/gather | solution.py:138
  265.0 2.6 fusion.15
  267.6 0.3 collective-permute-start
  267.9 1.6 fusion.16
  269.5 27.7 %collective-permute-done = bf16[128,4096]{1,0:T(8,128)(2,1)S(1)} collective-permute-done((bf16[128,4096]{1,0:T(8,128)(2,1)S(1)}, bf16[128,4096]{1,0:T(8,128)(2,1)S(1)}, u32[]{:S(2)}, u32[]{:S(2)}) %collective-permute-start) | collective-permute-done | bytes 1048608 | tf_op jit(solution)/shard_map/ppermute | solution.py:21
  297.2 1.0 copy-done.5
  298.2 0.3 fusion.17
  298.5 0.0 all-gather.2.cloned.1.call-done
  298.5 6.5 %fusion.47 = f32[128,1408]{1,0:T(8,128)S(1)} fusion(bf16[4096,1408]{1,0:T(8,128)(2,1)} %all-gather.2.cloned.1.call-done, bf16[128,4096]{1,0:T(8,128)(2,1)} %copy-done.5, f32[128]{0:T(128)S(1)} %add_rsqrt_fusion.2), kind=kOutput, calls=%fused_computation.41 | convolution fusion | flops 1477967872 | bytes 13304320 | tf_op jit(solution)/shard_map/dot_general | solution.py:146
  305.0 0.8 copy-done.7
  305.9 0.1 multiply_reduce_fusion.1
  306.0 0.0 copy-start.13
  306.0 0.0 copy-start.14
  306.0 2.9 slice_convert_fusion
  308.9 2.7 reshape.276
  311.6 0.9 fusion.71
  312.6 0.1 fusion.66
  312.6 0.9 select_reduce_fusion
  313.5 0.3 multiply_cosine_fusion
  313.8 1.0 fusion.68
  314.8 1.9 collective-permute-start.1
  316.8 3.4 %collective-permute-start.2 = (bf16[128,256]{1,0:T(8,128)(2,1)S(1)}, bf16[128,256]{1,0:T(8,128)(2,1)}, u32[]{:S(2)}, u32[]{:S(2)}) collective-permute-start(bf16[128,256]{1,0:T(8,128)(2,1)S(1)} %pad_maximum_fusion.2), channel_id=1, source_target_pairs={{0,3},{1,4},{2,5},{3,6},{4,7},{5,8},{6,9},{7,10},{8,11},{9,12},{10... | collective-permute-start | bytes 196616 | tf_op jit(solution)/shard_map/ppermute | solution.py:44
  320.2 1.9 collective-permute-start.3
  322.1 2.8 collective-permute-start.4
  324.9 1.1 slice_bitcast_fusion
  326.0 0.1 copy.32
  326.1 0.8 copy-done.3
  326.9 0.2 multiply_reduce_fusion
  327.1 0.1 copy.26
  327.3 0.0 copy-start.15
  327.3 1.3 multiply_multiply_fusion
  328.6 0.2 slice_negate_fusion
  328.8 0.3 fusion.60
  329.2 0.1 compare_and_fusion
  329.3 0.8 constant_dynamic-update-slice_fusion.4
  330.2 0.8 constant_dynamic-update-slice_fusion.3
  331.0 0.8 constant_dynamic-update-slice_fusion.2
  331.9 0.8 fusion.11
  332.8 0.6 fusion.39
  333.4 0.9 copy.29
  (45 shorter events, 0.2 us)
Async XLA Ops:
  7.2 138.1 %copy-start = (bf16[1,1,384,4096]{3,2,1,0:T(8,128)(2,1)S(1)}, bf16[1,1,384,4096]{3,2,1,0:T(8,128)(2,1)}, u32[]{:S(2)}) copy-start(bf16[1,1,384,4096]{3,2,1,0:T(8,128)(2,1)} %param.16) | copy-start | bytes 9437188
  7.2 291.3 %all-gather.2.cloned.1.call-start = ((), (), s32[]{:S(2)}) async-start(), calls=%async_computation.2 | async-start | bytes 12255232 | tf_op jit(solution)/shard_map/all_gather | solution.py:127
  36.0 106.0 %copy-start.16 = (bf16[1,1,4096,384]{3,2,1,0:T(8,128)(2,1)S(1)}, bf16[1,1,4096,384]{3,2,1,0:T(8,128)(2,1)}, u32[]{:S(2)}) copy-start(bf16[1,1,4096,384]{3,2,1,0:T(8,128)(2,1)} %param.14) | copy-start | bytes 9437188
  140.0 2.0 copy-start.6
  155.2 6.9 %copy-start.8 = (s32[1,128,8]{1,2,0:T(8,128)S(1)}, s32[1,128,8]{1,2,0:T(8,128)}, u32[]{:S(2)}) copy-start(s32[1,128,8]{1,2,0:T(8,128)} %param.12) | copy-start | bytes 12292
  155.2 6.9 %copy-start.9 = (f32[1,128,8]{1,2,0:T(8,128)S(1)}, f32[1,128,8]{1,2,0:T(8,128)}, u32[]{:S(2)}) copy-start(f32[1,128,8]{1,2,0:T(8,128)} %param.13) | copy-start | bytes 12292
  155.2 100.3 %all-to-all-start.1 = ((bf16[64,8,4096]{2,1,0:T(8,128)(2,1)}), bf16[64,8,4096]{2,1,0:T(8,128)(2,1)}, u32[]{:S(2)}, u32[]{:S(2)}) async-start(bf16[64,8,4096]{2,1,0:T(8,128)(2,1)} %convolution_convert_fusion), calls=%async_computation.1 | async-start | bytes 8388608 | tf_op jit(solution)/shard_map/all_to_all | solution.py:132
  265.0 2.9 copy-start.1
  265.0 2.9 copy-start.2
  267.6 29.6 %collective-permute-start = (bf16[128,4096]{1,0:T(8,128)(2,1)S(1)}, bf16[128,4096]{1,0:T(8,128)(2,1)S(1)}, u32[]{:S(2)}, u32[]{:S(2)}) collective-permute-start(bf16[128,4096]{1,0:T(8,128)(2,1)S(1)} %fusion.15), channel_id=1, source_target_pairs={{192,0},{0,64},{64,128},{128,192},{193,1},{1,65},{65,129},{129,193... | collective-permute-start | bytes 3145736 | tf_op jit(solution)/shard_map/ppermute | solution.py:21
  297.2 1.0 copy-start.5
  305.0 0.9 copy-start.7
  306.0 5.6 %copy-start.13 = (f32[1,128]{1,0:T(1,128)S(1)}, f32[1,128]{1,0:T(1,128)}, u32[]{:S(2)}) copy-start(f32[1,128]{1,0:T(1,128)} %param.20) | copy-start | bytes 1540
  306.0 6.7 %copy-start.14 = (s32[1,128]{1,0:T(1,128)S(1)}, s32[1,128]{1,0:T(1,128)}, u32[]{:S(2)}) copy-start(s32[1,128]{1,0:T(1,128)} %param.21) | copy-start | bytes 1540
  308.9 18.4 %copy-start.10 = (f32[1,128]{1,0:T(1,128)S(1)}, f32[1,128]{1,0:T(1,128)}, u32[]{:S(2)}) copy-start(f32[1,128]{1,0:T(1,128)} %param.19) | copy-start | bytes 1540
  313.5 12.6 %copy-start.11 = (s32[128]{0:T(128)}, s32[128]{0:T(128)S(1)}, u32[]{:S(2)}) copy-start(s32[128]{0:T(128)S(1)} %select_reduce_fusion) | copy-start | bytes 1540
  314.8 14.5 %collective-permute-start.1 = (bf16[128,256]{1,0:T(8,128)(2,1)S(1)}, bf16[128,256]{1,0:T(8,128)(2,1)}, u32[]{:S(2)}, u32[]{:S(2)}) collective-permute-start(bf16[128,256]{1,0:T(8,128)(2,1)S(1)} %pad_maximum_fusion.2), channel_id=1, source_target_pairs={{0,4},{1,5},{2,6},{3,7},{4,8},{5,9},{6,10},{7,11},{8,12},{9,13},{1... | collective-permute-start | bytes 196616 | tf_op jit(solution)/shard_map/ppermute | solution.py:44
  316.8 13.4 %collective-permute-start.2 = (bf16[128,256]{1,0:T(8,128)(2,1)S(1)}, bf16[128,256]{1,0:T(8,128)(2,1)}, u32[]{:S(2)}, u32[]{:S(2)}) collective-permute-start(bf16[128,256]{1,0:T(8,128)(2,1)S(1)} %pad_maximum_fusion.2), channel_id=1, source_target_pairs={{0,3},{1,4},{2,5},{3,6},{4,7},{5,8},{6,9},{7,10},{8,11},{9,12},{10... | collective-permute-start | bytes 196616 | tf_op jit(solution)/shard_map/ppermute | solution.py:44
  320.2 10.8 %collective-permute-start.3 = (bf16[128,256]{1,0:T(8,128)(2,1)S(1)}, bf16[128,256]{1,0:T(8,128)(2,1)}, u32[]{:S(2)}, u32[]{:S(2)}) collective-permute-start(bf16[128,256]{1,0:T(8,128)(2,1)S(1)} %pad_maximum_fusion.2), channel_id=1, source_target_pairs={{0,2},{1,3},{2,4},{3,5},{4,6},{5,7},{6,8},{7,9},{8,10},{9,11},{10,... | collective-permute-start | bytes 196616 | tf_op jit(solution)/shard_map/ppermute | solution.py:44
  322.1 9.8 %collective-permute-start.4 = (bf16[128,256]{1,0:T(8,128)(2,1)S(1)}, bf16[128,256]{1,0:T(8,128)(2,1)S(1)}, u32[]{:S(2)}, u32[]{:S(2)}) collective-permute-start(bf16[128,256]{1,0:T(8,128)(2,1)S(1)} %pad_maximum_fusion.2), channel_id=1, source_target_pairs={{0,1},{1,2},{2,3},{3,4},{4,5},{5,6},{6,7},{7,8},{8,9},{9,10},{10,1... | collective-permute-start | bytes 196616 | tf_op jit(solution)/shard_map/ppermute | solution.py:44
  326.1 0.8 copy-start.3
  327.3 1.5 copy-start.4
  327.3 1.9 copy-start.12
  327.3 1.9 copy-start.15
Sparse Core Ops, SparseCore 0:
  36.1 128.4 all-gather.1

commit v6 on v5

--- a/solution.py
+++ b/solution.py
@@ -112,19 +112,20 @@
         packed.reshape(expert_count, 1, capacity, model_width),
         (expert_count, OWNERS, capacity, model_width),
     ).reshape(device_count, capacity, model_width)
-    segment_row = segment_ids[0]
+    next_query, next_keyval, segment_row, next_gain_query, next_gain_key = passed_along(
+        (w_query[0], w_keyval[0], segment_ids[0], gain_query[0], gain_key[0]), "section", -1
+    )
     first_index = lax.axis_index(EP) * token_count
     reach = (SEG_MOST - 1) // token_count + 1
-    shard_rows = w_query.shape[1]
+    shard_rows = next_query.shape[0]
     per_row = -(-token_count // shard_rows)
     carried = jnp.pad(segment_row, (0, shard_rows * per_row - token_count)).reshape(
         shard_rows, per_row
     )
     carried = jnp.pad(carried.astype(jnp.bfloat16), ((0, 0), (0, 128 - per_row)))
-    projection = jnp.concatenate([w_query[0], w_keyval[0], carried], axis=-1)
-    projection = lax.all_gather(projection, EP[-1], axis=0, tiled=True)
-    spread, projection = lax.optimization_barrier((spread, projection))
-    projection = lax.all_gather(projection, EP[:-1], axis=0, tiled=True)
+    projection = jnp.concatenate([next_query, next_keyval, carried], axis=-1)
+    projection = lax.all_gather(projection, EP[1:], axis=0, tiled=True)
+    projection = lax.all_gather(projection, EP[:1], axis=0, tiled=True)
     received = lax.all_to_all(spread, EP, split_axis=0, concat_axis=0, tiled=True)
     partial_out = feed_forward(
         received.reshape(-1, model_width), gate_part, up_part, down_part
@@ -138,8 +139,7 @@
     fetched_rows = jnp.take(merged, jnp.maximum(slot_index, 0), axis=0)
     expert_out = jnp.where(has_route[:, None], fetched_rows, 0.0)
     layer_out = (wide_tokens + weight_kept[:, None] * expert_out).astype(jnp.bfloat16)
-    arrived = passed_along(layer_out, "section", 1)
-    lifted = rms_rows(arrived.astype(jnp.float32)).astype(jnp.bfloat16)
+    lifted = rms_rows(layer_out.astype(jnp.float32)).astype(jnp.bfloat16)
     head_dim = gain_query.shape[-1]
     query_width = w_query.shape[-1]
     head_count = query_width // head_dim
@@ -162,9 +162,9 @@
     )
     position = global_index - start_index
     query = rotary(
-        rms_rows(query_raw.reshape(token_count, head_count, head_dim)) * gain_query[0], position
+        rms_rows(query_raw.reshape(token_count, head_count, head_dim)) * next_gain_query, position
     ).astype(jnp.bfloat16)
-    key_part = rotary(rms_rows(keyval_raw[:, None, :head_dim]) * gain_key[0], position)[
+    key_part = rotary(rms_rows(keyval_raw[:, None, :head_dim]) * next_gain_key, position)[
         :, 0
     ].astype(jnp.bfloat16)
     value_part = keyval_raw[:, head_dim:].astype(jnp.bfloat16)
@@ -192,6 +192,7 @@
         preferred_element_type=jnp.float32,
     )
     attended = (mixed / total_mass[..., None]).astype(jnp.bfloat16).reshape(token_count, query_width)
+    attended = passed_along(attended, "section", 1)
     return (layer_out[None], attended[None])
 
 

time: 343 us -> 387 us (1.13)
  waiting for transfers between devices: 121 us -> 258 us
  blocking collectives: 123 us -> 0 us
  starting transfers between devices: 16.7 us -> 44.2 us
  matrix products: 22.7 us -> 26.6 us
    all_gather x1 -> x2, waiting for transfers between devices: 0.02 us -> 134 us  [the longest x1 128 us: on_device(): projection = lax.all_gather(projection, EP[1:], axis=0, tiled=True)]
    all_to_all x1 -> x0, blocking collectives: 104 us -> none  [on_device(): lax.all_to_all(spread, EP, split_axis=0, concat_axis=0, tiled=True)]
    all_to_all x0 -> x1, waiting for transfers between devices: none -> 22.2 us  [on_device(): lax.all_to_all(spread, EP, split_axis=0, concat_axis=0, tiled=True)]
    all_gather x1 -> x0, blocking collectives: 19.1 us -> none  [on_device(): projection = lax.all_gather(projection, EP[-1], axis=0, tiled=True)]
    ppermute x1 -> x6, waiting for transfers between devices: 27.7 us -> 11.5 us  [passed_along(): return lax.ppermute(block, axis, route)]
    ppermute x1 -> x6, starting transfers between devices: 0.26 us -> 12.2 us  [passed_along(): return lax.ppermute(block, axis, route)]
    all_to_all x0 -> x1, starting transfers between devices: none -> 11.3 us  [on_device(): lax.all_to_all(spread, EP, split_axis=0, concat_axis=0, tiled=True)]
    ppermute x4, starting transfers between devices: 10 us -> 15.1 us  [passed_along_2(): lax.ppermute(value, axis, [(source, source + steps) for source in range(l...]
  transfers between devices with their start and end apart: 7 -> 14, of which waited for: 2 -> 6; matrix products, arithmetic and copies ran while one was open for 10% -> 16% of each run, Pallas kernels for 0% -> 0%
where the time goes in v6:
time: 387 us; the launch traced here: 386 us
  waiting for transfers between devices  258 us (67%)
  starting transfers between devices  44.2 us (11%)
  matrix products  26.6 us (7%)
  other arithmetic  24.9 us (6%)
  local copies, waits for them, and re-layouts  17 us (4%)
  between operations  14.4 us (4%)
    all_gather x1, waiting for transfers between devices, on_device(): projection = lax.all_gather(projection, EP[1:], axis=0, tiled=True)  128 us
    all_to_all x1, waiting for transfers between devices, on_device(): lax.all_to_all(partial_out.astype(jnp.bfloat16), EP, split_axis=0, concat...  90.7 us
    all_to_all x1, waiting for transfers between devices, on_device(): lax.all_to_all(spread, EP, split_axis=0, concat_axis=0, tiled=True)  22.2 us
    ppermute x4, starting transfers between devices, passed_along_2(): lax.ppermute(value, axis, [(source, source + steps) for source in range(l...  15.1 us
    ppermute x6, starting transfers between devices, passed_along(): return lax.ppermute(block, axis, route)  12.2 us
    ppermute x6, waiting for transfers between devices, passed_along(): return lax.ppermute(block, axis, route)  11.5 us
    all_to_all x1, starting transfers between devices, on_device(): lax.all_to_all(spread, EP, split_axis=0, concat_axis=0, tiled=True)  11.3 us
    dot_general x1, matrix products, feed_forward(): return jnp.dot(activated, down_part, preferred_element_type=jnp.float32)  9.78 us
  transfers between devices with their start and end apart: 14, of which 6 were waited for; matrix products, arithmetic and copies ran while one was open for 16% of the time, Pallas kernels for 0%

profile of v6, /device:TPU:32, one launch (start us, length us, event | category | flops | bytes accessed | tf_op | source)
XLA Modules:
  0.0 385.6 jit_solution(1018160500610318779)
XLA Ops:
  7.2 0.0 all-gather.3.cloned.1.call-start
  7.2 5.8 %collective-permute-start = (bf16[64,1024]{1,0:T(8,128)(2,1)}, bf16[64,1024]{1,0:T(8,128)(2,1)S(1)}, u32[]{:S(2)}, u32[]{:S(2)}) collective-permute-start(bf16[64,1024]{1,0:T(8,128)(2,1)} %bitcast.115), channel_id=1, source_target_pairs={{64,0},{128,64},{192,128},{0,192},{65,1},{129,65},{193,129},{1,193... | collective-permute-start | bytes 393224 | tf_op jit(solution)/shard_map/ppermute | solution.py:21
  13.0 0.7 collective-permute-start.1
  13.7 0.1 collective-permute-start.2
  13.8 2.5 collective-permute-done.2
  16.3 0.1 convert_element_type.78
  16.5 0.7 fusion.65
  17.2 0.0 all-gather.3.cloned.1.call-update
  17.2 0.7 fusion.78
  17.9 0.7 fusion.74
  18.6 0.1 fusion.70
  18.7 0.2 reduce_window_sum.11
  18.9 0.2 select_reduce_fusion.1
  19.0 1.5 fusion.13
  20.6 1.7 fusion
  22.3 2.5 broadcast_in_dim.113
  24.8 11.3 %all-to-all-start = ((bf16[64,8,4096]{2,1,0:T(8,128)(2,1)}), bf16[64,8,4096]{2,1,0:T(8,128)(2,1)}, u32[]{:S(2)}, u32[]{:S(2)}) async-start(bf16[64,8,4096]{2,1,0:T(8,128)(2,1)} %bitcast.111), calls=%async_computation | async-start | bytes 8388608 | tf_op jit(solution)/shard_map/all_to_all | solution.py:129
  36.1 0.0 all-gather.5.cloned.1.call-start
  36.1 127.6 %all-gather.3.cloned.1.call-done = bf16[1024,1408]{1,0:T(8,128)(2,1)} async-done(((bf16[64,1408]{1,0:T(8,128)(2,1)}), bf16[1024,1408]{1,0:T(8,128)(2,1)}) %all-gather.3.cloned.1.call-update) | async-done | bytes 2883600 | tf_op jit(solution)/shard_map/all_gather | solution.py:127
  163.8 0.0 all-gather.5.cloned.1.call-update
  163.8 22.2 %all-to-all-done = bf16[64,8,4096]{2,1,0:T(8,128)(2,1)} async-done(((bf16[64,8,4096]{2,1,0:T(8,128)(2,1)}), bf16[64,8,4096]{2,1,0:T(8,128)(2,1)}, u32[]{:S(2)}, u32[]{:S(2)}) %all-to-all-start) | async-done | bytes 4194336 | tf_op jit(solution)/shard_map/all_to_all | solution.py:129
  186.0 6.5 %fusion.3 = f32[512,384]{1,0:T(8,128)} fusion(bf16[64,8,4096]{2,1,0:T(8,128)(2,1)} %all-to-all-done, bf16[1,1,4096,384]{3,2,1,0:T(8,128)(2,1)} %param.14), kind=kOutput, calls=%fused_computation.7 | convolution fusion | flops 1610612736 | bytes 8126464 | tf_op jit(solution)/shard_map/dot_general | solution.py:62
  192.5 9.8 %convolution_convert_fusion = bf16[64,8,4096]{2,1,0:T(8,128)(2,1)} fusion(bf16[1,1,384,4096]{3,2,1,0:T(8,128)(2,1)S(1)} %copy-done, bf16[1,1,4096,384]{3,2,1,0:T(8,128)(2,1)} %param.15, bf16[64,8,4096]{2,1,0:T(8,128)(2,1)} %all-to-all-done, f32[512,384]{1,0:T(8,128)} %fusion.3), kind=kOutput, calls=%fused_computation.2 | convolution fusion | flops 3224502272 | bytes 15466496 | tf_op jit(solution)/shard_map/dot_general | solution.py:65
  202.3 5.6 %all-to-all-start.1 = ((bf16[64,8,4096]{2,1,0:T(8,128)(2,1)}), bf16[64,8,4096]{2,1,0:T(8,128)(2,1)}, u32[]{:S(2)}, u32[]{:S(2)}) async-start(bf16[64,8,4096]{2,1,0:T(8,128)(2,1)} %convolution_convert_fusion), calls=%async_computation.1 | async-start | bytes 8388608 | tf_op jit(solution)/shard_map/all_to_all | solution.py:133
  207.9 4.6 %collective-permute-start.4 = (f32[128]{0:T(128)S(1)}, f32[128]{0:T(128)S(1)}, u32[]{:S(2)}, u32[]{:S(2)}) collective-permute-start(f32[128]{0:T(128)S(1)} %bitcast.118), channel_id=1, source_target_pairs={{64,0},{128,64},{192,128},{0,192},{65,1},{129,65},{193,129},{1,193... | collective-permute-start | bytes 1544 | tf_op jit(solution)/shard_map/ppermute | solution.py:21
  212.4 0.9 collective-permute-start.3
  213.4 0.5 iota_add_fusion.1
  214.0 90.7 %all-to-all-done.1 = bf16[64,8,4096]{2,1,0:T(8,128)(2,1)} async-done(((bf16[64,8,4096]{2,1,0:T(8,128)(2,1)}), bf16[64,8,4096]{2,1,0:T(8,128)(2,1)}, u32[]{:S(2)}, u32[]{:S(2)}) %all-to-all-start.1) | async-done | bytes 4194336 | tf_op jit(solution)/shard_map/all_to_all | solution.py:133
  304.6 4.4 %convert_reduce_fusion = f32[16,8,4096]{2,1,0:T(8,128)} fusion(bf16[64,8,4096]{2,1,0:T(8,128)(2,1)} %all-to-all-done.1), kind=kLoop, calls=%fused_computation.1 | loop fusion | flops 3670016 | bytes 6291456 | tf_op jit(solution)/shard_map/reduce_sum | solution.py:136
  309.1 5.1 %gather_fusion = f32[128,4096]{1,0:T(8,128)} fusion(f32[128,4096]{1,0:T(8,128)} %bitcast.110, s32[1024]{0:T(1024)S(1)} %pad_clamp_fusion), kind=kCustom, calls=%fused_computation | custom fusion | bytes 4194816 | tf_op jit(solution)/shard_map/jit(_take)/gather | solution.py:139
  314.2 3.4 fusion.17
  317.6 6.4 %all-gather.5.cloned.1.call-done = bf16[4096,1408]{1,0:T(8,128)(2,1)} async-done(((bf16[1024,1408]{1,0:T(8,128)(2,1)}), bf16[4096,1408]{1,0:T(8,128)(2,1)}) %all-gather.5.cloned.1.call-update) | async-done | bytes 11534352 | tf_op jit(solution)/shard_map/all_gather | solution.py:128
  324.0 6.5 %fusion.47 = f32[128,1408]{1,0:T(8,128)S(1)} fusion(bf16[4096,1408]{1,0:T(8,128)(2,1)} %all-gather.5.cloned.1.call-done, bf16[128,4096]{1,0:T(8,128)(2,1)} %get-tuple-element.3, f32[128]{0:T(128)S(1)} %add_rsqrt_fusion.2), kind=kOutput, calls=%fused_computation.41 | convolution fusion | flops 1477967872 | bytes 13304320 | tf_op jit(solution)/shard_map/dot_general | solution.py:146
  330.4 0.1 multiply_reduce_fusion.1
  330.5 2.9 slice_convert_fusion
  333.4 2.7 reshape.279
  336.2 0.9 fusion.71
  337.1 0.1 fusion.66
  337.2 0.9 select_reduce_fusion
  338.1 0.3 multiply_cosine_fusion
  338.4 1.0 fusion.68
  339.4 3.2 collective-permute-start.5
  342.6 3.3 collective-permute-start.6
  345.9 4.5 %collective-permute-start.7 = (bf16[128,256]{1,0:T(8,128)(2,1)S(1)}, bf16[128,256]{1,0:T(8,128)(2,1)}, u32[]{:S(2)}, u32[]{:S(2)}) collective-permute-start(bf16[128,256]{1,0:T(8,128)(2,1)S(1)} %pad_maximum_fusion.2), channel_id=1, source_target_pairs={{0,2},{1,3},{2,4},{3,5},{4,6},{5,7},{6,8},{7,9},{8,10},{9,11},{10,... | collective-permute-start | bytes 196616 | tf_op jit(solution)/shard_map/ppermute | solution.py:44
  350.3 4.2 %collective-permute-start.8 = (bf16[128,256]{1,0:T(8,128)(2,1)S(1)}, bf16[128,256]{1,0:T(8,128)(2,1)S(1)}, u32[]{:S(2)}, u32[]{:S(2)}) collective-permute-start(bf16[128,256]{1,0:T(8,128)(2,1)S(1)} %pad_maximum_fusion.2), channel_id=1, source_target_pairs={{0,1},{1,2},{2,3},{3,4},{4,5},{5,6},{6,7},{7,8},{8,9},{9,10},{10,1... | collective-permute-start | bytes 196616 | tf_op jit(solution)/shard_map/ppermute | solution.py:44
  354.5 1.1 slice_bitcast_fusion
  355.6 0.1 copy.32
  355.7 0.8 copy-done.1
  356.5 0.2 multiply_reduce_fusion
  356.8 0.1 copy.26
  357.0 1.3 multiply_multiply_fusion
  358.3 0.2 slice_negate_fusion
  358.5 1.0 fusion.60
  359.5 0.1 compare_and_fusion
  359.6 0.8 constant_dynamic-update-slice_fusion.4
  360.5 0.8 constant_dynamic-update-slice_fusion.3
  361.3 0.8 constant_dynamic-update-slice_fusion.2
  362.2 0.8 fusion.11
  363.1 1.3 fusion.39
  364.4 1.1 copy.29
  365.5 0.1 collective-permute-start.9
  365.6 3.4 fusion.16
  369.0 9.0 %collective-permute-done.9 = bf16[128,1024]{1,0:T(8,128)(2,1)S(1)} collective-permute-done((bf16[128,1024]{1,0:T(8,128)(2,1)S(1)}, bf16[128,1024]{1,0:T(8,128)(2,1)S(1)}, u32[]{:S(2)}, u32[]{:S(2)}) %collective-permute-start.9) | collective-permute-done | bytes 262176 | tf_op jit(solution)/shard_map/ppermute | solution.py:21
  378.1 0.7 copy.42
  (52 shorter events, 0.3 us)
Async XLA Ops:
  7.2 185.3 %copy-start = (bf16[1,1,384,4096]{3,2,1,0:T(8,128)(2,1)S(1)}, bf16[1,1,384,4096]{3,2,1,0:T(8,128)(2,1)}, u32[]{:S(2)}) copy-start(bf16[1,1,384,4096]{3,2,1,0:T(8,128)(2,1)} %param.16) | copy-start | bytes 9437188
  7.2 156.6 %all-gather.3.cloned.1.call-start = ((), (), s32[]{:S(2)}) async-start(), calls=%async_computation.2 | async-start | bytes 3063808 | tf_op jit(solution)/shard_map/all_gather | solution.py:127
  7.2 9.2 %collective-permute-start = (bf16[64,1024]{1,0:T(8,128)(2,1)}, bf16[64,1024]{1,0:T(8,128)(2,1)S(1)}, u32[]{:S(2)}, u32[]{:S(2)}) collective-permute-start(bf16[64,1024]{1,0:T(8,128)(2,1)} %bitcast.115), channel_id=1, source_target_pairs={{64,0},{128,64},{192,128},{0,192},{65,1},{129,65},{193,129},{1,193... | collective-permute-start | bytes 393224 | tf_op jit(solution)/shard_map/ppermute | solution.py:21
  13.0 3.4 collective-permute-start.1
  13.7 2.6 collective-permute-start.2
  20.6 293.6 %copy-start.5 = (pred[128]{0:T(512)(128)(4,1)}, pred[128]{0:T(512)(128)(4,1)S(1)}, u32[]{:S(2)}) copy-start(pred[128]{0:T(512)(128)(4,1)S(1)} %get-tuple-element.4) | copy-start | bytes 388
  24.8 161.2 %all-to-all-start = ((bf16[64,8,4096]{2,1,0:T(8,128)(2,1)}), bf16[64,8,4096]{2,1,0:T(8,128)(2,1)}, u32[]{:S(2)}, u32[]{:S(2)}) async-start(bf16[64,8,4096]{2,1,0:T(8,128)(2,1)} %bitcast.111), calls=%async_computation | async-start | bytes 8388608 | tf_op jit(solution)/shard_map/all_to_all | solution.py:129
  36.1 287.9 %all-gather.5.cloned.1.call-start = ((), (), s32[]{:S(2)}) async-start(), calls=%async_computation.3 | async-start | bytes 14417920 | tf_op jit(solution)/shard_map/all_gather | solution.py:128
  202.3 5.6 %copy-start.13 = (f32[1,128]{1,0:T(1,128)S(1)}, f32[1,128]{1,0:T(1,128)}, u32[]{:S(2)}) copy-start(f32[1,128]{1,0:T(1,128)} %param.20) | copy-start | bytes 1540
  202.3 11.6 %copy-start.4 = (s32[1,128,8]{1,2,0:T(8,128)S(1)}, s32[1,128,8]{1,2,0:T(8,128)}, u32[]{:S(2)}) copy-start(s32[1,128,8]{1,2,0:T(8,128)} %param.12) | copy-start | bytes 12292
  202.3 11.7 %copy-start.9 = (f32[1,128,8]{1,2,0:T(8,128)S(1)}, f32[1,128,8]{1,2,0:T(8,128)}, u32[]{:S(2)}) copy-start(f32[1,128,8]{1,2,0:T(8,128)} %param.13) | copy-start | bytes 12292
  202.3 102.3 %all-to-all-start.1 = ((bf16[64,8,4096]{2,1,0:T(8,128)(2,1)}), bf16[64,8,4096]{2,1,0:T(8,128)(2,1)}, u32[]{:S(2)}, u32[]{:S(2)}) async-start(bf16[64,8,4096]{2,1,0:T(8,128)(2,1)} %convolution_convert_fusion), calls=%async_computation.1 | async-start | bytes 8388608 | tf_op jit(solution)/shard_map/all_to_all | solution.py:133
  207.9 128.3 %collective-permute-start.4 = (f32[128]{0:T(128)S(1)}, f32[128]{0:T(128)S(1)}, u32[]{:S(2)}, u32[]{:S(2)}) collective-permute-start(f32[128]{0:T(128)S(1)} %bitcast.118), channel_id=1, source_target_pairs={{64,0},{128,64},{192,128},{0,192},{65,1},{129,65},{193,129},{1,193... | collective-permute-start | bytes 1544 | tf_op jit(solution)/shard_map/ppermute | solution.py:21
  212.4 144.5 %collective-permute-start.3 = (f32[128]{0:T(128)}, f32[128]{0:T(128)}, u32[]{:S(2)}, u32[]{:S(2)}) collective-permute-start(f32[128]{0:T(128)} %bitcast.17), channel_id=1, source_target_pairs={{64,0},{128,64},{192,128},{0,192},{65,1},{129,65},{193,129},{1,193... | collective-permute-start | bytes 1544 | tf_op jit(solution)/shard_map/ppermute | solution.py:21
  214.0 100.2 %copy-start.7 = (f32[128]{0:T(128)}, f32[128]{0:T(128)S(1)}, u32[]{:S(2)}) copy-start(f32[128]{0:T(128)S(1)} %fusion.73) | copy-start | bytes 1540
  330.4 3.0 copy-start.3
  338.1 17.7 %copy-start.10 = (s32[128]{0:T(128)}, s32[128]{0:T(128)S(1)}, u32[]{:S(2)}) copy-start(s32[128]{0:T(128)S(1)} %select_reduce_fusion) | copy-start | bytes 1540
  339.4 20.2 %collective-permute-start.5 = (bf16[128,256]{1,0:T(8,128)(2,1)S(1)}, bf16[128,256]{1,0:T(8,128)(2,1)}, u32[]{:S(2)}, u32[]{:S(2)}) collective-permute-start(bf16[128,256]{1,0:T(8,128)(2,1)S(1)} %pad_maximum_fusion.2), channel_id=1, source_target_pairs={{0,4},{1,5},{2,6},{3,7},{4,8},{5,9},{6,10},{7,11},{8,12},{9,13},{1... | collective-permute-start | bytes 196616 | tf_op jit(solution)/shard_map/ppermute | solution.py:44
  342.6 17.9 %collective-permute-start.6 = (bf16[128,256]{1,0:T(8,128)(2,1)S(1)}, bf16[128,256]{1,0:T(8,128)(2,1)}, u32[]{:S(2)}, u32[]{:S(2)}) collective-permute-start(bf16[128,256]{1,0:T(8,128)(2,1)S(1)} %pad_maximum_fusion.2), channel_id=1, source_target_pairs={{0,3},{1,4},{2,5},{3,6},{4,7},{5,8},{6,9},{7,10},{8,11},{9,12},{10... | collective-permute-start | bytes 196616 | tf_op jit(solution)/shard_map/ppermute | solution.py:44
  345.9 15.5 %collective-permute-start.7 = (bf16[128,256]{1,0:T(8,128)(2,1)S(1)}, bf16[128,256]{1,0:T(8,128)(2,1)}, u32[]{:S(2)}, u32[]{:S(2)}) collective-permute-start(bf16[128,256]{1,0:T(8,128)(2,1)S(1)} %pad_maximum_fusion.2), channel_id=1, source_target_pairs={{0,2},{1,3},{2,4},{3,5},{4,6},{5,7},{6,8},{7,9},{8,10},{9,11},{10,... | collective-permute-start | bytes 196616 | tf_op jit(solution)/shard_map/ppermute | solution.py:44
  350.3 11.8 %collective-permute-start.8 = (bf16[128,256]{1,0:T(8,128)(2,1)S(1)}, bf16[128,256]{1,0:T(8,128)(2,1)S(1)}, u32[]{:S(2)}, u32[]{:S(2)}) collective-permute-start(bf16[128,256]{1,0:T(8,128)(2,1)S(1)} %pad_maximum_fusion.2), channel_id=1, source_target_pairs={{0,1},{1,2},{2,3},{3,4},{4,5},{5,6},{6,7},{7,8},{8,9},{9,10},{10,1... | collective-permute-start | bytes 196616 | tf_op jit(solution)/shard_map/ppermute | solution.py:44
  355.7 0.8 copy-start.1
  356.9 1.6 copy-start.2
  356.9 2.5 copy-start.11
  356.9 2.5 copy-start.12
  363.0 2.5 copy-start.6
  363.1 2.5 copy-start.8
  365.5 12.6 %collective-permute-start.9 = (bf16[128,1024]{1,0:T(8,128)(2,1)S(1)}, bf16[128,1024]{1,0:T(8,128)(2,1)S(1)}, u32[]{:S(2)}, u32[]{:S(2)}) collective-permute-start(bf16[128,1024]{1,0:T(8,128)(2,1)S(1)} %copy.29), channel_id=1, source_target_pairs={{192,0},{0,64},{64,128},{128,192},{193,1},{1,65},{65,129},{129,193... | collective-permute-start | bytes 786440 | tf_op jit(solution)/shard_map/ppermute | solution.py:21
Sparse Core Ops, SparseCore 0:
  17.3 146.4 all-gather.2
  165.6 158.3 all-gather.4

commit v7 on v6

--- a/solution.py
+++ b/solution.py
@@ -124,8 +124,9 @@
     )
     carried = jnp.pad(carried.astype(jnp.bfloat16), ((0, 0), (0, 128 - per_row)))
     projection = jnp.concatenate([next_query, next_keyval, carried], axis=-1)
-    projection = lax.all_gather(projection, EP[1:], axis=0, tiled=True)
-    projection = lax.all_gather(projection, EP[:1], axis=0, tiled=True)
+    projection = lax.all_gather(projection, EP[-1], axis=0, tiled=True)
+    spread, projection = lax.optimization_barrier((spread, projection))
+    projection = lax.all_gather(projection, EP[:-1], axis=0, tiled=True)
     received = lax.all_to_all(spread, EP, split_axis=0, concat_axis=0, tiled=True)
     partial_out = feed_forward(
         received.reshape(-1, model_width), gate_part, up_part, down_part

time: 387 us -> 337 us (0.87)
  waiting for transfers between devices: 258 us -> 99.4 us
  blocking collectives: 0 us -> 125 us
  starting transfers between devices: 44.2 us -> 24.9 us
    all_gather x2 -> x1, waiting for transfers between devices: 134 us -> 0.01 us  [on_device(): projection = lax.all_gather(projection, EP[:-1], axis=0, tiled=True)]
    all_to_all x0 -> x1, blocking collectives: none -> 107 us  [on_device(): lax.all_to_all(spread, EP, split_axis=0, concat_axis=0, tiled=True)]
    all_to_all x1 -> x0, waiting for transfers between devices: 22.2 us -> none  [on_device(): lax.all_to_all(spread, EP, split_axis=0, concat_axis=0, tiled=True)]
    all_gather x0 -> x1, blocking collectives: none -> 17.7 us  [on_device(): projection = lax.all_gather(projection, EP[-1], axis=0, tiled=True)]
    all_to_all x1 -> x0, starting transfers between devices: 11.3 us -> none  [on_device(): lax.all_to_all(spread, EP, split_axis=0, concat_axis=0, tiled=True)]
    ppermute x6, waiting for transfers between devices: 11.5 us -> 6.35 us  [passed_along(): return lax.ppermute(block, axis, route)]
    ppermute x6, starting transfers between devices: 12.2 us -> 7.72 us  [passed_along(): return lax.ppermute(block, axis, route)]
    ppermute x4, starting transfers between devices: 15.1 us -> 10.8 us  [passed_along_2(): lax.ppermute(value, axis, [(source, source + steps) for source in range(l...]
  transfers between devices with their start and end apart: 14 -> 12, of which waited for: 6 -> 2; matrix products, arithmetic and copies ran while one was open for 16% -> 18% of each run, Pallas kernels for 0% -> 0%
where the time goes in v7:
time: 337 us; the launch traced here: 332 us
  blocking collectives  125 us (37%)
  waiting for transfers between devices  99.4 us (29%)
  starting transfers between devices  24.9 us (7%)
  matrix products  24.3 us (7%)
  other arithmetic  24.2 us (7%)
  local copies, waits for them, and re-layouts  20.4 us (6%)
  between operations  14.4 us (4%)
    all_to_all x1, blocking collectives, on_device(): lax.all_to_all(spread, EP, split_axis=0, concat_axis=0, tiled=True)  107 us
    all_to_all x1, waiting for transfers between devices, on_device(): lax.all_to_all(partial_out.astype(jnp.bfloat16), EP, split_axis=0, concat...  93 us
    all_gather x1, blocking collectives, on_device(): projection = lax.all_gather(projection, EP[-1], axis=0, tiled=True)  17.7 us
    ppermute x4, starting transfers between devices, passed_along_2(): lax.ppermute(value, axis, [(source, source + steps) for source in range(l...  10.8 us
    dot_general x1, matrix products, feed_forward(): return jnp.dot(activated, down_part, preferred_element_type=jnp.float32)  9.79 us
    ppermute x6, starting transfers between devices, passed_along(): return lax.ppermute(block, axis, route)  7.72 us
    unnamed x39, local copies, waits for them, and re-layouts  7.32 us
  transfers between devices with their start and end apart: 12, of which 2 were waited for; matrix products, arithmetic and copies ran while one was open for 18% of the time, Pallas kernels for 0%

profile of v7, /device:TPU:32, one launch (start us, length us, event | category | flops | bytes accessed | tf_op | source)
XLA Modules:
  0.0 332.5 jit_solution(2821371864683105371)
XLA Ops:
  7.2 0.0 copy-start
  7.2 0.0 all-gather.2.cloned.1.call-start
  7.2 5.8 %collective-permute-start.2 = (s32[128]{0:T(128)}, s32[128]{0:T(128)S(1)}, u32[]{:S(2)}, u32[]{:S(2)}) collective-permute-start(s32[128]{0:T(128)} %bitcast.117), channel_id=1, source_target_pairs={{64,0},{128,64},{192,128},{0,192},{65,1},{129,65},{193,129},{1,193... | collective-permute-start | bytes 1544 | tf_op jit(solution)/shard_map/ppermute | solution.py:21
  13.0 0.7 collective-permute-start.1
  13.7 0.1 collective-permute-start
  13.8 0.7 fusion.78
  14.5 0.7 fusion.74
  15.2 1.5 fusion.13
  16.7 0.1 fusion.70
  16.8 0.2 reduce_window_sum.11
  17.0 0.2 select_reduce_fusion.1
  17.2 2.7 fusion
  19.9 0.1 convert_element_type.75
  20.1 17.7 %all_gather.6 = bf16[256,1408]{1,0:T(8,128)(2,1)} all-gather(bf16[64,1408]{1,0:T(8,128)(2,1)S(1)} %fusion.65), channel_id=1, replica_groups=mesh['section'=4,'ep_y'=4,'ep_x'=4,'ep_z'=4] {'ep_z'}, dimensions={0}, use_global_device_ids=true | all-gather | bytes 901120 | tf_op jit(solution)/shard_map/all_gather | solution.py:127
  37.9 3.8 %broadcast_in_dim.113 = bf16[16,4,8,4096]{3,2,1,0:T(8,128)(2,1)} broadcast(bf16[16,8,4096]{2,1,0:T(8,128)(2,1)} %fusion), dimensions={0,2,3} | broadcast | bytes 5242880 | tf_op jit(solution)/shard_map/broadcast_in_dim | solution.py:111
  41.6 0.0 all-gather.2.cloned.1.call-update
  41.7 0.0 copy-start.14
  41.7 107.1 %all_to_all.10 = bf16[64,8,4096]{2,1,0:T(8,128)(2,1)S(1)} all-to-all(bf16[64,8,4096]{2,1,0:T(8,128)(2,1)} %bitcast.111), channel_id=1, replica_groups=mesh['section'=4,'ep_y'=4,'ep_x'=4,'ep_z'=4] {'ep_y','ep_x','ep_z'}, dimensions={0} | all-to-all | bytes 8388608 | tf_op jit(solution)/shard_map/all_to_all | solution.py:130
  148.8 2.0 copy-done.3
  150.8 3.2 fusion.3
  154.0 9.8 %convolution_convert_fusion = bf16[64,8,4096]{2,1,0:T(8,128)(2,1)} fusion(bf16[1,1,384,4096]{3,2,1,0:T(8,128)(2,1)S(1)} %copy-done, bf16[1,1,4096,384]{3,2,1,0:T(8,128)(2,1)} %param.15, bf16[64,8,4096]{2,1,0:T(8,128)(2,1)} %copy-done.3, f32[512,384]{1,0:T(8,128)} %fusion.3), kind=kOutput, calls=%fused_computation.2 | convolution fusion | flops 3224502272 | bytes 15466496 | tf_op jit(solution)/shard_map/dot_general | solution.py:65
  163.8 6.4 %all-to-all-start.1 = ((bf16[64,8,4096]{2,1,0:T(8,128)(2,1)}), bf16[64,8,4096]{2,1,0:T(8,128)(2,1)}, u32[]{:S(2)}, u32[]{:S(2)}) async-start(bf16[64,8,4096]{2,1,0:T(8,128)(2,1)} %convolution_convert_fusion), calls=%async_computation.1 | async-start | bytes 8388608 | tf_op jit(solution)/shard_map/all_to_all | solution.py:134
  170.2 0.1 collective-permute-start.4
  170.3 1.0 collective-permute-start.3
  171.3 0.5 iota_add_fusion.1
  171.9 93.0 %all-to-all-done.1 = bf16[64,8,4096]{2,1,0:T(8,128)(2,1)} async-done(((bf16[64,8,4096]{2,1,0:T(8,128)(2,1)}), bf16[64,8,4096]{2,1,0:T(8,128)(2,1)}, u32[]{:S(2)}, u32[]{:S(2)}) %all-to-all-start.1) | async-done | bytes 4194336 | tf_op jit(solution)/shard_map/all_to_all | solution.py:134
  264.9 4.4 %convert_reduce_fusion = f32[16,8,4096]{2,1,0:T(8,128)} fusion(bf16[64,8,4096]{2,1,0:T(8,128)(2,1)} %all-to-all-done.1), kind=kLoop, calls=%fused_computation.1 | loop fusion | flops 3670016 | bytes 6291456 | tf_op jit(solution)/shard_map/reduce_sum | solution.py:137
  269.3 5.1 %gather_fusion = f32[128,4096]{1,0:T(8,128)} fusion(f32[128,4096]{1,0:T(8,128)} %bitcast.110, s32[1024]{0:T(1024)S(1)} %pad_clamp_fusion), kind=kCustom, calls=%fused_computation | custom fusion | bytes 4194816 | tf_op jit(solution)/shard_map/jit(_take)/gather | solution.py:140
  274.5 3.4 %fusion.17 = (f32[128]{0:T(128)S(1)}, bf16[128,4096]{1,0:T(8,128)(2,1)}) fusion(f32[128,4096]{1,0:T(8,128)} %gather_fusion, pred[128]{0:T(512)(128)(4,1)S(1)} %get-tuple-element.8, pred[128]{0:T(512)(128)(4,1)S(1)} %fusion.78, f32[128]{0:T(128)S(1)} %fusion.73, bf16[1,128,4096]{2,1,0:T(8,128)(2,1)} %param.11), kind=kLoop, calls=%fused_computation.27 | loop fusion | flops 4718464 | bytes 4195584 | tf_op jit(solution)/shard_map/reduce_sum | solution.py:48
  277.9 6.5 %fusion.47 = f32[128,1408]{1,0:T(8,128)S(1)} fusion(bf16[4096,1408]{1,0:T(8,128)(2,1)} %all-gather.2.cloned.1.call-done, bf16[128,4096]{1,0:T(8,128)(2,1)} %get-tuple-element.7, f32[128]{0:T(128)S(1)} %add_rsqrt_fusion.2), kind=kOutput, calls=%fused_computation.41 | convolution fusion | flops 1477967872 | bytes 13304320 | tf_op jit(solution)/shard_map/dot_general | solution.py:147
  284.4 0.0 copy-start.4
  284.4 0.1 multiply_reduce_fusion.1
  284.5 2.9 slice_convert_fusion
  287.4 2.7 reshape.279
  290.1 0.9 fusion.71
  291.1 0.1 fusion.66
  291.1 0.9 select_reduce_fusion
  292.0 0.3 multiply_cosine_fusion
  292.3 1.0 fusion.68
  293.3 2.0 collective-permute-start.5
  295.3 3.4 %collective-permute-start.6 = (bf16[128,256]{1,0:T(8,128)(2,1)S(1)}, bf16[128,256]{1,0:T(8,128)(2,1)}, u32[]{:S(2)}, u32[]{:S(2)}) collective-permute-start(bf16[128,256]{1,0:T(8,128)(2,1)S(1)} %pad_maximum_fusion.2), channel_id=1, source_target_pairs={{0,3},{1,4},{2,5},{3,6},{4,7},{5,8},{6,9},{7,10},{8,11},{9,12},{10... | collective-permute-start | bytes 196616 | tf_op jit(solution)/shard_map/ppermute | solution.py:44
  298.7 1.9 collective-permute-start.7
  300.6 3.5 %collective-permute-start.8 = (bf16[128,256]{1,0:T(8,128)(2,1)S(1)}, bf16[128,256]{1,0:T(8,128)(2,1)S(1)}, u32[]{:S(2)}, u32[]{:S(2)}) collective-permute-start(bf16[128,256]{1,0:T(8,128)(2,1)S(1)} %pad_maximum_fusion.2), channel_id=1, source_target_pairs={{0,1},{1,2},{2,3},{3,4},{4,5},{5,6},{6,7},{7,8},{8,9},{9,10},{10,1... | collective-permute-start | bytes 196616 | tf_op jit(solution)/shard_map/ppermute | solution.py:44
  304.1 1.1 slice_bitcast_fusion
  305.2 0.1 copy.32
  305.3 0.8 copy-done.1
  306.1 0.2 multiply_reduce_fusion
  306.4 0.1 copy.26
  306.5 0.0 copy-start.2
  306.5 0.0 copy-start.13
  306.5 1.3 multiply_multiply_fusion
  307.8 0.2 slice_negate_fusion
  308.1 1.0 fusion.60
  309.1 0.1 compare_and_fusion
  309.2 0.8 constant_dynamic-update-slice_fusion.4
  310.1 0.8 constant_dynamic-update-slice_fusion.3
  310.9 0.8 constant_dynamic-update-slice_fusion.2
  311.8 0.8 fusion.11
  312.6 1.3 fusion.39
  313.9 1.1 copy.29
  315.0 0.1 collective-permute-start.9
  315.1 3.4 %fusion.16 = bf16[1,128,4096]{2,1,0:T(8,128)(2,1)} fusion(bf16[1,128,4096]{2,1,0:T(8,128)(2,1)} %param.11, f32[128,4096]{1,0:T(8,128)} %gather_fusion, f32[128]{0:T(128)S(1)} %copy-done.9, pred[128]{0:T(512)(128)(4,1)S(1)} %copy-done.7, pred[128]{0:T(512)(128)(4,1)S(1)} %fusion.78), kind=kLoop, calls=%fused_computation.26 | loop fusion | flops 3145728 | bytes 4195072 | tf_op jit(solution)/shard_map/convert_element_type | solution.py:142
  318.6 6.3 %collective-permute-done.9 = bf16[128,1024]{1,0:T(8,128)(2,1)S(1)} collective-permute-done((bf16[128,1024]{1,0:T(8,128)(2,1)S(1)}, bf16[128,1024]{1,0:T(8,128)(2,1)S(1)}, u32[]{:S(2)}, u32[]{:S(2)}) %collective-permute-start.9) | collective-permute-done | bytes 262176 | tf_op jit(solution)/shard_map/ppermute | solution.py:21
  324.9 0.7 copy.42
  (53 shorter events, 0.3 us)
Async XLA Ops:
  7.2 146.9 %copy-start = (bf16[1,1,384,4096]{3,2,1,0:T(8,128)(2,1)S(1)}, bf16[1,1,384,4096]{3,2,1,0:T(8,128)(2,1)}, u32[]{:S(2)}) copy-start(bf16[1,1,384,4096]{3,2,1,0:T(8,128)(2,1)} %param.16) | copy-start | bytes 9437188
  7.2 270.7 %all-gather.2.cloned.1.call-start = ((), (), s32[]{:S(2)}) async-start(), calls=%async_computation.2 | async-start | bytes 12255232 | tf_op jit(solution)/shard_map/all_gather | solution.py:129
  7.2 12.7 %collective-permute-start.2 = (s32[128]{0:T(128)}, s32[128]{0:T(128)S(1)}, u32[]{:S(2)}, u32[]{:S(2)}) collective-permute-start(s32[128]{0:T(128)} %bitcast.117), channel_id=1, source_target_pairs={{64,0},{128,64},{192,128},{0,192},{65,1},{129,65},{193,129},{1,193... | collective-permute-start | bytes 1544 | tf_op jit(solution)/shard_map/ppermute | solution.py:21
  13.0 7.1 %collective-permute-start.1 = (bf16[64,256]{1,0:T(8,128)(2,1)}, bf16[64,256]{1,0:T(8,128)(2,1)S(1)}, u32[]{:S(2)}, u32[]{:S(2)}) collective-permute-start(bf16[64,256]{1,0:T(8,128)(2,1)} %bitcast.116), channel_id=1, source_target_pairs={{64,0},{128,64},{192,128},{0,192},{65,1},{129,65},{193,129},{1,193... | collective-permute-start | bytes 98312 | tf_op jit(solution)/shard_map/ppermute | solution.py:21
  13.7 6.4 %collective-permute-start = (bf16[64,1024]{1,0:T(8,128)(2,1)}, bf16[64,1024]{1,0:T(8,128)(2,1)S(1)}, u32[]{:S(2)}, u32[]{:S(2)}) collective-permute-start(bf16[64,1024]{1,0:T(8,128)(2,1)} %bitcast.115), channel_id=1, source_target_pairs={{64,0},{128,64},{192,128},{0,192},{65,1},{129,65},{193,129},{1,193... | collective-permute-start | bytes 393224 | tf_op jit(solution)/shard_map/ppermute | solution.py:21
  17.2 257.3 %copy-start.6 = (pred[128]{0:T(512)(128)(4,1)}, pred[128]{0:T(512)(128)(4,1)S(1)}, u32[]{:S(2)}) copy-start(pred[128]{0:T(512)(128)(4,1)S(1)} %get-tuple-element.8) | copy-start | bytes 388
  41.7 109.1 %copy-start.14 = (bf16[1,1,4096,384]{3,2,1,0:T(8,128)(2,1)S(1)}, bf16[1,1,4096,384]{3,2,1,0:T(8,128)(2,1)}, u32[]{:S(2)}) copy-start(bf16[1,1,4096,384]{3,2,1,0:T(8,128)(2,1)} %param.14) | copy-start | bytes 9437188
  148.8 2.0 copy-start.3
  163.8 6.4 %copy-start.15 = (f32[1,128]{1,0:T(1,128)S(1)}, f32[1,128]{1,0:T(1,128)}, u32[]{:S(2)}) copy-start(f32[1,128]{1,0:T(1,128)} %param.20) | copy-start | bytes 1540
  163.8 8.0 %copy-start.5 = (s32[1,128,8]{1,2,0:T(8,128)S(1)}, s32[1,128,8]{1,2,0:T(8,128)}, u32[]{:S(2)}) copy-start(s32[1,128,8]{1,2,0:T(8,128)} %param.12) | copy-start | bytes 12292
  163.8 8.0 %copy-start.10 = (f32[1,128,8]{1,2,0:T(8,128)S(1)}, f32[1,128,8]{1,2,0:T(8,128)}, u32[]{:S(2)}) copy-start(f32[1,128,8]{1,2,0:T(8,128)} %param.13) | copy-start | bytes 12292
  163.8 101.1 %all-to-all-start.1 = ((bf16[64,8,4096]{2,1,0:T(8,128)(2,1)}), bf16[64,8,4096]{2,1,0:T(8,128)(2,1)}, u32[]{:S(2)}, u32[]{:S(2)}) async-start(bf16[64,8,4096]{2,1,0:T(8,128)(2,1)} %convolution_convert_fusion), calls=%async_computation.1 | async-start | bytes 8388608 | tf_op jit(solution)/shard_map/all_to_all | solution.py:134
  170.2 119.9 %collective-permute-start.4 = (f32[128]{0:T(128)S(1)}, f32[128]{0:T(128)S(1)}, u32[]{:S(2)}, u32[]{:S(2)}) collective-permute-start(f32[128]{0:T(128)S(1)} %bitcast.118), channel_id=1, source_target_pairs={{64,0},{128,64},{192,128},{0,192},{65,1},{129,65},{193,129},{1,193... | collective-permute-start | bytes 1544 | tf_op jit(solution)/shard_map/ppermute | solution.py:21
  170.3 136.3 %collective-permute-start.3 = (f32[128]{0:T(128)}, f32[128]{0:T(128)}, u32[]{:S(2)}, u32[]{:S(2)}) collective-permute-start(f32[128]{0:T(128)} %bitcast.17), channel_id=1, source_target_pairs={{64,0},{128,64},{192,128},{0,192},{65,1},{129,65},{193,129},{1,193... | collective-permute-start | bytes 1544 | tf_op jit(solution)/shard_map/ppermute | solution.py:21
  171.9 102.6 %copy-start.8 = (f32[128]{0:T(128)}, f32[128]{0:T(128)S(1)}, u32[]{:S(2)}) copy-start(f32[128]{0:T(128)S(1)} %fusion.73) | copy-start | bytes 1540
  284.4 3.0 copy-start.4
  292.0 13.3 %copy-start.11 = (s32[128]{0:T(128)}, s32[128]{0:T(128)S(1)}, u32[]{:S(2)}) copy-start(s32[128]{0:T(128)S(1)} %select_reduce_fusion) | copy-start | bytes 1540
  293.3 15.9 %collective-permute-start.5 = (bf16[128,256]{1,0:T(8,128)(2,1)S(1)}, bf16[128,256]{1,0:T(8,128)(2,1)}, u32[]{:S(2)}, u32[]{:S(2)}) collective-permute-start(bf16[128,256]{1,0:T(8,128)(2,1)S(1)} %pad_maximum_fusion.2), channel_id=1, source_target_pairs={{0,4},{1,5},{2,6},{3,7},{4,8},{5,9},{6,10},{7,11},{8,12},{9,13},{1... | collective-permute-start | bytes 196616 | tf_op jit(solution)/shard_map/ppermute | solution.py:44
  295.3 14.8 %collective-permute-start.6 = (bf16[128,256]{1,0:T(8,128)(2,1)S(1)}, bf16[128,256]{1,0:T(8,128)(2,1)}, u32[]{:S(2)}, u32[]{:S(2)}) collective-permute-start(bf16[128,256]{1,0:T(8,128)(2,1)S(1)} %pad_maximum_fusion.2), channel_id=1, source_target_pairs={{0,3},{1,4},{2,5},{3,6},{4,7},{5,8},{6,9},{7,10},{8,11},{9,12},{10... | collective-permute-start | bytes 196616 | tf_op jit(solution)/shard_map/ppermute | solution.py:44
  298.7 12.2 %collective-permute-start.7 = (bf16[128,256]{1,0:T(8,128)(2,1)S(1)}, bf16[128,256]{1,0:T(8,128)(2,1)}, u32[]{:S(2)}, u32[]{:S(2)}) collective-permute-start(bf16[128,256]{1,0:T(8,128)(2,1)S(1)} %pad_maximum_fusion.2), channel_id=1, source_target_pairs={{0,2},{1,3},{2,4},{3,5},{4,6},{5,7},{6,8},{7,9},{8,10},{9,11},{10,... | collective-permute-start | bytes 196616 | tf_op jit(solution)/shard_map/ppermute | solution.py:44
  300.6 11.2 %collective-permute-start.8 = (bf16[128,256]{1,0:T(8,128)(2,1)S(1)}, bf16[128,256]{1,0:T(8,128)(2,1)S(1)}, u32[]{:S(2)}, u32[]{:S(2)}) collective-permute-start(bf16[128,256]{1,0:T(8,128)(2,1)S(1)} %pad_maximum_fusion.2), channel_id=1, source_target_pairs={{0,1},{1,2},{2,3},{3,4},{4,5},{5,6},{6,7},{7,8},{8,9},{9,10},{10,1... | collective-permute-start | bytes 196616 | tf_op jit(solution)/shard_map/ppermute | solution.py:44
  305.3 0.8 copy-start.1
  306.5 1.6 copy-start.2
  306.5 2.5 copy-start.12
  306.5 2.5 copy-start.13
  312.6 2.5 copy-start.7
  312.6 2.5 copy-start.9
  315.0 9.9 %collective-permute-start.9 = (bf16[128,1024]{1,0:T(8,128)(2,1)S(1)}, bf16[128,1024]{1,0:T(8,128)(2,1)S(1)}, u32[]{:S(2)}, u32[]{:S(2)}) collective-permute-start(bf16[128,1024]{1,0:T(8,128)(2,1)S(1)} %copy.29), channel_id=1, source_target_pairs={{192,0},{0,64},{64,128},{128,192},{193,1},{1,65},{65,129},{129,193... | collective-permute-start | bytes 786440 | tf_op jit(solution)/shard_map/ppermute | solution.py:21
Sparse Core Ops, SparseCore 0:
  41.8 129.6 all-gather.1

commit v8 on v7

--- a/solution.py
+++ b/solution.py
@@ -5,6 +5,7 @@
 from jax import lax
 from jax.sharding import PartitionSpec as P
 
+
 OWNERS = 4
 SEG_MOST = 512
 
@@ -19,23 +20,6 @@
     devices = range(lax.axis_size(axis))
     route = [((i - distance) % len(devices), i) for i in devices]
     return lax.ppermute(block, axis, route)
-
-
-def prefix(shard, axis, combine, identity):
-    length, mine = (lax.axis_size(axis), lax.axis_index(axis))
-    everything = jax.tree.map(lambda part: lax.all_gather(part, axis), shard)
-    start = jax.tree.map(
-        lambda part, zero: jnp.broadcast_to(jnp.asarray(zero, part.dtype), part.shape),
-        shard,
-        identity,
-    )
-
-    def step(k, before):
-        reached = k < mine
-        new = combine(before, jax.tree.map(lambda part: part[k], everything))
-        return jax.tree.map(lambda a, b: jnp.where(reached, a, b), new, before)
-
-    return lax.fori_loop(0, length, step, start)
 
 
 def passed_along_2(value, axis, steps):
@@ -63,15 +47,6 @@
     up_proj = jnp.dot(row_block, up_part, preferred_element_type=jnp.float32)
     activated = (jax.nn.silu(gate_proj) * up_proj).astype(jnp.bfloat16)
     return jnp.dot(activated, down_part, preferred_element_type=jnp.float32)
-
-
-def keep_later(earlier, later):
-    same_id = earlier[0] == later[0]
-    newer_id = later[0] > earlier[0]
-    start_at = jnp.where(
-        same_id, jnp.minimum(earlier[1], later[1]), jnp.where(newer_id, later[1], earlier[1])
-    )
-    return (jnp.maximum(earlier[0], later[0]), start_at)
 
 
 def on_device(
@@ -133,7 +108,8 @@
     ).reshape(received.shape)
     returned_rows = lax.all_to_all(
         partial_out.astype(jnp.bfloat16), EP, split_axis=0, concat_axis=0, tiled=True
-    ).astype(partial_out.dtype)
+    )
+    returned_rows = returned_rows.astype(partial_out.dtype)
     merged = jnp.sum(
         returned_rows.reshape(expert_count, OWNERS, capacity, model_width), axis=1
     ).reshape(expert_count * capacity, model_width)
@@ -153,15 +129,15 @@
         .reshape(-1)[: device_count * token_count]
     )
     global_index = first_index + jnp.arange(token_count, dtype=jnp.int32)
-    key_index = (
-        first_index - reach * token_count + jnp.arange((reach + 1) * token_count, dtype=jnp.int32)
-    )
     section_index = jnp.arange(device_count * token_count, dtype=jnp.int32)
     start_index = jnp.min(
         jnp.where(all_segments[None, :] == segment_row[:, None], section_index[None, :], FAR_INDEX),
         axis=1,
     )
     position = global_index - start_index
+    key_index = (
+        first_index - reach * token_count + jnp.arange((reach + 1) * token_count, dtype=jnp.int32)
+    )
     query = rotary(
         rms_rows(query_raw.reshape(token_count, head_count, head_dim)) * next_gain_query, position
     ).astype(jnp.bfloat16)
@@ -221,6 +197,7 @@
         P("section", EP),
     )
     out_specs = (P("section", EP, None), P("section", EP, None))
+
     return jax.shard_map(
         on_device, mesh=split_mesh, in_specs=in_specs, out_specs=out_specs, check_vma=False
     )

time: 337 us -> 337 us (level)
  no operation moved by 1% of the time
where the time goes in v8:
time: 337 us; the launch traced here: 332 us
  blocking collectives  125 us (37%)
  waiting for transfers between devices  99.4 us (29%)
  starting transfers between devices  24.9 us (7%)
  matrix products  24.3 us (7%)
  other arithmetic  24.2 us (7%)
  local copies, waits for them, and re-layouts  20.4 us (6%)
  between operations  14.4 us (4%)
    all_to_all x1, blocking collectives, on_device(): lax.all_to_all(spread, EP, split_axis=0, concat_axis=0, tiled=True)  107 us
    all_to_all x1, waiting for transfers between devices, on_device(): lax.all_to_all(partial_out.astype(jnp.bfloat16), EP, split_axis=0, concat...  93 us
    all_gather x1, blocking collectives, on_device(): projection = lax.all_gather(projection, EP[-1], axis=0, tiled=True)  17.7 us
    ppermute x4, starting transfers between devices, passed_along_2(): lax.ppermute(value, axis, [(source, source + steps) for source in range(l...  10.8 us
    dot_general x1, matrix products, feed_forward(): return jnp.dot(activated, down_part, preferred_element_type=jnp.float32)  9.79 us
    ppermute x6, starting transfers between devices, passed_along(): return lax.ppermute(block, axis, route)  7.72 us
    unnamed x39, local copies, waits for them, and re-layouts  7.32 us
  transfers between devices with their start and end apart: 12, of which 2 were waited for; matrix products, arithmetic and copies ran while one was open for 18% of the time, Pallas kernels for 0%

profile of v8, /device:TPU:32, one launch (start us, length us, event | category | flops | bytes accessed | tf_op | source)
XLA Modules:
  0.0 332.5 jit_solution(2821371864683105371)
XLA Ops:
  7.2 0.0 copy-start
  7.2 0.0 all-gather.2.cloned.1.call-start
  7.2 5.8 %collective-permute-start.2 = (s32[128]{0:T(128)}, s32[128]{0:T(128)S(1)}, u32[]{:S(2)}, u32[]{:S(2)}) collective-permute-start(s32[128]{0:T(128)} %bitcast.117), channel_id=1, source_target_pairs={{64,0},{128,64},{192,128},{0,192},{65,1},{129,65},{193,129},{1,193... | collective-permute-start | bytes 1544 | tf_op jit(solution)/shard_map/ppermute | solution.py:22
  13.0 0.7 collective-permute-start.1
  13.7 0.1 collective-permute-start
  13.8 0.7 fusion.78
  14.5 0.7 fusion.74
  15.2 1.5 fusion.13
  16.7 0.1 fusion.70
  16.8 0.2 reduce_window_sum.11
  17.0 0.2 select_reduce_fusion.1
  17.2 2.7 fusion
  19.9 0.1 convert_element_type.75
  20.1 17.7 %all_gather.6 = bf16[256,1408]{1,0:T(8,128)(2,1)} all-gather(bf16[64,1408]{1,0:T(8,128)(2,1)S(1)} %fusion.65), channel_id=1, replica_groups=mesh['section'=4,'ep_y'=4,'ep_x'=4,'ep_z'=4] {'ep_z'}, dimensions={0}, use_global_device_ids=true | all-gather | bytes 901120 | tf_op jit(solution)/shard_map/all_gather | solution.py:102
  37.9 3.8 %broadcast_in_dim.113 = bf16[16,4,8,4096]{3,2,1,0:T(8,128)(2,1)} broadcast(bf16[16,8,4096]{2,1,0:T(8,128)(2,1)} %fusion), dimensions={0,2,3} | broadcast | bytes 5242880 | tf_op jit(solution)/shard_map/broadcast_in_dim | solution.py:86
  41.6 0.0 all-gather.2.cloned.1.call-update
  41.7 0.0 copy-start.14
  41.7 107.1 %all_to_all.10 = bf16[64,8,4096]{2,1,0:T(8,128)(2,1)S(1)} all-to-all(bf16[64,8,4096]{2,1,0:T(8,128)(2,1)} %bitcast.111), channel_id=1, replica_groups=mesh['section'=4,'ep_y'=4,'ep_x'=4,'ep_z'=4] {'ep_y','ep_x','ep_z'}, dimensions={0} | all-to-all | bytes 8388608 | tf_op jit(solution)/shard_map/all_to_all | solution.py:105
  148.8 2.0 copy-done.3
  150.8 3.2 fusion.3
  154.0 9.8 %convolution_convert_fusion = bf16[64,8,4096]{2,1,0:T(8,128)(2,1)} fusion(bf16[1,1,384,4096]{3,2,1,0:T(8,128)(2,1)S(1)} %copy-done, bf16[1,1,4096,384]{3,2,1,0:T(8,128)(2,1)} %param.15, bf16[64,8,4096]{2,1,0:T(8,128)(2,1)} %copy-done.3, f32[512,384]{1,0:T(8,128)} %fusion.3), kind=kOutput, calls=%fused_computation.2 | convolution fusion | flops 3224502272 | bytes 15466496 | tf_op jit(solution)/shard_map/dot_general | solution.py:49
  163.8 6.4 %all-to-all-start.1 = ((bf16[64,8,4096]{2,1,0:T(8,128)(2,1)}), bf16[64,8,4096]{2,1,0:T(8,128)(2,1)}, u32[]{:S(2)}, u32[]{:S(2)}) async-start(bf16[64,8,4096]{2,1,0:T(8,128)(2,1)} %convolution_convert_fusion), calls=%async_computation.1 | async-start | bytes 8388608 | tf_op jit(solution)/shard_map/all_to_all | solution.py:109
  170.2 0.1 collective-permute-start.4
  170.3 1.0 collective-permute-start.3
  171.3 0.5 iota_add_fusion.1
  171.9 93.0 %all-to-all-done.1 = bf16[64,8,4096]{2,1,0:T(8,128)(2,1)} async-done(((bf16[64,8,4096]{2,1,0:T(8,128)(2,1)}), bf16[64,8,4096]{2,1,0:T(8,128)(2,1)}, u32[]{:S(2)}, u32[]{:S(2)}) %all-to-all-start.1) | async-done | bytes 4194336 | tf_op jit(solution)/shard_map/all_to_all | solution.py:109
  264.9 4.4 %convert_reduce_fusion = f32[16,8,4096]{2,1,0:T(8,128)} fusion(bf16[64,8,4096]{2,1,0:T(8,128)(2,1)} %all-to-all-done.1), kind=kLoop, calls=%fused_computation.1 | loop fusion | flops 3670016 | bytes 6291456 | tf_op jit(solution)/shard_map/reduce_sum | solution.py:113
  269.3 5.1 %gather_fusion = f32[128,4096]{1,0:T(8,128)} fusion(f32[128,4096]{1,0:T(8,128)} %bitcast.110, s32[1024]{0:T(1024)S(1)} %pad_clamp_fusion), kind=kCustom, calls=%fused_computation | custom fusion | bytes 4194816 | tf_op jit(solution)/shard_map/jit(_take)/gather | solution.py:116
  274.5 3.4 %fusion.17 = (f32[128]{0:T(128)S(1)}, bf16[128,4096]{1,0:T(8,128)(2,1)}) fusion(f32[128,4096]{1,0:T(8,128)} %gather_fusion, pred[128]{0:T(512)(128)(4,1)S(1)} %get-tuple-element.8, pred[128]{0:T(512)(128)(4,1)S(1)} %fusion.78, f32[128]{0:T(128)S(1)} %fusion.73, bf16[1,128,4096]{2,1,0:T(8,128)(2,1)} %param.11), kind=kLoop, calls=%fused_computation.27 | loop fusion | flops 4718464 | bytes 4195584 | tf_op jit(solution)/shard_map/reduce_sum | solution.py:32
  277.9 6.5 %fusion.47 = f32[128,1408]{1,0:T(8,128)S(1)} fusion(bf16[4096,1408]{1,0:T(8,128)(2,1)} %all-gather.2.cloned.1.call-done, bf16[128,4096]{1,0:T(8,128)(2,1)} %get-tuple-element.7, f32[128]{0:T(128)S(1)} %add_rsqrt_fusion.2), kind=kOutput, calls=%fused_computation.41 | convolution fusion | flops 1477967872 | bytes 13304320 | tf_op jit(solution)/shard_map/dot_general | solution.py:123
  284.4 0.0 copy-start.4
  284.4 0.1 multiply_reduce_fusion.1
  284.5 2.9 slice_convert_fusion
  287.4 2.7 reshape.279
  290.1 0.9 fusion.71
  291.1 0.1 fusion.66
  291.1 0.9 select_reduce_fusion
  292.0 0.3 multiply_cosine_fusion
  292.3 1.0 fusion.68
  293.3 2.0 collective-permute-start.5
  295.3 3.4 %collective-permute-start.6 = (bf16[128,256]{1,0:T(8,128)(2,1)S(1)}, bf16[128,256]{1,0:T(8,128)(2,1)}, u32[]{:S(2)}, u32[]{:S(2)}) collective-permute-start(bf16[128,256]{1,0:T(8,128)(2,1)S(1)} %pad_maximum_fusion.2), channel_id=1, source_target_pairs={{0,3},{1,4},{2,5},{3,6},{4,7},{5,8},{6,9},{7,10},{8,11},{9,12},{10... | collective-permute-start | bytes 196616 | tf_op jit(solution)/shard_map/ppermute | solution.py:28
  298.7 1.9 collective-permute-start.7
  300.6 3.5 %collective-permute-start.8 = (bf16[128,256]{1,0:T(8,128)(2,1)S(1)}, bf16[128,256]{1,0:T(8,128)(2,1)S(1)}, u32[]{:S(2)}, u32[]{:S(2)}) collective-permute-start(bf16[128,256]{1,0:T(8,128)(2,1)S(1)} %pad_maximum_fusion.2), channel_id=1, source_target_pairs={{0,1},{1,2},{2,3},{3,4},{4,5},{5,6},{6,7},{7,8},{8,9},{9,10},{10,1... | collective-permute-start | bytes 196616 | tf_op jit(solution)/shard_map/ppermute | solution.py:28
  304.1 1.1 slice_bitcast_fusion
  305.2 0.1 copy.32
  305.3 0.0 copy-start.1
  305.3 0.8 copy-done.1
  306.1 0.2 multiply_reduce_fusion
  306.4 0.1 copy.26
  306.5 0.0 copy-start.2
  306.5 1.3 multiply_multiply_fusion
  307.8 0.2 slice_negate_fusion
  308.1 1.0 fusion.60
  309.1 0.1 compare_and_fusion
  309.2 0.8 constant_dynamic-update-slice_fusion.4
  310.1 0.8 constant_dynamic-update-slice_fusion.3
  310.9 0.8 constant_dynamic-update-slice_fusion.2
  311.8 0.8 fusion.11
  312.6 1.3 fusion.39
  313.9 1.1 copy.29
  315.0 0.1 collective-permute-start.9
  315.1 3.4 %fusion.16 = bf16[1,128,4096]{2,1,0:T(8,128)(2,1)} fusion(bf16[1,128,4096]{2,1,0:T(8,128)(2,1)} %param.11, f32[128,4096]{1,0:T(8,128)} %gather_fusion, f32[128]{0:T(128)S(1)} %copy-done.9, pred[128]{0:T(512)(128)(4,1)S(1)} %copy-done.7, pred[128]{0:T(512)(128)(4,1)S(1)} %fusion.78), kind=kLoop, calls=%fused_computation.26 | loop fusion | flops 3145728 | bytes 4195072 | tf_op jit(solution)/shard_map/convert_element_type | solution.py:118
  318.6 6.3 %collective-permute-done.9 = bf16[128,1024]{1,0:T(8,128)(2,1)S(1)} collective-permute-done((bf16[128,1024]{1,0:T(8,128)(2,1)S(1)}, bf16[128,1024]{1,0:T(8,128)(2,1)S(1)}, u32[]{:S(2)}, u32[]{:S(2)}) %collective-permute-start.9) | collective-permute-done | bytes 262176 | tf_op jit(solution)/shard_map/ppermute | solution.py:22
  324.9 0.7 copy.42
  (53 shorter events, 0.3 us)
Async XLA Ops:
  7.2 146.9 %copy-start = (bf16[1,1,384,4096]{3,2,1,0:T(8,128)(2,1)S(1)}, bf16[1,1,384,4096]{3,2,1,0:T(8,128)(2,1)}, u32[]{:S(2)}) copy-start(bf16[1,1,384,4096]{3,2,1,0:T(8,128)(2,1)} %param.16) | copy-start | bytes 9437188
  7.2 270.7 %all-gather.2.cloned.1.call-start = ((), (), s32[]{:S(2)}) async-start(), calls=%async_computation.2 | async-start | bytes 12255232 | tf_op jit(solution)/shard_map/all_gather | solution.py:104
  7.2 12.7 %collective-permute-start.2 = (s32[128]{0:T(128)}, s32[128]{0:T(128)S(1)}, u32[]{:S(2)}, u32[]{:S(2)}) collective-permute-start(s32[128]{0:T(128)} %bitcast.117), channel_id=1, source_target_pairs={{64,0},{128,64},{192,128},{0,192},{65,1},{129,65},{193,129},{1,193... | collective-permute-start | bytes 1544 | tf_op jit(solution)/shard_map/ppermute | solution.py:22
  13.0 7.1 %collective-permute-start.1 = (bf16[64,256]{1,0:T(8,128)(2,1)}, bf16[64,256]{1,0:T(8,128)(2,1)S(1)}, u32[]{:S(2)}, u32[]{:S(2)}) collective-permute-start(bf16[64,256]{1,0:T(8,128)(2,1)} %bitcast.116), channel_id=1, source_target_pairs={{64,0},{128,64},{192,128},{0,192},{65,1},{129,65},{193,129},{1,193... | collective-permute-start | bytes 98312 | tf_op jit(solution)/shard_map/ppermute | solution.py:22
  13.7 6.4 %collective-permute-start = (bf16[64,1024]{1,0:T(8,128)(2,1)}, bf16[64,1024]{1,0:T(8,128)(2,1)S(1)}, u32[]{:S(2)}, u32[]{:S(2)}) collective-permute-start(bf16[64,1024]{1,0:T(8,128)(2,1)} %bitcast.115), channel_id=1, source_target_pairs={{64,0},{128,64},{192,128},{0,192},{65,1},{129,65},{193,129},{1,193... | collective-permute-start | bytes 393224 | tf_op jit(solution)/shard_map/ppermute | solution.py:22
  17.2 257.3 %copy-start.6 = (pred[128]{0:T(512)(128)(4,1)}, pred[128]{0:T(512)(128)(4,1)S(1)}, u32[]{:S(2)}) copy-start(pred[128]{0:T(512)(128)(4,1)S(1)} %get-tuple-element.8) | copy-start | bytes 388
  41.7 109.1 %copy-start.14 = (bf16[1,1,4096,384]{3,2,1,0:T(8,128)(2,1)S(1)}, bf16[1,1,4096,384]{3,2,1,0:T(8,128)(2,1)}, u32[]{:S(2)}) copy-start(bf16[1,1,4096,384]{3,2,1,0:T(8,128)(2,1)} %param.14) | copy-start | bytes 9437188
  148.8 2.0 copy-start.3
  163.8 6.4 %copy-start.15 = (f32[1,128]{1,0:T(1,128)S(1)}, f32[1,128]{1,0:T(1,128)}, u32[]{:S(2)}) copy-start(f32[1,128]{1,0:T(1,128)} %param.20) | copy-start | bytes 1540
  163.8 8.0 %copy-start.5 = (s32[1,128,8]{1,2,0:T(8,128)S(1)}, s32[1,128,8]{1,2,0:T(8,128)}, u32[]{:S(2)}) copy-start(s32[1,128,8]{1,2,0:T(8,128)} %param.12) | copy-start | bytes 12292
  163.8 8.0 %copy-start.10 = (f32[1,128,8]{1,2,0:T(8,128)S(1)}, f32[1,128,8]{1,2,0:T(8,128)}, u32[]{:S(2)}) copy-start(f32[1,128,8]{1,2,0:T(8,128)} %param.13) | copy-start | bytes 12292
  163.8 101.1 %all-to-all-start.1 = ((bf16[64,8,4096]{2,1,0:T(8,128)(2,1)}), bf16[64,8,4096]{2,1,0:T(8,128)(2,1)}, u32[]{:S(2)}, u32[]{:S(2)}) async-start(bf16[64,8,4096]{2,1,0:T(8,128)(2,1)} %convolution_convert_fusion), calls=%async_computation.1 | async-start | bytes 8388608 | tf_op jit(solution)/shard_map/all_to_all | solution.py:109
  170.2 119.9 %collective-permute-start.4 = (f32[128]{0:T(128)S(1)}, f32[128]{0:T(128)S(1)}, u32[]{:S(2)}, u32[]{:S(2)}) collective-permute-start(f32[128]{0:T(128)S(1)} %bitcast.118), channel_id=1, source_target_pairs={{64,0},{128,64},{192,128},{0,192},{65,1},{129,65},{193,129},{1,193... | collective-permute-start | bytes 1544 | tf_op jit(solution)/shard_map/ppermute | solution.py:22
  170.3 136.3 %collective-permute-start.3 = (f32[128]{0:T(128)}, f32[128]{0:T(128)}, u32[]{:S(2)}, u32[]{:S(2)}) collective-permute-start(f32[128]{0:T(128)} %bitcast.17), channel_id=1, source_target_pairs={{64,0},{128,64},{192,128},{0,192},{65,1},{129,65},{193,129},{1,193... | collective-permute-start | bytes 1544 | tf_op jit(solution)/shard_map/ppermute | solution.py:22
  171.9 102.6 %copy-start.8 = (f32[128]{0:T(128)}, f32[128]{0:T(128)S(1)}, u32[]{:S(2)}) copy-start(f32[128]{0:T(128)S(1)} %fusion.73) | copy-start | bytes 1540
  284.4 3.0 copy-start.4
  292.0 13.3 %copy-start.11 = (s32[128]{0:T(128)}, s32[128]{0:T(128)S(1)}, u32[]{:S(2)}) copy-start(s32[128]{0:T(128)S(1)} %select_reduce_fusion) | copy-start | bytes 1540
  293.3 15.9 %collective-permute-start.5 = (bf16[128,256]{1,0:T(8,128)(2,1)S(1)}, bf16[128,256]{1,0:T(8,128)(2,1)}, u32[]{:S(2)}, u32[]{:S(2)}) collective-permute-start(bf16[128,256]{1,0:T(8,128)(2,1)S(1)} %pad_maximum_fusion.2), channel_id=1, source_target_pairs={{0,4},{1,5},{2,6},{3,7},{4,8},{5,9},{6,10},{7,11},{8,12},{9,13},{1... | collective-permute-start | bytes 196616 | tf_op jit(solution)/shard_map/ppermute | solution.py:28
  295.3 14.8 %collective-permute-start.6 = (bf16[128,256]{1,0:T(8,128)(2,1)S(1)}, bf16[128,256]{1,0:T(8,128)(2,1)}, u32[]{:S(2)}, u32[]{:S(2)}) collective-permute-start(bf16[128,256]{1,0:T(8,128)(2,1)S(1)} %pad_maximum_fusion.2), channel_id=1, source_target_pairs={{0,3},{1,4},{2,5},{3,6},{4,7},{5,8},{6,9},{7,10},{8,11},{9,12},{10... | collective-permute-start | bytes 196616 | tf_op jit(solution)/shard_map/ppermute | solution.py:28
  298.7 12.2 %collective-permute-start.7 = (bf16[128,256]{1,0:T(8,128)(2,1)S(1)}, bf16[128,256]{1,0:T(8,128)(2,1)}, u32[]{:S(2)}, u32[]{:S(2)}) collective-permute-start(bf16[128,256]{1,0:T(8,128)(2,1)S(1)} %pad_maximum_fusion.2), channel_id=1, source_target_pairs={{0,2},{1,3},{2,4},{3,5},{4,6},{5,7},{6,8},{7,9},{8,10},{9,11},{10,... | collective-permute-start | bytes 196616 | tf_op jit(solution)/shard_map/ppermute | solution.py:28
  300.6 11.2 %collective-permute-start.8 = (bf16[128,256]{1,0:T(8,128)(2,1)S(1)}, bf16[128,256]{1,0:T(8,128)(2,1)S(1)}, u32[]{:S(2)}, u32[]{:S(2)}) collective-permute-start(bf16[128,256]{1,0:T(8,128)(2,1)S(1)} %pad_maximum_fusion.2), channel_id=1, source_target_pairs={{0,1},{1,2},{2,3},{3,4},{4,5},{5,6},{6,7},{7,8},{8,9},{9,10},{10,1... | collective-permute-start | bytes 196616 | tf_op jit(solution)/shard_map/ppermute | solution.py:28
  305.3 0.8 copy-start.1
  306.5 1.6 copy-start.2
  306.5 2.5 copy-start.12
  306.5 2.5 copy-start.13
  312.6 2.5 copy-start.7
  312.6 2.5 copy-start.9
  315.0 9.9 %collective-permute-start.9 = (bf16[128,1024]{1,0:T(8,128)(2,1)S(1)}, bf16[128,1024]{1,0:T(8,128)(2,1)S(1)}, u32[]{:S(2)}, u32[]{:S(2)}) collective-permute-start(bf16[128,1024]{1,0:T(8,128)(2,1)S(1)} %copy.29), channel_id=1, source_target_pairs={{192,0},{0,64},{64,128},{128,192},{193,1},{1,65},{65,129},{129,193... | collective-permute-start | bytes 786440 | tf_op jit(solution)/shard_map/ppermute | solution.py:22
Sparse Core Ops, SparseCore 0:
  41.8 129.6 all-gather.1

commit v9 on v8

--- a/solution.py
+++ b/solution.py
@@ -77,29 +77,44 @@
     member = ((chosen[:, None] == expert_ids[None, :]) & has_route[:, None]).astype(jnp.int32)
     rank_within = jnp.sum((jnp.cumsum(member, axis=0) - member) * member, axis=-1)
     slot_index = jnp.where(has_route, chosen * capacity + rank_within, -1)
-    slot_ids = jnp.arange(expert_count * capacity, dtype=jnp.int32)
-    placing = (slot_ids[:, None] == slot_index[None, :]).astype(jnp.bfloat16)
-    packed = jnp.dot(placing, normed, preferred_element_type=jnp.float32).astype(jnp.bfloat16)
+    row_ids = jnp.arange(device_count * capacity, dtype=jnp.int32)
+    row_expert = row_ids // (OWNERS * capacity)
+    row_slot = row_ids % capacity
+    placing = (
+        (row_expert * capacity + row_slot)[:, None] == slot_index[None, :]
+    ).astype(jnp.bfloat16)
+    spread = (
+        jnp.dot(placing, normed, preferred_element_type=jnp.float32)
+        .astype(jnp.bfloat16)
+        .reshape(device_count, capacity, model_width)
+    )
     gate_part = w_gate[0, 0]
     up_part = w_up[0, 0]
     down_part = w_down[0, 0]
-    spread = jnp.broadcast_to(
-        packed.reshape(expert_count, 1, capacity, model_width),
-        (expert_count, OWNERS, capacity, model_width),
-    ).reshape(device_count, capacity, model_width)
-    next_query, next_keyval, segment_row, next_gain_query, next_gain_key = passed_along(
-        (w_query[0], w_keyval[0], segment_ids[0], gain_query[0], gain_key[0]), "section", -1
+    segment_row, next_gain_query, next_gain_key = passed_along(
+        (segment_ids[0], gain_query[0], gain_key[0]), "section", -1
     )
     first_index = lax.axis_index(EP) * token_count
     reach = (SEG_MOST - 1) // token_count + 1
-    shard_rows = next_query.shape[0]
+    shard_rows = w_query.shape[1]
     per_row = -(-token_count // shard_rows)
-    carried = jnp.pad(segment_row, (0, shard_rows * per_row - token_count)).reshape(
+    carried = jnp.pad(segment_ids[0], (0, shard_rows * per_row - token_count)).reshape(
         shard_rows, per_row
     )
     carried = jnp.pad(carried.astype(jnp.bfloat16), ((0, 0), (0, 128 - per_row)))
-    projection = jnp.concatenate([next_query, next_keyval, carried], axis=-1)
-    projection = lax.all_gather(projection, EP[-1], axis=0, tiled=True)
+    own_shard = jnp.concatenate([w_query[0], w_keyval[0], carried], axis=-1)
+    section_count = lax.axis_size("section")
+    owner_count = lax.axis_size(EP[-1])
+    pieces = []
+    for shift in range(owner_count):
+        route = [
+            (((s + 1) % section_count) * owner_count + (z + shift) % owner_count, s * owner_count + z)
+            for s in range(section_count)
+            for z in range(owner_count)
+        ]
+        pieces.append(lax.ppermute(own_shard, ("section", EP[-1]), route))
+    projection = jnp.roll(jnp.stack(pieces), lax.axis_index(EP[-1]), axis=0)
+    projection = projection.reshape(-1, own_shard.shape[-1])
     spread, projection = lax.optimization_barrier((spread, projection))
     projection = lax.all_gather(projection, EP[:-1], axis=0, tiled=True)
     received = lax.all_to_all(spread, EP, split_axis=0, concat_axis=0, tiled=True)
@@ -109,12 +124,9 @@
     returned_rows = lax.all_to_all(
         partial_out.astype(jnp.bfloat16), EP, split_axis=0, concat_axis=0, tiled=True
     )
-    returned_rows = returned_rows.astype(partial_out.dtype)
-    merged = jnp.sum(
-        returned_rows.reshape(expert_count, OWNERS, capacity, model_width), axis=1
-    ).reshape(expert_count * capacity, model_width)
-    fetched_rows = jnp.take(merged, jnp.maximum(slot_index, 0), axis=0)
-    expert_out = jnp.where(has_route[:, None], fetched_rows, 0.0)
+    expert_out = jnp.dot(
+        placing.T, returned_rows.reshape(-1, model_width), preferred_element_type=jnp.float32
+    )
     layer_out = (wide_tokens + weight_kept[:, None] * expert_out).astype(jnp.bfloat16)
     lifted = rms_rows(layer_out.astype(jnp.float32)).astype(jnp.bfloat16)
     head_dim = gain_query.shape[-1]

time: 337 us -> 322 us (0.955)
  blocking collectives: 125 us -> 106 us
  other arithmetic: 24.2 us -> 16.9 us
  matrix products: 24.3 us -> 30.1 us
  waiting for transfers between devices: 99.4 us -> 105 us
  local copies, waits for them, and re-layouts: 20.4 us -> 15.9 us
    all_gather x1 -> x0, blocking collectives: 17.7 us -> none  [on_device(): projection = lax.all_gather(projection, EP[-1], axis=0, tiled=True)]
    ppermute x0 -> x4, starting transfers between devices: none -> 7.24 us  [on_device(): pieces.append(lax.ppermute(own_shard, ('section', EP[-1]), route))]
    gather x1 -> x0, local copies, waits for them, and re-layouts: 5.12 us -> none  [on_device(): fetched_rows = jnp.take(merged, jnp.maximum(slot_index, 0), axis=0)]
    dot_general x0 -> x1, matrix products: none -> 4.52 us  [on_device(): jnp.dot(placing.T, returned_rows.reshape(-1, model_width), preferred_elem...]
    reduce_sum x1 -> x0, other arithmetic: 4.44 us -> none  [on_device(): jnp.sum(returned_rows.reshape(expert_count, OWNERS, capacity, model_width...]
    ppermute x0 -> x4, waiting for transfers between devices: none -> 4.21 us  [on_device(): pieces.append(lax.ppermute(own_shard, ('section', EP[-1]), route))]
    ppermute x6 -> x4, starting transfers between devices: 7.72 us -> 3.61 us  [passed_along(): return lax.ppermute(block, axis, route)]
    broadcast_in_dim x1 -> x0, local copies, waits for them, and re-layouts: 3.78 us -> none  [on_device(): jnp.broadcast_to(packed.reshape(expert_count, 1, capacity, model_width),...]
  transfers between devices with their start and end apart: 12 -> 14, of which waited for: 2 -> 4; matrix products, arithmetic and copies ran while one was open for 18% -> 16% of each run, Pallas kernels for 0% -> 0%
where the time goes in v9:
time: 322 us; the launch traced here: 316 us
  blocking collectives  106 us (33%)
  waiting for transfers between devices  105 us (33%)
  matrix products  30.1 us (9%)
  starting transfers between devices  28.2 us (9%)
  other arithmetic  16.9 us (5%)
  local copies, waits for them, and re-layouts  15.9 us (5%)
  between operations  14.4 us (4%)
    all_to_all x1, blocking collectives, on_device(): lax.all_to_all(spread, EP, split_axis=0, concat_axis=0, tiled=True)  106 us
    all_to_all x1, waiting for transfers between devices, on_device(): lax.all_to_all(partial_out.astype(jnp.bfloat16), EP, split_axis=0, concat...  90.5 us
    ppermute x4, starting transfers between devices, passed_along_2(): lax.ppermute(value, axis, [(source, source + steps) for source in range(l...  10.8 us
    unnamed x40, local copies, waits for them, and re-layouts  10.1 us
    ppermute x4, waiting for transfers between devices, passed_along(): return lax.ppermute(block, axis, route)  10 us
    dot_general x1, matrix products, feed_forward(): return jnp.dot(activated, down_part, preferred_element_type=jnp.float32)  9.88 us
    ppermute x4, starting transfers between devices, on_device(): pieces.append(lax.ppermute(own_shard, ('section', EP[-1]), route))  7.24 us
    all_to_all x1, starting transfers between devices, on_device(): lax.all_to_all(partial_out.astype(jnp.bfloat16), EP, split_axis=0, concat...  6.52 us
  transfers between devices with their start and end apart: 14, of which 4 were waited for; matrix products, arithmetic and copies ran while one was open for 16% of the time, Pallas kernels for 0%

profile of v9, /device:TPU:32, one launch (start us, length us, event | category | flops | bytes accessed | tf_op | source)
XLA Modules:
  0.0 316.3 jit_solution(10946617933914244820)
XLA Ops:
  7.2 0.0 all-gather.2.cloned.1.call-start
  7.2 0.8 convert_reduce_fusion
  8.0 0.1 convert_element_type.67
  8.2 1.6 fusion.64
  9.8 5.7 %collective-permute-start = (bf16[64,1408]{1,0:T(8,128)(2,1)}, bf16[64,1408]{1,0:T(8,128)(2,1)S(1)}, u32[]{:S(2)}, u32[]{:S(2)}) collective-permute-start(bf16[64,1408]{1,0:T(8,128)(2,1)} %fusion.64), channel_id=1, source_target_pairs={{64,0},{65,1},{66,2},{67,3},{128,64},{129,65},{130,66},{131,67},{1... | collective-permute-start | bytes 540680 | tf_op jit(solution)/shard_map/ppermute | solution.py:115
  15.6 0.2 collective-permute-start.1
  15.8 0.2 collective-permute-start.2
  16.0 1.1 collective-permute-start.3
  17.1 0.7 fusion.90
  17.8 0.7 fusion.80
  18.5 1.5 fusion.15
  20.0 0.7 fusion.73
  20.7 1.6 reduce_window_sum.11
  22.4 1.0 select_reduce_fusion.1
  23.4 4.6 %fusion = bf16[64,8,4096]{2,1,0:T(8,128)(2,1)} fusion(bf16[1,128,4096]{2,1,0:T(8,128)(2,1)} %param.11, f32[128]{0:T(128)S(1)} %add_rsqrt_fusion.3, s32[128]{0:T(128)S(1)} %add_select_fusion.1, s32[512]{0:T(512)S(1)} %fusion.82), kind=kOutput, calls=%fused_computation.2 | convolution fusion | flops 540606464 | bytes 5245952 | tf_op jit(solution)/shard_map/dot_general | solution.py:87
  28.1 2.0 collective-permute-done.2
  30.0 0.9 bitcast_dynamic-update-slice_fusion.2
  31.0 2.2 collective-permute-done.3
  33.2 0.9 bitcast_dynamic-update-slice_fusion
  34.2 0.9 bitcast_dynamic-update-slice_fusion.3
  35.2 0.9 bitcast_dynamic-update-slice_fusion.1
  36.1 0.9 constant_dynamic-slice_fusion
  37.0 0.0 all-gather.2.cloned.1.call-update
  37.1 106.0 %all_to_all.10 = bf16[64,8,4096]{2,1,0:T(8,128)(2,1)S(1)} all-to-all(bf16[64,8,4096]{2,1,0:T(8,128)(2,1)} %fusion), channel_id=1, replica_groups=mesh['section'=4,'ep_y'=4,'ep_x'=4,'ep_z'=4] {'ep_y','ep_x','ep_z'}, dimensions={0} | all-to-all | bytes 8388608 | tf_op jit(solution)/shard_map/all_to_all | solution.py:120
  143.1 2.0 copy-done.3
  145.1 3.2 %fusion.6 = f32[512,384]{1,0:T(8,128)} fusion(bf16[64,8,4096]{2,1,0:T(8,128)(2,1)S(1)} %all_to_all.10, bf16[1,1,4096,384]{3,2,1,0:T(8,128)(2,1)S(1)} %copy-done.10), kind=kOutput, calls=%fused_computation.9 | convolution fusion | flops 1610612736 | bytes 8126464 | tf_op jit(solution)/shard_map/dot_general | solution.py:46
  148.3 9.9 %convolution_convert_fusion.1 = bf16[64,8,4096]{2,1,0:T(8,128)(2,1)} fusion(bf16[1,1,384,4096]{3,2,1,0:T(8,128)(2,1)S(1)} %copy-done, bf16[1,1,4096,384]{3,2,1,0:T(8,128)(2,1)} %param.15, bf16[64,8,4096]{2,1,0:T(8,128)(2,1)} %copy-done.3, f32[512,384]{1,0:T(8,128)} %fusion.6), kind=kOutput, calls=%fused_computation.1 | convolution fusion | flops 3224502272 | bytes 15466496 | tf_op jit(solution)/shard_map/dot_general | solution.py:49
  158.2 6.5 %all-to-all-start.1 = ((bf16[64,8,4096]{2,1,0:T(8,128)(2,1)}), bf16[64,8,4096]{2,1,0:T(8,128)(2,1)}, u32[]{:S(2)}, u32[]{:S(2)}) async-start(bf16[64,8,4096]{2,1,0:T(8,128)(2,1)} %convolution_convert_fusion.1), calls=%async_computation.1 | async-start | bytes 8388608 | tf_op jit(solution)/shard_map/all_to_all | solution.py:124
  164.7 1.8 collective-permute-start.4
  166.5 0.1 collective-permute-start.6
  166.6 1.7 collective-permute-start.5
  168.3 0.5 iota_add_fusion.1
  168.9 90.5 %all-to-all-done.1 = bf16[64,8,4096]{2,1,0:T(8,128)(2,1)} async-done(((bf16[64,8,4096]{2,1,0:T(8,128)(2,1)}), bf16[64,8,4096]{2,1,0:T(8,128)(2,1)}, u32[]{:S(2)}, u32[]{:S(2)}) %all-to-all-start.1) | async-done | bytes 4194336 | tf_op jit(solution)/shard_map/all_to_all | solution.py:124
  259.4 4.5 %fusion.13 = (f32[128]{0:T(128)S(1)}, bf16[128,4096]{1,0:T(8,128)(2,1)}) fusion(bf16[64,8,4096]{2,1,0:T(8,128)(2,1)} %all-to-all-done.1, s32[128]{0:T(128)S(1)} %add_select_fusion.1, s32[512]{0:T(512)S(1)} %fusion.82, f32[128]{0:T(128)S(1)} %fusion.79, bf16[1,128,4096]{2,1,0:T(8,128)(2,1)} %param.11), kind=kOutput, calls=%fused_computation.22 | convolution fusion | flops 540606336 | bytes 6295040 | tf_op jit(solution)/shard_map/dot_general | solution.py:127
  263.9 6.5 %fusion.44 = f32[128,1408]{1,0:T(8,128)S(1)} fusion(bf16[4096,1408]{1,0:T(8,128)(2,1)} %all-gather.2.cloned.1.call-done, bf16[128,4096]{1,0:T(8,128)(2,1)} %get-tuple-element.16, f32[128]{0:T(128)S(1)} %add_rsqrt_fusion.2), kind=kOutput, calls=%fused_computation.35 | convolution fusion | flops 1477967872 | bytes 13304320 | tf_op jit(solution)/shard_map/dot_general | solution.py:135
  270.4 0.1 multiply_reduce_fusion.1
  270.5 3.0 slice_convert_fusion
  273.5 0.1 fusion.74
  273.6 0.1 fusion.69
  273.7 2.7 reshape.193
  276.5 0.8 select_reduce_fusion
  277.3 0.3 multiply_cosine_fusion
  277.7 1.0 fusion.71
  278.7 2.0 collective-permute-start.7
  280.7 3.3 %collective-permute-start.8 = (bf16[128,256]{1,0:T(8,128)(2,1)S(1)}, bf16[128,256]{1,0:T(8,128)(2,1)}, u32[]{:S(2)}, u32[]{:S(2)}) collective-permute-start(bf16[128,256]{1,0:T(8,128)(2,1)S(1)} %pad_maximum_fusion.2), channel_id=1, source_target_pairs={{0,3},{1,4},{2,5},{3,6},{4,7},{5,8},{6,9},{7,10},{8,11},{9,12},{10... | collective-permute-start | bytes 196616 | tf_op jit(solution)/shard_map/ppermute | solution.py:28
  284.0 1.9 collective-permute-start.9
  285.9 3.5 %collective-permute-start.10 = (bf16[128,256]{1,0:T(8,128)(2,1)S(1)}, bf16[128,256]{1,0:T(8,128)(2,1)S(1)}, u32[]{:S(2)}, u32[]{:S(2)}) collective-permute-start(bf16[128,256]{1,0:T(8,128)(2,1)S(1)} %pad_maximum_fusion.2), channel_id=1, source_target_pairs={{0,1},{1,2},{2,3},{3,4},{4,5},{5,6},{6,7},{7,8},{8,9},{9,10},{10,1... | collective-permute-start | bytes 196616 | tf_op jit(solution)/shard_map/ppermute | solution.py:28
  289.5 1.1 slice_bitcast_fusion
  290.5 0.1 copy.32
  290.7 0.8 copy-done.1
  291.4 0.2 multiply_reduce_fusion
  291.7 0.1 copy.26
  291.9 1.3 multiply_multiply_fusion
  293.2 0.2 slice_negate_fusion
  293.4 0.3 fusion.57
  293.8 0.1 compare_and_fusion
  293.9 0.8 constant_dynamic-update-slice_fusion.4
  294.8 0.8 constant_dynamic-update-slice_fusion.3
  295.6 0.8 constant_dynamic-update-slice_fusion.2
  296.5 0.8 fusion.11
  297.3 0.6 fusion.35
  297.9 0.9 copy.29
  298.8 10.0 %collective-permute-done.11 = bf16[128,1024]{1,0:T(8,128)(2,1)S(1)} collective-permute-done((bf16[128,1024]{1,0:T(8,128)(2,1)}, bf16[128,1024]{1,0:T(8,128)(2,1)S(1)}, u32[]{:S(2)}, u32[]{:S(2)}) %collective-permute-start.11) | collective-permute-done | bytes 262176 | tf_op jit(solution)/shard_map/ppermute | solution.py:22
  308.8 0.7 copy.49
  (54 shorter events, 0.3 us)
Async XLA Ops:
  7.2 141.1 %copy-start = (bf16[1,1,384,4096]{3,2,1,0:T(8,128)(2,1)S(1)}, bf16[1,1,384,4096]{3,2,1,0:T(8,128)(2,1)}, u32[]{:S(2)}) copy-start(bf16[1,1,384,4096]{3,2,1,0:T(8,128)(2,1)} %param.16) | copy-start | bytes 9437188
  7.2 256.8 %all-gather.2.cloned.1.call-start = ((), (), s32[]{:S(2)}) async-start(), calls=%async_computation.2 | async-start | bytes 12255232 | tf_op jit(solution)/shard_map/all_gather | solution.py:119
  9.8 18.2 %collective-permute-start = (bf16[64,1408]{1,0:T(8,128)(2,1)}, bf16[64,1408]{1,0:T(8,128)(2,1)S(1)}, u32[]{:S(2)}, u32[]{:S(2)}) collective-permute-start(bf16[64,1408]{1,0:T(8,128)(2,1)} %fusion.64), channel_id=1, source_target_pairs={{64,0},{65,1},{66,2},{67,3},{128,64},{129,65},{130,66},{131,67},{1... | collective-permute-start | bytes 540680 | tf_op jit(solution)/shard_map/ppermute | solution.py:115
  15.6 12.5 %collective-permute-start.1 = (bf16[64,1408]{1,0:T(8,128)(2,1)}, bf16[64,1408]{1,0:T(8,128)(2,1)S(1)}, u32[]{:S(2)}, u32[]{:S(2)}) collective-permute-start(bf16[64,1408]{1,0:T(8,128)(2,1)} %fusion.64), channel_id=1, source_target_pairs={{65,0},{66,1},{67,2},{64,3},{129,64},{130,65},{131,66},{128,67},{1... | collective-permute-start | bytes 540680 | tf_op jit(solution)/shard_map/ppermute | solution.py:115
  15.8 14.3 %collective-permute-start.2 = (bf16[64,1408]{1,0:T(8,128)(2,1)}, bf16[64,1408]{1,0:T(8,128)(2,1)}, u32[]{:S(2)}, u32[]{:S(2)}) collective-permute-start(bf16[64,1408]{1,0:T(8,128)(2,1)} %fusion.64), channel_id=1, source_target_pairs={{66,0},{67,1},{64,2},{65,3},{130,64},{131,65},{128,66},{129,67},{1... | collective-permute-start | bytes 540680 | tf_op jit(solution)/shard_map/ppermute | solution.py:115
  16.0 17.3 %collective-permute-start.3 = (bf16[64,1408]{1,0:T(8,128)(2,1)}, bf16[64,1408]{1,0:T(8,128)(2,1)}, u32[]{:S(2)}, u32[]{:S(2)}) collective-permute-start(bf16[64,1408]{1,0:T(8,128)(2,1)} %fusion.64), channel_id=1, source_target_pairs={{67,0},{64,1},{65,2},{66,3},{131,64},{128,65},{129,66},{130,67},{1... | collective-permute-start | bytes 540680 | tf_op jit(solution)/shard_map/ppermute | solution.py:115
  37.1 108.0 %copy-start.10 = (bf16[1,1,4096,384]{3,2,1,0:T(8,128)(2,1)S(1)}, bf16[1,1,4096,384]{3,2,1,0:T(8,128)(2,1)}, u32[]{:S(2)}) copy-start(bf16[1,1,4096,384]{3,2,1,0:T(8,128)(2,1)} %param.14) | copy-start | bytes 9437188
  143.1 2.0 copy-start.3
  158.1 6.5 %copy-start.12 = (s32[1,128]{1,0:T(1,128)S(1)}, s32[1,128]{1,0:T(1,128)}, u32[]{:S(2)}) copy-start(s32[1,128]{1,0:T(1,128)} %param.21) | copy-start | bytes 1540
  158.1 8.3 %copy-start.11 = (f32[1,128]{1,0:T(1,128)S(1)}, f32[1,128]{1,0:T(1,128)}, u32[]{:S(2)}) copy-start(f32[1,128]{1,0:T(1,128)} %param.20) | copy-start | bytes 1540
  158.1 10.7 %copy-start.5 = (s32[1,128,8]{1,2,0:T(8,128)S(1)}, s32[1,128,8]{1,2,0:T(8,128)}, u32[]{:S(2)}) copy-start(s32[1,128,8]{1,2,0:T(8,128)} %param.12) | copy-start | bytes 12292
  158.1 10.7 %copy-start.6 = (f32[1,128,8]{1,2,0:T(8,128)S(1)}, f32[1,128,8]{1,2,0:T(8,128)}, u32[]{:S(2)}) copy-start(f32[1,128,8]{1,2,0:T(8,128)} %param.13) | copy-start | bytes 12292
  158.2 101.3 %all-to-all-start.1 = ((bf16[64,8,4096]{2,1,0:T(8,128)(2,1)}), bf16[64,8,4096]{2,1,0:T(8,128)(2,1)}, u32[]{:S(2)}, u32[]{:S(2)}) async-start(bf16[64,8,4096]{2,1,0:T(8,128)(2,1)} %convolution_convert_fusion.1), calls=%async_computation.1 | async-start | bytes 8388608 | tf_op jit(solution)/shard_map/all_to_all | solution.py:124
  164.7 111.8 %collective-permute-start.4 = (s32[128]{0:T(128)S(1)}, s32[128]{0:T(128)S(1)}, u32[]{:S(2)}, u32[]{:S(2)}) collective-permute-start(s32[128]{0:T(128)S(1)} %bitcast.116), channel_id=1, source_target_pairs={{64,0},{128,64},{192,128},{0,192},{65,1},{129,65},{193,129},{1,193... | collective-permute-start | bytes 1544 | tf_op jit(solution)/shard_map/ppermute | solution.py:22
  166.5 107.1 %collective-permute-start.6 = (f32[128]{0:T(128)S(1)}, f32[128]{0:T(128)S(1)}, u32[]{:S(2)}, u32[]{:S(2)}) collective-permute-start(f32[128]{0:T(128)S(1)} %bitcast.115), channel_id=1, source_target_pairs={{64,0},{128,64},{192,128},{0,192},{65,1},{129,65},{193,129},{1,193... | collective-permute-start | bytes 1544 | tf_op jit(solution)/shard_map/ppermute | solution.py:22
  166.6 125.3 %collective-permute-start.5 = (f32[128]{0:T(128)}, f32[128]{0:T(128)S(1)}, u32[]{:S(2)}, u32[]{:S(2)}) collective-permute-start(f32[128]{0:T(128)} %bitcast.21), channel_id=1, source_target_pairs={{64,0},{128,64},{192,128},{0,192},{65,1},{129,65},{193,129},{1,193... | collective-permute-start | bytes 1544 | tf_op jit(solution)/shard_map/ppermute | solution.py:22
  270.4 3.3 %copy-start.4 = (f32[128,1408]{1,0:T(8,128)}, f32[128,1408]{1,0:T(8,128)S(1)}, u32[]{:S(2)}) copy-start(f32[128,1408]{1,0:T(8,128)S(1)} %fusion.44) | copy-start | bytes 2162692
  277.3 13.3 %copy-start.7 = (s32[128]{0:T(128)}, s32[128]{0:T(128)S(1)}, u32[]{:S(2)}) copy-start(s32[128]{0:T(128)S(1)} %select_reduce_fusion) | copy-start | bytes 1540
  278.7 15.2 %collective-permute-start.7 = (bf16[128,256]{1,0:T(8,128)(2,1)S(1)}, bf16[128,256]{1,0:T(8,128)(2,1)}, u32[]{:S(2)}, u32[]{:S(2)}) collective-permute-start(bf16[128,256]{1,0:T(8,128)(2,1)S(1)} %pad_maximum_fusion.2), channel_id=1, source_target_pairs={{0,4},{1,5},{2,6},{3,7},{4,8},{5,9},{6,10},{7,11},{8,12},{9,13},{1... | collective-permute-start | bytes 196616 | tf_op jit(solution)/shard_map/ppermute | solution.py:28
  280.7 14.1 %collective-permute-start.8 = (bf16[128,256]{1,0:T(8,128)(2,1)S(1)}, bf16[128,256]{1,0:T(8,128)(2,1)}, u32[]{:S(2)}, u32[]{:S(2)}) collective-permute-start(bf16[128,256]{1,0:T(8,128)(2,1)S(1)} %pad_maximum_fusion.2), channel_id=1, source_target_pairs={{0,3},{1,4},{2,5},{3,6},{4,7},{5,8},{6,9},{7,10},{8,11},{9,12},{10... | collective-permute-start | bytes 196616 | tf_op jit(solution)/shard_map/ppermute | solution.py:28
  284.0 11.6 %collective-permute-start.9 = (bf16[128,256]{1,0:T(8,128)(2,1)S(1)}, bf16[128,256]{1,0:T(8,128)(2,1)}, u32[]{:S(2)}, u32[]{:S(2)}) collective-permute-start(bf16[128,256]{1,0:T(8,128)(2,1)S(1)} %pad_maximum_fusion.2), channel_id=1, source_target_pairs={{0,2},{1,3},{2,4},{3,5},{4,6},{5,7},{6,8},{7,9},{8,10},{9,11},{10,... | collective-permute-start | bytes 196616 | tf_op jit(solution)/shard_map/ppermute | solution.py:28
  285.9 10.5 %collective-permute-start.10 = (bf16[128,256]{1,0:T(8,128)(2,1)S(1)}, bf16[128,256]{1,0:T(8,128)(2,1)S(1)}, u32[]{:S(2)}, u32[]{:S(2)}) collective-permute-start(bf16[128,256]{1,0:T(8,128)(2,1)S(1)} %pad_maximum_fusion.2), channel_id=1, source_target_pairs={{0,1},{1,2},{2,3},{3,4},{4,5},{5,6},{6,7},{7,8},{8,9},{9,10},{10,1... | collective-permute-start | bytes 196616 | tf_op jit(solution)/shard_map/ppermute | solution.py:28
  290.6 0.8 copy-start.1
  291.8 1.5 copy-start.2
  291.8 1.9 copy-start.8
  291.8 1.9 copy-start.9
  298.8 10.0 %collective-permute-start.11 = (bf16[128,1024]{1,0:T(8,128)(2,1)}, bf16[128,1024]{1,0:T(8,128)(2,1)S(1)}, u32[]{:S(2)}, u32[]{:S(2)}) collective-permute-start(bf16[128,1024]{1,0:T(8,128)(2,1)} %copy.29), channel_id=1, source_target_pairs={{192,0},{0,64},{64,128},{128,192},{193,1},{1,65},{65,129},{129,193... | collective-permute-start | bytes 786440 | tf_op jit(solution)/shard_map/ppermute | solution.py:22
Sparse Core Ops, SparseCore 0:
  37.2 128.6 all-gather.1

commit v10 on v9

--- a/solution.py
+++ b/solution.py
@@ -91,33 +91,23 @@
     gate_part = w_gate[0, 0]
     up_part = w_up[0, 0]
     down_part = w_down[0, 0]
-    segment_row, next_gain_query, next_gain_key = passed_along(
-        (segment_ids[0], gain_query[0], gain_key[0]), "section", -1
+    next_query, next_keyval, segment_row, next_gain_query, next_gain_key = passed_along(
+        (w_query[0], w_keyval[0], segment_ids[0], gain_query[0], gain_key[0]), "section", -1
     )
     first_index = lax.axis_index(EP) * token_count
     reach = (SEG_MOST - 1) // token_count + 1
-    shard_rows = w_query.shape[1]
+    shard_rows = next_query.shape[0]
     per_row = -(-token_count // shard_rows)
-    carried = jnp.pad(segment_ids[0], (0, shard_rows * per_row - token_count)).reshape(
+    carried = jnp.pad(segment_row, (0, shard_rows * per_row - token_count)).reshape(
         shard_rows, per_row
     )
     carried = jnp.pad(carried.astype(jnp.bfloat16), ((0, 0), (0, 128 - per_row)))
-    own_shard = jnp.concatenate([w_query[0], w_keyval[0], carried], axis=-1)
-    section_count = lax.axis_size("section")
-    owner_count = lax.axis_size(EP[-1])
-    pieces = []
-    for shift in range(owner_count):
-        route = [
-            (((s + 1) % section_count) * owner_count + (z + shift) % owner_count, s * owner_count + z)
-            for s in range(section_count)
-            for z in range(owner_count)
-        ]
-        pieces.append(lax.ppermute(own_shard, ("section", EP[-1]), route))
-    projection = jnp.roll(jnp.stack(pieces), lax.axis_index(EP[-1]), axis=0)
-    projection = projection.reshape(-1, own_shard.shape[-1])
+    projection = jnp.concatenate([next_query, next_keyval, carried], axis=-1)
+    projection = lax.all_gather(projection, EP[-1], axis=0, tiled=True)
     spread, projection = lax.optimization_barrier((spread, projection))
+    received = lax.all_to_all(spread, EP, split_axis=0, concat_axis=0, tiled=True)
+    received, projection = lax.optimization_barrier((received, projection))
     projection = lax.all_gather(projection, EP[:-1], axis=0, tiled=True)
-    received = lax.all_to_all(spread, EP, split_axis=0, concat_axis=0, tiled=True)
     partial_out = feed_forward(
         received.reshape(-1, model_width), gate_part, up_part, down_part
     ).reshape(received.shape)

time: 322 us -> 337 us (1.047)
  blocking collectives: 106 us -> 122 us
  waiting for transfers between devices: 105 us -> 115 us
  local copies, waits for them, and re-layouts: 15.9 us -> 9.13 us
  other arithmetic: 16.9 us -> 13.1 us
  matrix products: 30.1 us -> 33.5 us
    all_gather x0 -> x1, blocking collectives: none -> 17.7 us  [on_device(): projection = lax.all_gather(projection, EP[-1], axis=0, tiled=True)]
    all_gather x1, waiting for transfers between devices: 0.01 us -> 11.5 us  [on_device(): projection = lax.all_gather(projection, EP[:-1], axis=0, tiled=True)]
    ppermute x4 -> x0, starting transfers between devices: 7.24 us -> none  [on_device(): pieces.append(lax.ppermute(own_shard, ('section', EP[-1]), route))]
    unnamed x40 -> x25, local copies, waits for them, and re-layouts: 10.1 us -> 5.23 us
    ppermute x4 -> x0, waiting for transfers between devices: 4.21 us -> none  [on_device(): pieces.append(lax.ppermute(own_shard, ('section', EP[-1]), route))]
    ppermute x4 -> x6, starting transfers between devices: 3.61 us -> 7.17 us  [passed_along(): return lax.ppermute(block, axis, route)]
    ppermute x4 -> x6, waiting for transfers between devices: 10 us -> 10 us  [passed_along(): return lax.ppermute(block, axis, route)]
  transfers between devices with their start and end apart: 14 -> 12, of which waited for: 4 -> 3; matrix products, arithmetic and copies ran while one was open for 16% -> 16% of each run, Pallas kernels for 0% -> 0%
where the time goes in v10:
time: 337 us; the launch traced here: 333 us
  blocking collectives  122 us (36%)
  waiting for transfers between devices  115 us (34%)
  matrix products  33.5 us (10%)
  starting transfers between devices  26 us (8%)
  between operations  14.3 us (4%)
  other arithmetic  13.1 us (4%)
  local copies, waits for them, and re-layouts  9.13 us (3%)
    all_to_all x1, blocking collectives, on_device(): lax.all_to_all(spread, EP, split_axis=0, concat_axis=0, tiled=True)  104 us
    all_to_all x1, waiting for transfers between devices, on_device(): lax.all_to_all(partial_out.astype(jnp.bfloat16), EP, split_axis=0, concat...  93.6 us
    all_gather x1, blocking collectives, on_device(): projection = lax.all_gather(projection, EP[-1], axis=0, tiled=True)  17.7 us
    ppermute x4, starting transfers between devices, passed_along_2(): lax.ppermute(value, axis, [(source, source + steps) for source in range(l...  12.5 us
    all_gather x1, waiting for transfers between devices, on_device(): projection = lax.all_gather(projection, EP[:-1], axis=0, tiled=True)  11.5 us
    dot_general x1, matrix products, feed_forward(): return jnp.dot(activated, down_part, preferred_element_type=jnp.float32)  10.1 us
    ppermute x6, waiting for transfers between devices, passed_along(): return lax.ppermute(block, axis, route)  10 us
    ppermute x6, starting transfers between devices, passed_along(): return lax.ppermute(block, axis, route)  7.17 us
  transfers between devices with their start and end apart: 12, of which 3 were waited for; matrix products, arithmetic and copies ran while one was open for 16% of the time, Pallas kernels for 0%

profile of v10, /device:TPU:32, one launch (start us, length us, event | category | flops | bytes accessed | tf_op | source)
XLA Modules:
  0.0 333.1 jit_solution(5371644204692236944)
XLA Ops:
  7.2 0.0 copy-start
  7.2 0.0 all-gather.2.cloned.1.call-start
  7.2 5.8 %collective-permute-start.2 = (s32[128]{0:T(128)}, s32[128]{0:T(128)S(1)}, u32[]{:S(2)}, u32[]{:S(2)}) collective-permute-start(s32[128]{0:T(128)} %bitcast.101), channel_id=1, source_target_pairs={{64,0},{128,64},{192,128},{0,192},{65,1},{129,65},{193,129},{1,193... | collective-permute-start | bytes 1544 | tf_op jit(solution)/shard_map/ppermute | solution.py:22
  13.0 0.7 collective-permute-start.1
  13.7 0.1 collective-permute-start
  13.8 0.7 fusion.90
  14.5 0.7 fusion.80
  15.2 1.5 fusion.15
  16.7 0.1 fusion.73
  16.8 0.2 reduce_window_sum.11
  17.0 0.2 select_reduce_fusion.1
  17.2 4.5 %fusion = bf16[64,8,4096]{2,1,0:T(8,128)(2,1)} fusion(bf16[1,128,4096]{2,1,0:T(8,128)(2,1)} %param.11, f32[128]{0:T(128)S(1)} %add_rsqrt_fusion.3, s32[128]{0:T(128)S(1)} %add_select_fusion.1, s32[512]{0:T(512)S(1)} %fusion.82), kind=kOutput, calls=%fused_computation.2 | convolution fusion | flops 540606464 | bytes 5245952 | tf_op jit(solution)/shard_map/dot_general | solution.py:87
  21.7 0.0 collective-permute-done.2
  21.7 0.1 convert_element_type.67
  21.9 0.0 collective-permute-done.1
  21.9 0.0 collective-permute-done
  21.9 17.7 %all_gather.6 = bf16[256,1408]{1,0:T(8,128)(2,1)} all-gather(bf16[64,1408]{1,0:T(8,128)(2,1)S(1)} %fusion.64), channel_id=1, replica_groups=mesh['section'=4,'ep_y'=4,'ep_x'=4,'ep_z'=4] {'ep_z'}, dimensions={0}, use_global_device_ids=true | all-gather | bytes 901120 | tf_op jit(solution)/shard_map/all_gather | solution.py:106
  39.6 104.2 %all_to_all.10 = bf16[64,8,4096]{2,1,0:T(8,128)(2,1)} all-to-all(bf16[64,8,4096]{2,1,0:T(8,128)(2,1)} %fusion), channel_id=1, replica_groups=mesh['section'=4,'ep_y'=4,'ep_x'=4,'ep_z'=4] {'ep_y','ep_x','ep_z'}, dimensions={0} | all-to-all | bytes 8388608 | tf_op jit(solution)/shard_map/all_to_all | solution.py:108
  143.8 0.0 all-gather.2.cloned.1.call-update
  143.8 6.4 %fusion.6 = f32[512,384]{1,0:T(8,128)} fusion(bf16[64,8,4096]{2,1,0:T(8,128)(2,1)} %all_to_all.10, bf16[1,1,4096,384]{3,2,1,0:T(8,128)(2,1)} %param.14), kind=kOutput, calls=%fused_computation.9 | convolution fusion | flops 1610612736 | bytes 8126464 | tf_op jit(solution)/shard_map/dot_general | solution.py:46
  150.2 10.1 %convolution_convert_fusion.1 = bf16[64,8,4096]{2,1,0:T(8,128)(2,1)} fusion(bf16[1,1,384,4096]{3,2,1,0:T(8,128)(2,1)S(1)} %copy-done, bf16[1,1,4096,384]{3,2,1,0:T(8,128)(2,1)} %param.15, bf16[64,8,4096]{2,1,0:T(8,128)(2,1)} %all_to_all.10, f32[512,384]{1,0:T(8,128)} %fusion.6), kind=kOutput, calls=%fused_computation.1 | convolution fusion | flops 3224502272 | bytes 15466496 | tf_op jit(solution)/shard_map/dot_general | solution.py:49
  160.3 6.2 %all-to-all-start.1 = ((bf16[64,8,4096]{2,1,0:T(8,128)(2,1)}), bf16[64,8,4096]{2,1,0:T(8,128)(2,1)}, u32[]{:S(2)}, u32[]{:S(2)}) async-start(bf16[64,8,4096]{2,1,0:T(8,128)(2,1)} %convolution_convert_fusion.1), calls=%async_computation.1 | async-start | bytes 8388608 | tf_op jit(solution)/shard_map/all_to_all | solution.py:114
  166.6 0.1 collective-permute-start.4
  166.7 0.5 collective-permute-start.3
  167.2 0.5 iota_add_fusion.1
  167.8 93.6 %all-to-all-done.1 = bf16[64,8,4096]{2,1,0:T(8,128)(2,1)} async-done(((bf16[64,8,4096]{2,1,0:T(8,128)(2,1)}), bf16[64,8,4096]{2,1,0:T(8,128)(2,1)}, u32[]{:S(2)}, u32[]{:S(2)}) %all-to-all-start.1) | async-done | bytes 4194336 | tf_op jit(solution)/shard_map/all_to_all | solution.py:114
  261.3 4.6 %fusion.13 = (f32[128]{0:T(128)S(1)}, bf16[128,4096]{1,0:T(8,128)(2,1)}) fusion(bf16[64,8,4096]{2,1,0:T(8,128)(2,1)} %all-to-all-done.1, s32[128]{0:T(128)S(1)} %add_select_fusion.1, s32[512]{0:T(512)S(1)} %fusion.82, f32[128]{0:T(128)S(1)} %fusion.79, bf16[1,128,4096]{2,1,0:T(8,128)(2,1)} %param.11), kind=kOutput, calls=%fused_computation.22 | convolution fusion | flops 540606336 | bytes 6295040 | tf_op jit(solution)/shard_map/dot_general | solution.py:117
  266.0 11.5 %all-gather.2.cloned.1.call-done = bf16[4096,1408]{1,0:T(8,128)(2,1)} async-done(((bf16[256,1408]{1,0:T(8,128)(2,1)}), bf16[4096,1408]{1,0:T(8,128)(2,1)}) %all-gather.2.cloned.1.call-update) | async-done | bytes 11534352 | tf_op jit(solution)/shard_map/all_gather | solution.py:110
  277.5 6.5 %fusion.44 = f32[128,1408]{1,0:T(8,128)S(1)} fusion(bf16[4096,1408]{1,0:T(8,128)(2,1)} %all-gather.2.cloned.1.call-done, bf16[128,4096]{1,0:T(8,128)(2,1)} %get-tuple-element.20, f32[128]{0:T(128)S(1)} %add_rsqrt_fusion.2), kind=kOutput, calls=%fused_computation.35 | convolution fusion | flops 1477967872 | bytes 13304320 | tf_op jit(solution)/shard_map/dot_general | solution.py:125
  283.9 0.1 multiply_reduce_fusion.1
  284.0 3.0 slice_convert_fusion
  287.1 2.7 reshape.188
  289.8 0.0 collective-permute-done.4
  289.8 0.9 fusion.74
  290.7 0.1 fusion.69
  290.8 0.9 select_reduce_fusion
  291.7 0.3 multiply_cosine_fusion
  292.0 1.0 fusion.71
  293.0 1.9 collective-permute-start.5
  294.9 1.9 collective-permute-start.6
  296.8 6.8 %collective-permute-start.7 = (bf16[128,256]{1,0:T(8,128)(2,1)S(1)}, bf16[128,256]{1,0:T(8,128)(2,1)}, u32[]{:S(2)}, u32[]{:S(2)}) collective-permute-start(bf16[128,256]{1,0:T(8,128)(2,1)S(1)} %pad_maximum_fusion.2), channel_id=1, source_target_pairs={{0,2},{1,3},{2,4},{3,5},{4,6},{5,7},{6,8},{7,9},{8,10},{9,11},{10,... | collective-permute-start | bytes 196616 | tf_op jit(solution)/shard_map/ppermute | solution.py:28
  303.6 1.9 collective-permute-start.8
  305.5 1.1 slice_bitcast_fusion
  306.6 0.1 copy.32
  306.8 0.8 copy-done.1
  307.5 0.2 multiply_reduce_fusion
  307.8 0.1 copy.26
  307.9 0.0 collective-permute-done.3
  307.9 1.3 multiply_multiply_fusion
  309.2 0.2 slice_negate_fusion
  309.5 0.3 fusion.57
  309.8 0.8 compare_and_fusion
  310.6 0.0 collective-permute-done.5
  310.6 0.8 constant_dynamic-update-slice_fusion.4
  311.5 0.0 collective-permute-done.6
  311.5 0.8 constant_dynamic-update-slice_fusion.3
  312.3 0.0 collective-permute-done.7
  312.3 0.8 constant_dynamic-update-slice_fusion.2
  313.2 0.8 fusion.11
  314.0 0.6 fusion.35
  314.6 0.9 copy.29
  315.5 0.0 collective-permute-start.9
  315.5 10.0 %collective-permute-done.9 = bf16[128,1024]{1,0:T(8,128)(2,1)S(1)} collective-permute-done((bf16[128,1024]{1,0:T(8,128)(2,1)}, bf16[128,1024]{1,0:T(8,128)(2,1)S(1)}, u32[]{:S(2)}, u32[]{:S(2)}) %collective-permute-start.9) | collective-permute-done | bytes 262176 | tf_op jit(solution)/shard_map/ppermute | solution.py:22
  325.5 0.7 copy.42
  (34 shorter events, 0.2 us)
Async XLA Ops:
  7.2 143.0 %copy-start = (bf16[1,1,384,4096]{3,2,1,0:T(8,128)(2,1)S(1)}, bf16[1,1,384,4096]{3,2,1,0:T(8,128)(2,1)}, u32[]{:S(2)}) copy-start(bf16[1,1,384,4096]{3,2,1,0:T(8,128)(2,1)} %param.16) | copy-start | bytes 9437188
  7.2 270.3 %all-gather.2.cloned.1.call-start = ((), (), s32[]{:S(2)}) async-start(), calls=%async_computation.2 | async-start | bytes 12255232 | tf_op jit(solution)/shard_map/all_gather | solution.py:110
  7.2 14.5 %collective-permute-start.2 = (s32[128]{0:T(128)}, s32[128]{0:T(128)S(1)}, u32[]{:S(2)}, u32[]{:S(2)}) collective-permute-start(s32[128]{0:T(128)} %bitcast.101), channel_id=1, source_target_pairs={{64,0},{128,64},{192,128},{0,192},{65,1},{129,65},{193,129},{1,193... | collective-permute-start | bytes 1544 | tf_op jit(solution)/shard_map/ppermute | solution.py:22
  13.0 8.8 %collective-permute-start.1 = (bf16[64,256]{1,0:T(8,128)(2,1)}, bf16[64,256]{1,0:T(8,128)(2,1)S(1)}, u32[]{:S(2)}, u32[]{:S(2)}) collective-permute-start(bf16[64,256]{1,0:T(8,128)(2,1)} %bitcast.100), channel_id=1, source_target_pairs={{64,0},{128,64},{192,128},{0,192},{65,1},{129,65},{193,129},{1,193... | collective-permute-start | bytes 98312 | tf_op jit(solution)/shard_map/ppermute | solution.py:22
  13.7 8.2 %collective-permute-start = (bf16[64,1024]{1,0:T(8,128)(2,1)}, bf16[64,1024]{1,0:T(8,128)(2,1)S(1)}, u32[]{:S(2)}, u32[]{:S(2)}) collective-permute-start(bf16[64,1024]{1,0:T(8,128)(2,1)} %bitcast.99), channel_id=1, source_target_pairs={{64,0},{128,64},{192,128},{0,192},{65,1},{129,65},{193,129},{1,193... | collective-permute-start | bytes 393224 | tf_op jit(solution)/shard_map/ppermute | solution.py:22
  160.3 6.2 %copy-start.8 = (f32[1,128]{1,0:T(1,128)S(1)}, f32[1,128]{1,0:T(1,128)}, u32[]{:S(2)}) copy-start(f32[1,128]{1,0:T(1,128)} %param.20) | copy-start | bytes 1540
  160.3 7.4 %copy-start.4 = (s32[1,128,8]{1,2,0:T(8,128)S(1)}, s32[1,128,8]{1,2,0:T(8,128)}, u32[]{:S(2)}) copy-start(s32[1,128,8]{1,2,0:T(8,128)} %param.12) | copy-start | bytes 12292
  160.3 7.4 %copy-start.5 = (f32[1,128,8]{1,2,0:T(8,128)S(1)}, f32[1,128,8]{1,2,0:T(8,128)}, u32[]{:S(2)}) copy-start(f32[1,128,8]{1,2,0:T(8,128)} %param.13) | copy-start | bytes 12292
  160.3 101.0 %all-to-all-start.1 = ((bf16[64,8,4096]{2,1,0:T(8,128)(2,1)}), bf16[64,8,4096]{2,1,0:T(8,128)(2,1)}, u32[]{:S(2)}, u32[]{:S(2)}) async-start(bf16[64,8,4096]{2,1,0:T(8,128)(2,1)} %convolution_convert_fusion.1), calls=%async_computation.1 | async-start | bytes 8388608 | tf_op jit(solution)/shard_map/all_to_all | solution.py:114
  166.6 123.2 %collective-permute-start.4 = (f32[128]{0:T(128)S(1)}, f32[128]{0:T(128)S(1)}, u32[]{:S(2)}, u32[]{:S(2)}) collective-permute-start(f32[128]{0:T(128)S(1)} %bitcast.102), channel_id=1, source_target_pairs={{64,0},{128,64},{192,128},{0,192},{65,1},{129,65},{193,129},{1,193... | collective-permute-start | bytes 1544 | tf_op jit(solution)/shard_map/ppermute | solution.py:22
  166.7 141.3 %collective-permute-start.3 = (f32[128]{0:T(128)}, f32[128]{0:T(128)S(1)}, u32[]{:S(2)}, u32[]{:S(2)}) collective-permute-start(f32[128]{0:T(128)} %bitcast.16), channel_id=1, source_target_pairs={{64,0},{128,64},{192,128},{0,192},{65,1},{129,65},{193,129},{1,193... | collective-permute-start | bytes 1544 | tf_op jit(solution)/shard_map/ppermute | solution.py:22
  283.9 3.1 copy-start.3
  291.7 15.1 %copy-start.6 = (s32[128]{0:T(128)}, s32[128]{0:T(128)S(1)}, u32[]{:S(2)}) copy-start(s32[128]{0:T(128)S(1)} %select_reduce_fusion) | copy-start | bytes 1540
  293.0 17.6 %collective-permute-start.5 = (bf16[128,256]{1,0:T(8,128)(2,1)S(1)}, bf16[128,256]{1,0:T(8,128)(2,1)}, u32[]{:S(2)}, u32[]{:S(2)}) collective-permute-start(bf16[128,256]{1,0:T(8,128)(2,1)S(1)} %pad_maximum_fusion.2), channel_id=1, source_target_pairs={{0,4},{1,5},{2,6},{3,7},{4,8},{5,9},{6,10},{7,11},{8,12},{9,13},{1... | collective-permute-start | bytes 196616 | tf_op jit(solution)/shard_map/ppermute | solution.py:28
  294.9 16.6 %collective-permute-start.6 = (bf16[128,256]{1,0:T(8,128)(2,1)S(1)}, bf16[128,256]{1,0:T(8,128)(2,1)}, u32[]{:S(2)}, u32[]{:S(2)}) collective-permute-start(bf16[128,256]{1,0:T(8,128)(2,1)S(1)} %pad_maximum_fusion.2), channel_id=1, source_target_pairs={{0,3},{1,4},{2,5},{3,6},{4,7},{5,8},{6,9},{7,10},{8,11},{9,12},{10... | collective-permute-start | bytes 196616 | tf_op jit(solution)/shard_map/ppermute | solution.py:28
  296.8 15.5 %collective-permute-start.7 = (bf16[128,256]{1,0:T(8,128)(2,1)S(1)}, bf16[128,256]{1,0:T(8,128)(2,1)}, u32[]{:S(2)}, u32[]{:S(2)}) collective-permute-start(bf16[128,256]{1,0:T(8,128)(2,1)S(1)} %pad_maximum_fusion.2), channel_id=1, source_target_pairs={{0,2},{1,3},{2,4},{3,5},{4,6},{5,7},{6,8},{7,9},{8,10},{9,11},{10,... | collective-permute-start | bytes 196616 | tf_op jit(solution)/shard_map/ppermute | solution.py:28
  303.6 9.5 %collective-permute-start.8 = (bf16[128,256]{1,0:T(8,128)(2,1)S(1)}, bf16[128,256]{1,0:T(8,128)(2,1)S(1)}, u32[]{:S(2)}, u32[]{:S(2)}) collective-permute-start(bf16[128,256]{1,0:T(8,128)(2,1)S(1)} %pad_maximum_fusion.2), channel_id=1, source_target_pairs={{0,1},{1,2},{2,3},{3,4},{4,5},{5,6},{6,7},{7,8},{8,9},{9,10},{10,1... | collective-permute-start | bytes 196616 | tf_op jit(solution)/shard_map/ppermute | solution.py:28
  306.7 0.8 copy-start.1
  307.8 2.0 copy-start.7
  307.9 1.5 copy-start.2
  315.5 10.0 %collective-permute-start.9 = (bf16[128,1024]{1,0:T(8,128)(2,1)}, bf16[128,1024]{1,0:T(8,128)(2,1)S(1)}, u32[]{:S(2)}, u32[]{:S(2)}) collective-permute-start(bf16[128,1024]{1,0:T(8,128)(2,1)} %copy.29), channel_id=1, source_target_pairs={{192,0},{0,64},{64,128},{128,192},{193,1},{1,65},{65,129},{129,193... | collective-permute-start | bytes 786440 | tf_op jit(solution)/shard_map/ppermute | solution.py:22
Sparse Core Ops, SparseCore 0:
  143.9 133.4 all-gather.1

commit v11 on v10

--- a/solution.py
+++ b/solution.py
@@ -105,18 +105,24 @@
     projection = jnp.concatenate([next_query, next_keyval, carried], axis=-1)
     projection = lax.all_gather(projection, EP[-1], axis=0, tiled=True)
     spread, projection = lax.optimization_barrier((spread, projection))
+    projection = lax.all_gather(projection, EP[:-1], axis=0, tiled=True)
     received = lax.all_to_all(spread, EP, split_axis=0, concat_axis=0, tiled=True)
-    received, projection = lax.optimization_barrier((received, projection))
-    projection = lax.all_gather(projection, EP[:-1], axis=0, tiled=True)
-    partial_out = feed_forward(
-        received.reshape(-1, model_width), gate_part, up_part, down_part
-    ).reshape(received.shape)
-    returned_rows = lax.all_to_all(
-        partial_out.astype(jnp.bfloat16), EP, split_axis=0, concat_axis=0, tiled=True
-    )
-    expert_out = jnp.dot(
-        placing.T, returned_rows.reshape(-1, model_width), preferred_element_type=jnp.float32
-    )
+    half = capacity // 2
+    placing_rows = placing.reshape(device_count, capacity, token_count)
+    expert_out = 0.0
+    for first, last in ((0, half), (half, capacity)):
+        block = received[:, first:last]
+        partial_out = feed_forward(
+            block.reshape(-1, model_width), gate_part, up_part, down_part
+        ).reshape(block.shape)
+        returned_rows = lax.all_to_all(
+            partial_out.astype(jnp.bfloat16), EP, split_axis=0, concat_axis=0, tiled=True
+        )
+        expert_out = expert_out + jnp.dot(
+            placing_rows[:, first:last].reshape(-1, token_count).T,
+            returned_rows.reshape(-1, model_width),
+            preferred_element_type=jnp.float32,
+        )
     layer_out = (wide_tokens + weight_kept[:, None] * expert_out).astype(jnp.bfloat16)
     lifted = rms_rows(layer_out.astype(jnp.float32)).astype(jnp.bfloat16)
     head_dim = gain_query.shape[-1]

time: 337 us -> 328 us (0.973)
  waiting for transfers between devices: 115 us -> 92.2 us
  local copies, waits for them, and re-layouts: 9.13 us -> 21.1 us
  other arithmetic: 13.1 us -> 7.6 us
  starting transfers between devices: 26 us -> 30.1 us
    all_to_all x1 -> x2, waiting for transfers between devices: 93.6 us -> 79.3 us  [on_device(): lax.all_to_all(partial_out.astype(jnp.bfloat16), EP, split_axis=0, concat...]
    all_gather x1, waiting for transfers between devices: 11.5 us -> 0.01 us  [on_device(): projection = lax.all_gather(projection, EP[:-1], axis=0, tiled=True)]
    dot_general x1 -> x4, matrix products: 4.64 us -> 13.3 us  [the longest x2 10.8 us: on_device(): jnp.dot(placing_rows[:, first:last].reshape(-1, token_count).T, returned_...]
    reshape x0 -> x2, local copies, waits for them, and re-layouts: none -> 7.94 us  [on_device(): block.reshape(-1, model_width)]
    dot_general x1 -> x2, matrix products: 10.1 us -> 2.51 us  [feed_forward(): return jnp.dot(activated, down_part, preferred_element_type=jnp.float32)]
    convert_element_type x0 -> x2, local copies, waits for them, and re-layouts: none -> 5.85 us  [on_device(): partial_out.astype(jnp.bfloat16)]
    all_to_all x1 -> x2, starting transfers between devices: 6.23 us -> 11.4 us  [on_device(): lax.all_to_all(partial_out.astype(jnp.bfloat16), EP, split_axis=0, concat...]
    unnamed x25 -> x29, local copies, waits for them, and re-layouts: 5.23 us -> 1.17 us
  transfers between devices with their start and end apart: 12 -> 13, of which waited for: 3 -> 4; matrix products, arithmetic and copies ran while one was open for 16% -> 19% of each run, Pallas kernels for 0% -> 0%
where the time goes in v11:
time: 328 us; the launch traced here: 324 us
  blocking collectives  122 us (37%)
  waiting for transfers between devices  92.2 us (28%)
  matrix products  36.4 us (11%)
  starting transfers between devices  30.1 us (9%)
  local copies, waits for them, and re-layouts  21.1 us (6%)
  between operations  14.5 us (4%)
  other arithmetic  7.6 us (2%)
    all_to_all x1, blocking collectives, on_device(): lax.all_to_all(spread, EP, split_axis=0, concat_axis=0, tiled=True)  104 us
    all_to_all x2, waiting for transfers between devices, on_device(): lax.all_to_all(partial_out.astype(jnp.bfloat16), EP, split_axis=0, concat...  79.3 us
    all_gather x1, blocking collectives, on_device(): projection = lax.all_gather(projection, EP[-1], axis=0, tiled=True)  17.6 us
    ppermute x6, waiting for transfers between devices, passed_along(): return lax.ppermute(block, axis, route)  12.7 us
    ppermute x4, starting transfers between devices, passed_along_2(): lax.ppermute(value, axis, [(source, source + steps) for source in range(l...  11.7 us
    all_to_all x2, starting transfers between devices, on_device(): lax.all_to_all(partial_out.astype(jnp.bfloat16), EP, split_axis=0, concat...  11.4 us
    dot_general x2, matrix products, on_device(): jnp.dot(placing_rows[:, first:last].reshape(-1, token_count).T, returned_...  10.8 us
    dot_general x2, matrix products, feed_forward(): jnp.dot(row_block, gate_part, preferred_element_type=jnp.float32)  8.12 us
  transfers between devices with their start and end apart: 13, of which 4 were waited for; matrix products, arithmetic and copies ran while one was open for 19% of the time, Pallas kernels for 0%

profile of v11, /device:TPU:32, one launch (start us, length us, event | category | flops | bytes accessed | tf_op | source)
XLA Modules:
  0.0 323.6 jit_solution(12953635887922499647)
XLA Ops:
  7.2 0.0 all-gather.2.cloned.1.call-start
  7.2 5.8 %collective-permute-start.2 = (s32[128]{0:T(128)}, s32[128]{0:T(128)S(1)}, u32[]{:S(2)}, u32[]{:S(2)}) collective-permute-start(s32[128]{0:T(128)} %bitcast.101), channel_id=1, source_target_pairs={{64,0},{128,64},{192,128},{0,192},{65,1},{129,65},{193,129},{1,193... | collective-permute-start | bytes 1544 | tf_op jit(solution)/shard_map/ppermute | solution.py:22
  13.0 0.7 collective-permute-start.1
  13.7 0.1 collective-permute-start
  13.8 0.7 fusion.96
  14.5 0.7 fusion.82
  15.2 1.5 fusion.19
  16.7 0.1 fusion.73
  16.8 0.2 reduce_window_sum.11
  17.0 0.2 select_reduce_fusion.1
  17.2 4.6 %fusion = bf16[64,8,4096]{2,1,0:T(8,128)(2,1)} fusion(bf16[1,128,4096]{2,1,0:T(8,128)(2,1)} %param.11, f32[128]{0:T(128)S(1)} %add_rsqrt_fusion.3, s32[128]{0:T(128)S(1)} %add_select_fusion.3, s32[512]{0:T(512)S(1)} %fusion.89), kind=kOutput, calls=%fused_computation.1 | convolution fusion | flops 540606464 | bytes 5245952 | tf_op jit(solution)/shard_map/dot_general | solution.py:87
  21.8 0.1 convert_element_type.73
  22.0 17.6 %all_gather.6 = bf16[256,1408]{1,0:T(8,128)(2,1)} all-gather(bf16[64,1408]{1,0:T(8,128)(2,1)S(1)} %fusion.62), channel_id=1, replica_groups=mesh['section'=4,'ep_y'=4,'ep_x'=4,'ep_z'=4] {'ep_z'}, dimensions={0}, use_global_device_ids=true | all-gather | bytes 901120 | tf_op jit(solution)/shard_map/all_gather | solution.py:106
  39.6 0.0 all-gather.2.cloned.1.call-update
  39.7 104.1 %all_to_all.15 = bf16[64,8,4096]{2,1,0:T(8,128)(2,1)S(1)} all-to-all(bf16[64,8,4096]{2,1,0:T(8,128)(2,1)} %fusion), channel_id=1, replica_groups=mesh['section'=4,'ep_y'=4,'ep_x'=4,'ep_z'=4] {'ep_y','ep_x','ep_z'}, dimensions={0} | all-to-all | bytes 8388608 | tf_op jit(solution)/shard_map/all_to_all | solution.py:109
  143.8 3.7 %fusion.97 = (bf16[64,4,4096]{2,1,0:T(4,128)(2,1)}, bf16[64,4,4096]{2,1,0:T(4,128)(2,1)}) fusion(bf16[64,8,4096]{2,1,0:T(8,128)(2,1)S(1)} %all_to_all.15), kind=kLoop, calls=%fused_computation.143 | loop fusion | bytes 8388608 | tf_op jit(solution)/shard_map/slice | solution.py:114
  147.5 4.0 %reshape.205 = bf16[256,4096]{1,0:T(8,128)(2,1)} reshape(bf16[64,4,4096]{2,1,0:T(4,128)(2,1)} %get-tuple-element.7) | data formatting | bytes 4194304 | tf_op jit(solution)/shard_map/reshape | solution.py:116
  151.4 4.2 %fusion.11 = f32[256,384]{1,0:T(8,128)S(1)} fusion(bf16[256,4096]{1,0:T(8,128)(2,1)} %reshape.205, bf16[1,1,4096,384]{3,2,1,0:T(8,128)(2,1)} %param.14), kind=kOutput, calls=%fused_computation.17 | convolution fusion | flops 805306368 | bytes 5636096 | tf_op jit(solution)/shard_map/dot_general | solution.py:46
  155.6 0.1 copy-done.7
  155.8 1.3 fusion.40
  157.0 0.1 dot_general.48
  157.1 1.3 convolution_convert_fusion.1
  158.4 2.9 copy.41
  161.3 6.0 %all-to-all-start.2 = ((bf16[64,4,4096]{2,1,0:T(4,128)(2,1)}), bf16[64,4,4096]{2,1,0:T(4,128)(2,1)}, u32[]{:S(2)}, u32[]{:S(2)}) async-start(bf16[64,4,4096]{2,1,0:T(4,128)(2,1)} %copy.41), calls=%async_computation.2 | async-start | bytes 4194304 | tf_op jit(solution)/shard_map/all_to_all | solution.py:118
  167.2 4.0 %reshape.204 = bf16[256,4096]{1,0:T(8,128)(2,1)} reshape(bf16[64,4,4096]{2,1,0:T(4,128)(2,1)} %get-tuple-element.6) | data formatting | bytes 4194304 | tf_op jit(solution)/shard_map/reshape | solution.py:116
  171.2 3.9 %fusion.13 = f32[256,384]{1,0:T(8,128)S(1)} fusion(bf16[256,4096]{1,0:T(8,128)(2,1)} %reshape.204, bf16[1,1,4096,384]{3,2,1,0:T(8,128)(2,1)} %param.14), kind=kOutput, calls=%fused_computation.19 | convolution fusion | flops 805306368 | bytes 5636096 | tf_op jit(solution)/shard_map/dot_general | solution.py:46
  175.2 0.1 copy-done.8
  175.3 1.3 fusion.43
  176.6 0.1 dot_general.43
  176.6 1.3 convolution_convert_fusion.2
  177.9 2.9 copy.38
  180.8 35.6 %all-to-all-done.2 = bf16[64,4,4096]{2,1,0:T(4,128)(2,1)} async-done(((bf16[64,4,4096]{2,1,0:T(4,128)(2,1)}), bf16[64,4,4096]{2,1,0:T(4,128)(2,1)}, u32[]{:S(2)}, u32[]{:S(2)}) %all-to-all-start.2) | async-done | bytes 2097184 | tf_op jit(solution)/shard_map/all_to_all | solution.py:118
  216.5 5.4 %all-to-all-start.1 = ((bf16[64,4,4096]{2,1,0:T(4,128)(2,1)}), bf16[64,4,4096]{2,1,0:T(4,128)(2,1)S(1)}, u32[]{:S(2)}, u32[]{:S(2)}) async-start(bf16[64,4,4096]{2,1,0:T(4,128)(2,1)} %copy.38), calls=%async_computation.1 | async-start | bytes 4194304 | tf_op jit(solution)/shard_map/all_to_all | solution.py:118
  221.9 0.1 collective-permute-start.4
  222.0 0.3 collective-permute-start.3
  222.4 5.5 %convolution_bitcast_fusion = f32[128,4096]{1,0:T(8,128)} fusion(bf16[64,4,4096]{2,1,0:T(4,128)(2,1)} %all-to-all-done.2, s32[128]{0:T(128)S(1)} %add_select_fusion.3, s32[64,8]{0,1:T(8,128)S(1)} %fusion.80), kind=kOutput, calls=%fused_computation.4 | convolution fusion | flops 268500992 | bytes 4196864 | tf_op jit(solution)/shard_map/dot_general | solution.py:121
  227.9 43.7 %all-to-all-done.1 = bf16[64,4,4096]{2,1,0:T(4,128)(2,1)S(1)} async-done(((bf16[64,4,4096]{2,1,0:T(4,128)(2,1)}), bf16[64,4,4096]{2,1,0:T(4,128)(2,1)S(1)}, u32[]{:S(2)}, u32[]{:S(2)}) %all-to-all-start.1) | async-done | bytes 2097184 | tf_op jit(solution)/shard_map/all_to_all | solution.py:118
  271.6 5.3 %fusion.17 = (f32[128]{0:T(128)S(1)}, bf16[128,4096]{1,0:T(8,128)(2,1)}) fusion(f32[128,4096]{1,0:T(8,128)} %convolution_bitcast_fusion, bf16[64,4,4096]{2,1,0:T(4,128)(2,1)S(1)} %all-to-all-done.1, s32[128]{0:T(128)S(1)} %add_select_fusion.3, s32[64,8]{0,1:T(8,128)S(1)} %fusion.80, f32[128]{0:T(128)S(1)} %fusion.81, bf16[1,128,4096]{2,1,0:T(8,128)(2,1)S(1)} %copy-done.2), kind=kOutput, calls=%fused_computation.28 | convolution fusion | flops 272695168 | bytes 6295040 | tf_op jit(solution)/shard_map/dot_general | solution.py:121
  276.9 6.5 %fusion.47 = f32[128,1408]{1,0:T(8,128)S(1)} fusion(bf16[4096,1408]{1,0:T(8,128)(2,1)} %all-gather.2.cloned.1.call-done, bf16[128,4096]{1,0:T(8,128)(2,1)} %get-tuple-element.18, f32[128]{0:T(128)S(1)} %add_rsqrt_fusion.2), kind=kOutput, calls=%fused_computation.44 | convolution fusion | flops 1477967872 | bytes 13304320 | tf_op jit(solution)/shard_map/dot_general | solution.py:131
  283.3 0.1 multiply_reduce_fusion.1
  283.4 1.4 slice_convert_fusion
  284.9 1.2 reshape.209
  286.1 0.1 fusion.74
  286.2 0.1 fusion.69
  286.3 0.9 select_reduce_fusion
  287.2 0.3 multiply_cosine_fusion
  287.5 0.1 fusion.71
  287.6 1.3 collective-permute-start.5
  288.9 3.8 %collective-permute-start.6 = (bf16[128,256]{1,0:T(8,128)(2,1)S(1)}, bf16[128,256]{1,0:T(8,128)(2,1)S(1)}, u32[]{:S(2)}, u32[]{:S(2)}) collective-permute-start(bf16[128,256]{1,0:T(8,128)(2,1)S(1)} %pad_maximum_fusion.2), channel_id=1, source_target_pairs={{0,3},{1,4},{2,5},{3,6},{4,7},{5,8},{6,9},{7,10},{8,11},{9,12},{10... | collective-permute-start | bytes 196616 | tf_op jit(solution)/shard_map/ppermute | solution.py:28
  292.7 1.3 collective-permute-start.7
  294.0 5.3 %collective-permute-start.8 = (bf16[128,256]{1,0:T(8,128)(2,1)S(1)}, bf16[128,256]{1,0:T(8,128)(2,1)S(1)}, u32[]{:S(2)}, u32[]{:S(2)}) collective-permute-start(bf16[128,256]{1,0:T(8,128)(2,1)S(1)} %pad_maximum_fusion.2), channel_id=1, source_target_pairs={{0,1},{1,2},{2,3},{3,4},{4,5},{5,6},{6,7},{7,8},{8,9},{9,10},{10,1... | collective-permute-start | bytes 196616 | tf_op jit(solution)/shard_map/ppermute | solution.py:28
  299.4 0.1 copy.50
  299.5 0.2 multiply_reduce_fusion
  299.8 0.1 copy.44
  299.9 0.2 multiply_multiply_fusion
  300.1 0.2 slice_negate_fusion
  300.3 0.3 fusion.53
  300.7 0.1 compare_and_fusion
  300.9 0.1 collective-permute-done.8
  301.0 0.9 fusion.15
  301.9 0.6 fusion.31
  302.5 0.9 copy.47
  303.3 12.7 %collective-permute-done.9 = bf16[128,1024]{1,0:T(8,128)(2,1)S(1)} collective-permute-done((bf16[128,1024]{1,0:T(8,128)(2,1)}, bf16[128,1024]{1,0:T(8,128)(2,1)S(1)}, u32[]{:S(2)}, u32[]{:S(2)}) %collective-permute-start.9) | collective-permute-done | bytes 262176 | tf_op jit(solution)/shard_map/ppermute | solution.py:22
  316.0 0.7 copy.70
  (53 shorter events, 0.3 us)
Async XLA Ops:
  7.2 149.9 %copy-start = (bf16[1,1,384,4096]{3,2,1,0:T(8,128)(2,1)S(1)}, bf16[1,1,384,4096]{3,2,1,0:T(8,128)(2,1)}, u32[]{:S(2)}) copy-start(bf16[1,1,384,4096]{3,2,1,0:T(8,128)(2,1)} %param.16) | copy-start | bytes 9437188
  7.2 269.7 %all-gather.2.cloned.1.call-start = ((), (), s32[]{:S(2)}) async-start(), calls=%async_computation.3 | async-start | bytes 12255232 | tf_op jit(solution)/shard_map/all_gather | solution.py:108
  7.2 14.6 %collective-permute-start.2 = (s32[128]{0:T(128)}, s32[128]{0:T(128)S(1)}, u32[]{:S(2)}, u32[]{:S(2)}) collective-permute-start(s32[128]{0:T(128)} %bitcast.101), channel_id=1, source_target_pairs={{64,0},{128,64},{192,128},{0,192},{65,1},{129,65},{193,129},{1,193... | collective-permute-start | bytes 1544 | tf_op jit(solution)/shard_map/ppermute | solution.py:22
  13.0 8.9 %collective-permute-start.1 = (bf16[64,256]{1,0:T(8,128)(2,1)}, bf16[64,256]{1,0:T(8,128)(2,1)S(1)}, u32[]{:S(2)}, u32[]{:S(2)}) collective-permute-start(bf16[64,256]{1,0:T(8,128)(2,1)} %bitcast.100), channel_id=1, source_target_pairs={{64,0},{128,64},{192,128},{0,192},{65,1},{129,65},{193,129},{1,193... | collective-permute-start | bytes 98312 | tf_op jit(solution)/shard_map/ppermute | solution.py:22
  13.7 8.3 %collective-permute-start = (bf16[64,1024]{1,0:T(8,128)(2,1)}, bf16[64,1024]{1,0:T(8,128)(2,1)S(1)}, u32[]{:S(2)}, u32[]{:S(2)}) collective-permute-start(bf16[64,1024]{1,0:T(8,128)(2,1)} %bitcast.99), channel_id=1, source_target_pairs={{64,0},{128,64},{192,128},{0,192},{65,1},{129,65},{193,129},{1,193... | collective-permute-start | bytes 393224 | tf_op jit(solution)/shard_map/ppermute | solution.py:22
  151.4 4.2 %copy-start.3 = (bf16[256,4096]{1,0:T(8,128)(2,1)S(1)}, bf16[256,4096]{1,0:T(8,128)(2,1)}, u32[]{:S(2)}) copy-start(bf16[256,4096]{1,0:T(8,128)(2,1)} %reshape.205) | copy-start | bytes 6291460
  151.4 4.3 %copy-start.7 = (bf16[1,1,4096,384]{3,2,1,0:T(8,128)(2,1)S(1)}, bf16[1,1,4096,384]{3,2,1,0:T(8,128)(2,1)}, u32[]{:S(2)}) copy-start(bf16[1,1,4096,384]{3,2,1,0:T(8,128)(2,1)} %param.15) | copy-start | bytes 9437188
  161.3 55.2 %all-to-all-start.2 = ((bf16[64,4,4096]{2,1,0:T(4,128)(2,1)}), bf16[64,4,4096]{2,1,0:T(4,128)(2,1)}, u32[]{:S(2)}, u32[]{:S(2)}) async-start(bf16[64,4,4096]{2,1,0:T(4,128)(2,1)} %copy.41), calls=%async_computation.2 | async-start | bytes 4194304 | tf_op jit(solution)/shard_map/all_to_all | solution.py:118
  171.2 4.0 %copy-start.4 = (bf16[256,4096]{1,0:T(8,128)(2,1)S(1)}, bf16[256,4096]{1,0:T(8,128)(2,1)}, u32[]{:S(2)}) copy-start(bf16[256,4096]{1,0:T(8,128)(2,1)} %reshape.204) | copy-start | bytes 6291460
  171.2 4.1 %copy-start.8 = (bf16[1,1,4096,384]{3,2,1,0:T(8,128)(2,1)S(1)}, bf16[1,1,4096,384]{3,2,1,0:T(8,128)(2,1)}, u32[]{:S(2)}) copy-start(bf16[1,1,4096,384]{3,2,1,0:T(8,128)(2,1)} %param.15) | copy-start | bytes 9437188
  180.8 41.1 %copy-start.9 = (f32[1,128]{1,0:T(1,128)S(1)}, f32[1,128]{1,0:T(1,128)}, u32[]{:S(2)}) copy-start(f32[1,128]{1,0:T(1,128)} %param.20) | copy-start | bytes 1540
  180.8 41.2 %copy-start.10 = (f32[1,128]{1,0:T(1,128)S(1)}, f32[1,128]{1,0:T(1,128)}, u32[]{:S(2)}) copy-start(f32[1,128]{1,0:T(1,128)} %param.19) | copy-start | bytes 1540
  180.8 41.5 %copy-start.5 = (s32[1,128,8]{1,2,0:T(8,128)S(1)}, s32[1,128,8]{1,2,0:T(8,128)}, u32[]{:S(2)}) copy-start(s32[1,128,8]{1,2,0:T(8,128)} %param.12) | copy-start | bytes 12292
  180.8 41.6 %copy-start.6 = (f32[1,128,8]{1,2,0:T(8,128)S(1)}, f32[1,128,8]{1,2,0:T(8,128)}, u32[]{:S(2)}) copy-start(f32[1,128,8]{1,2,0:T(8,128)} %param.13) | copy-start | bytes 12292
  216.5 55.1 %all-to-all-start.1 = ((bf16[64,4,4096]{2,1,0:T(4,128)(2,1)}), bf16[64,4,4096]{2,1,0:T(4,128)(2,1)S(1)}, u32[]{:S(2)}, u32[]{:S(2)}) async-start(bf16[64,4,4096]{2,1,0:T(4,128)(2,1)} %copy.38), calls=%async_computation.1 | async-start | bytes 4194304 | tf_op jit(solution)/shard_map/all_to_all | solution.py:118
  221.9 64.2 %collective-permute-start.4 = (f32[128]{0:T(128)S(1)}, f32[128]{0:T(128)S(1)}, u32[]{:S(2)}, u32[]{:S(2)}) collective-permute-start(f32[128]{0:T(128)S(1)} %bitcast.102), channel_id=1, source_target_pairs={{64,0},{128,64},{192,128},{0,192},{65,1},{129,65},{193,129},{1,193... | collective-permute-start | bytes 1544 | tf_op jit(solution)/shard_map/ppermute | solution.py:22
  222.0 77.9 %collective-permute-start.3 = (f32[128]{0:T(128)S(1)}, f32[128]{0:T(128)S(1)}, u32[]{:S(2)}, u32[]{:S(2)}) collective-permute-start(f32[128]{0:T(128)S(1)} %bitcast.103), channel_id=1, source_target_pairs={{64,0},{128,64},{192,128},{0,192},{65,1},{129,65},{193,129},{1,193... | collective-permute-start | bytes 1544 | tf_op jit(solution)/shard_map/ppermute | solution.py:22
  222.4 49.2 %copy-start.2 = (bf16[1,128,4096]{2,1,0:T(8,128)(2,1)S(1)}, bf16[1,128,4096]{2,1,0:T(8,128)(2,1)}, u32[]{:S(2)}) copy-start(bf16[1,128,4096]{2,1,0:T(8,128)(2,1)} %param.11) | copy-start | bytes 3145732
  287.6 13.2 %collective-permute-start.5 = (bf16[128,256]{1,0:T(8,128)(2,1)S(1)}, bf16[128,256]{1,0:T(8,128)(2,1)S(1)}, u32[]{:S(2)}, u32[]{:S(2)}) collective-permute-start(bf16[128,256]{1,0:T(8,128)(2,1)S(1)} %pad_maximum_fusion.2), channel_id=1, source_target_pairs={{0,4},{1,5},{2,6},{3,7},{4,8},{5,9},{6,10},{7,11},{8,12},{9,13},{1... | collective-permute-start | bytes 196616 | tf_op jit(solution)/shard_map/ppermute | solution.py:28
  288.9 11.9 %collective-permute-start.6 = (bf16[128,256]{1,0:T(8,128)(2,1)S(1)}, bf16[128,256]{1,0:T(8,128)(2,1)S(1)}, u32[]{:S(2)}, u32[]{:S(2)}) collective-permute-start(bf16[128,256]{1,0:T(8,128)(2,1)S(1)} %pad_maximum_fusion.2), channel_id=1, source_target_pairs={{0,3},{1,4},{2,5},{3,6},{4,7},{5,8},{6,9},{7,10},{8,11},{9,12},{10... | collective-permute-start | bytes 196616 | tf_op jit(solution)/shard_map/ppermute | solution.py:28
  292.7 8.2 %collective-permute-start.7 = (bf16[128,256]{1,0:T(8,128)(2,1)S(1)}, bf16[128,256]{1,0:T(8,128)(2,1)S(1)}, u32[]{:S(2)}, u32[]{:S(2)}) collective-permute-start(bf16[128,256]{1,0:T(8,128)(2,1)S(1)} %pad_maximum_fusion.2), channel_id=1, source_target_pairs={{0,2},{1,3},{2,4},{3,5},{4,6},{5,7},{6,8},{7,9},{8,10},{9,11},{10,... | collective-permute-start | bytes 196616 | tf_op jit(solution)/shard_map/ppermute | solution.py:28
  294.0 7.0 %collective-permute-start.8 = (bf16[128,256]{1,0:T(8,128)(2,1)S(1)}, bf16[128,256]{1,0:T(8,128)(2,1)S(1)}, u32[]{:S(2)}, u32[]{:S(2)}) collective-permute-start(bf16[128,256]{1,0:T(8,128)(2,1)S(1)} %pad_maximum_fusion.2), channel_id=1, source_target_pairs={{0,1},{1,2},{2,3},{3,4},{4,5},{5,6},{6,7},{7,8},{8,9},{9,10},{10,1... | collective-permute-start | bytes 196616 | tf_op jit(solution)/shard_map/ppermute | solution.py:28
  301.8 14.9 %copy-start.1 = (bf16[1,1,384,4096]{3,2,1,0:T(8,128)(2,1)S(1)}, bf16[1,1,384,4096]{3,2,1,0:T(8,128)(2,1)}, u32[]{:S(2)}) copy-start(bf16[1,1,384,4096]{3,2,1,0:T(8,128)(2,1)} %param.16) | copy-start | bytes 9437188
  303.3 12.7 %collective-permute-start.9 = (bf16[128,1024]{1,0:T(8,128)(2,1)}, bf16[128,1024]{1,0:T(8,128)(2,1)S(1)}, u32[]{:S(2)}, u32[]{:S(2)}) collective-permute-start(bf16[128,1024]{1,0:T(8,128)(2,1)} %copy.47), channel_id=1, source_target_pairs={{192,0},{0,64},{64,128},{128,192},{193,1},{1,65},{65,129},{129,193... | collective-permute-start | bytes 786440 | tf_op jit(solution)/shard_map/ppermute | solution.py:22
Sparse Core Ops, SparseCore 0:
  39.8 126.9 all-gather.1

commit v12 on v10

--- a/solution.py
+++ b/solution.py
@@ -105,9 +105,8 @@
     projection = jnp.concatenate([next_query, next_keyval, carried], axis=-1)
     projection = lax.all_gather(projection, EP[-1], axis=0, tiled=True)
     spread, projection = lax.optimization_barrier((spread, projection))
+    projection = lax.all_gather(projection, EP[:-1], axis=0, tiled=True)
     received = lax.all_to_all(spread, EP, split_axis=0, concat_axis=0, tiled=True)
-    received, projection = lax.optimization_barrier((received, projection))
-    projection = lax.all_gather(projection, EP[:-1], axis=0, tiled=True)
     partial_out = feed_forward(
         received.reshape(-1, model_width), gate_part, up_part, down_part
     ).reshape(received.shape)
@@ -153,25 +152,32 @@
         earlier_pieces.append(passed_along_2(key_value, EP, distance))
     window = jnp.concatenate(earlier_pieces[::-1] + [key_value], axis=0)
     score_scale = 1.0 / math.sqrt(head_dim)
-    scores = (
-        jnp.einsum(
-            "thd,kd->thk", query, window[:, :head_dim], preferred_element_type=jnp.float32
-        )
-        * score_scale
-    )
     allowed = (
         (key_index[None, :] >= start_index[:, None]) & (key_index[None, :] <= global_index[:, None])
     )[:, None, :]
-    probabilities = jnp.where(allowed, jnp.exp(scores), 0.0)
-    total_mass = jnp.sum(probabilities, axis=-1)
-    mixed = jnp.einsum(
-        "thk,kd->thd",
-        probabilities.astype(jnp.bfloat16),
-        window[:, head_dim:],
-        preferred_element_type=jnp.float32,
-    )
-    attended = (mixed / total_mass[..., None]).astype(jnp.bfloat16).reshape(token_count, query_width)
-    attended = passed_along(attended, "section", 1)
+    head_half = head_count // 2
+    handed = []
+    for first in (0, head_half):
+        scores = (
+            jnp.einsum(
+                "thd,kd->thk",
+                query[:, first : first + head_half],
+                window[:, :head_dim],
+                preferred_element_type=jnp.float32,
+            )
+            * score_scale
+        )
+        probabilities = jnp.where(allowed, jnp.exp(scores), 0.0)
+        total_mass = jnp.sum(probabilities, axis=-1)
+        mixed = jnp.einsum(
+            "thk,kd->thd",
+            probabilities.astype(jnp.bfloat16),
+            window[:, head_dim:],
+            preferred_element_type=jnp.float32,
+        )
+        part = (mixed / total_mass[..., None]).astype(jnp.bfloat16)
+        handed.append(passed_along(part.reshape(token_count, -1), "section", 1))
+    attended = jnp.concatenate(handed, axis=-1)
     return (layer_out[None], attended[None])
 
 

time: 337 us -> 323 us (0.958)
  waiting for transfers between devices: 115 us -> 100 us
    all_gather x1, waiting for transfers between devices: 11.5 us -> 0.01 us  [on_device(): projection = lax.all_gather(projection, EP[:-1], axis=0, tiled=True)]
    unnamed x25 -> x24, local copies, waits for them, and re-layouts: 5.23 us -> 7.27 us
    ppermute x6 -> x7, waiting for transfers between devices: 10 us -> 8.24 us  [passed_along(): return lax.ppermute(block, axis, route)]
    ppermute x6 -> x7, starting transfers between devices: 7.17 us -> 8.1 us  [passed_along(): return lax.ppermute(block, axis, route)]
  transfers between devices with their start and end apart: 12 -> 13, of which waited for: 3 -> 3; matrix products, arithmetic and copies ran while one was open for 16% -> 16% of each run, Pallas kernels for 0% -> 0%
where the time goes in v12:
time: 323 us; the launch traced here: 318 us
  blocking collectives  122 us (38%)
  waiting for transfers between devices  100 us (31%)
  matrix products  32.4 us (10%)
  starting transfers between devices  25.1 us (8%)
  between operations  14.3 us (4%)
  other arithmetic  13.7 us (4%)
  local copies, waits for them, and re-layouts  10.4 us (3%)
    all_to_all x1, blocking collectives, on_device(): lax.all_to_all(spread, EP, split_axis=0, concat_axis=0, tiled=True)  104 us
    all_to_all x1, waiting for transfers between devices, on_device(): lax.all_to_all(partial_out.astype(jnp.bfloat16), EP, split_axis=0, concat...  92.2 us
    all_gather x1, blocking collectives, on_device(): projection = lax.all_gather(projection, EP[-1], axis=0, tiled=True)  17.4 us
    ppermute x4, starting transfers between devices, passed_along_2(): lax.ppermute(value, axis, [(source, source + steps) for source in range(l...  10.6 us
    dot_general x1, matrix products, feed_forward(): return jnp.dot(activated, down_part, preferred_element_type=jnp.float32)  9.89 us
    ppermute x7, waiting for transfers between devices, passed_along(): return lax.ppermute(block, axis, route)  8.24 us
    ppermute x7, starting transfers between devices, passed_along(): return lax.ppermute(block, axis, route)  8.1 us
    unnamed x24, local copies, waits for them, and re-layouts  7.27 us
  transfers between devices with their start and end apart: 13, of which 3 were waited for; matrix products, arithmetic and copies ran while one was open for 16% of the time, Pallas kernels for 0%

profile of v12, /device:TPU:32, one launch (start us, length us, event | category | flops | bytes accessed | tf_op | source)
XLA Modules:
  0.0 318.3 jit_solution(12190277921333163825)
XLA Ops:
  7.2 0.0 copy-start
  7.2 0.0 all-gather.2.cloned.1.call-start
  7.2 5.8 %collective-permute-start.2 = (s32[128]{0:T(128)}, s32[128]{0:T(128)S(1)}, u32[]{:S(2)}, u32[]{:S(2)}) collective-permute-start(s32[128]{0:T(128)} %bitcast.117), channel_id=1, source_target_pairs={{64,0},{128,64},{192,128},{0,192},{65,1},{129,65},{193,129},{1,193... | collective-permute-start | bytes 1544 | tf_op jit(solution)/shard_map/ppermute | solution.py:22
  13.0 0.7 collective-permute-start
  13.7 0.1 collective-permute-start.1
  13.8 0.7 fusion.74
  14.5 0.7 fusion.82
  15.2 0.1 fusion.67
  15.3 0.2 reduce_window_sum.11
  15.5 0.2 select_reduce_fusion.1
  15.7 1.5 fusion.13
  17.2 4.6 %fusion = bf16[64,8,4096]{2,1,0:T(8,128)(2,1)} fusion(bf16[1,128,4096]{2,1,0:T(8,128)(2,1)} %param.11, f32[128]{0:T(128)S(1)} %add_rsqrt_fusion.3, s32[128]{0:T(128)S(1)} %add_select_fusion.1, s32[512]{0:T(512)S(1)} %fusion.76), kind=kOutput, calls=%fused_computation.2 | convolution fusion | flops 540606464 | bytes 5245952 | tf_op jit(solution)/shard_map/dot_general | solution.py:87
  21.8 0.0 collective-permute-done.2
  21.8 0.1 convert_element_type.73
  22.0 0.0 collective-permute-done.1
  22.0 17.4 %all_gather.6 = bf16[256,1408]{1,0:T(8,128)(2,1)} all-gather(bf16[64,1408]{1,0:T(8,128)(2,1)S(1)} %fusion.58), channel_id=1, replica_groups=mesh['section'=4,'ep_y'=4,'ep_x'=4,'ep_z'=4] {'ep_z'}, dimensions={0}, use_global_device_ids=true | all-gather | bytes 901120 | tf_op jit(solution)/shard_map/all_gather | solution.py:106
  39.5 0.0 all-gather.2.cloned.1.call-update
  39.5 0.0 copy-start.7
  39.5 104.4 %all_to_all.10 = bf16[64,8,4096]{2,1,0:T(8,128)(2,1)S(1)} all-to-all(bf16[64,8,4096]{2,1,0:T(8,128)(2,1)} %fusion), channel_id=1, replica_groups=mesh['section'=4,'ep_y'=4,'ep_x'=4,'ep_z'=4] {'ep_y','ep_x','ep_z'}, dimensions={0} | all-to-all | bytes 8388608 | tf_op jit(solution)/shard_map/all_to_all | solution.py:109
  143.9 2.0 copy-done.2
  145.8 3.2 %fusion.6 = f32[512,384]{1,0:T(8,128)} fusion(bf16[64,8,4096]{2,1,0:T(8,128)(2,1)S(1)} %all_to_all.10, bf16[1,1,4096,384]{3,2,1,0:T(8,128)(2,1)S(1)} %copy-done.7), kind=kOutput, calls=%fused_computation.9 | convolution fusion | flops 1610612736 | bytes 8126464 | tf_op jit(solution)/shard_map/dot_general | solution.py:46
  149.0 9.9 %convolution_convert_fusion.1 = bf16[64,8,4096]{2,1,0:T(8,128)(2,1)} fusion(bf16[1,1,384,4096]{3,2,1,0:T(8,128)(2,1)S(1)} %copy-done, bf16[1,1,4096,384]{3,2,1,0:T(8,128)(2,1)} %param.15, bf16[64,8,4096]{2,1,0:T(8,128)(2,1)} %copy-done.2, f32[512,384]{1,0:T(8,128)} %fusion.6), kind=kOutput, calls=%fused_computation.1 | convolution fusion | flops 3224502272 | bytes 15466496 | tf_op jit(solution)/shard_map/dot_general | solution.py:49
  158.9 6.4 %all-to-all-start.1 = ((bf16[64,8,4096]{2,1,0:T(8,128)(2,1)}), bf16[64,8,4096]{2,1,0:T(8,128)(2,1)}, u32[]{:S(2)}, u32[]{:S(2)}) async-start(bf16[64,8,4096]{2,1,0:T(8,128)(2,1)} %convolution_convert_fusion.1), calls=%async_computation.1 | async-start | bytes 8388608 | tf_op jit(solution)/shard_map/all_to_all | solution.py:113
  165.3 0.1 collective-permute-start.4
  165.4 1.2 collective-permute-start.3
  166.6 0.5 iota_add_fusion.1
  167.2 92.2 %all-to-all-done.1 = bf16[64,8,4096]{2,1,0:T(8,128)(2,1)} async-done(((bf16[64,8,4096]{2,1,0:T(8,128)(2,1)}), bf16[64,8,4096]{2,1,0:T(8,128)(2,1)}, u32[]{:S(2)}, u32[]{:S(2)}) %all-to-all-start.1) | async-done | bytes 4194336 | tf_op jit(solution)/shard_map/all_to_all | solution.py:113
  259.4 4.5 %fusion.11 = (f32[128]{0:T(128)S(1)}, bf16[128,4096]{1,0:T(8,128)(2,1)}) fusion(bf16[64,8,4096]{2,1,0:T(8,128)(2,1)} %all-to-all-done.1, s32[128]{0:T(128)S(1)} %add_select_fusion.1, s32[512]{0:T(512)S(1)} %fusion.76, f32[128]{0:T(128)S(1)} %fusion.73, bf16[1,128,4096]{2,1,0:T(8,128)(2,1)} %param.11), kind=kOutput, calls=%fused_computation.19 | convolution fusion | flops 540606336 | bytes 6295040 | tf_op jit(solution)/shard_map/dot_general | solution.py:116
  263.9 6.5 %fusion.37 = f32[128,1408]{1,0:T(8,128)S(1)} fusion(bf16[4096,1408]{1,0:T(8,128)(2,1)} %all-gather.2.cloned.1.call-done, bf16[128,4096]{1,0:T(8,128)(2,1)} %get-tuple-element.18, f32[128]{0:T(128)S(1)} %add_rsqrt_fusion.2), kind=kOutput, calls=%fused_computation.36 | convolution fusion | flops 1477967872 | bytes 13304320 | tf_op jit(solution)/shard_map/dot_general | solution.py:124
  270.4 0.1 multiply_reduce_fusion.1
  270.5 0.7 copy-done.3
  271.3 0.1 fusion.68
  271.3 0.1 fusion.63
  271.4 2.9 slice_convert_fusion
  274.3 2.7 reshape.193
  277.0 0.8 select_reduce_fusion
  277.9 0.3 multiply_cosine_fusion
  278.2 1.0 fusion.65
  279.2 1.9 collective-permute-start.5
  281.1 3.4 %collective-permute-start.6 = (bf16[128,256]{1,0:T(8,128)(2,1)S(1)}, bf16[128,256]{1,0:T(8,128)(2,1)}, u32[]{:S(2)}, u32[]{:S(2)}) collective-permute-start(bf16[128,256]{1,0:T(8,128)(2,1)S(1)} %pad_maximum_fusion.2), channel_id=1, source_target_pairs={{0,3},{1,4},{2,5},{3,6},{4,7},{5,8},{6,9},{7,10},{8,11},{9,12},{10... | collective-permute-start | bytes 196616 | tf_op jit(solution)/shard_map/ppermute | solution.py:28
  284.5 1.9 collective-permute-start.7
  286.4 3.4 %collective-permute-start.8 = (bf16[128,256]{1,0:T(8,128)(2,1)S(1)}, bf16[128,256]{1,0:T(8,128)(2,1)S(1)}, u32[]{:S(2)}, u32[]{:S(2)}) collective-permute-start(bf16[128,256]{1,0:T(8,128)(2,1)S(1)} %pad_maximum_fusion.2), channel_id=1, source_target_pairs={{0,1},{1,2},{2,3},{3,4},{4,5},{5,6},{6,7},{7,8},{8,9},{9,10},{10,1... | collective-permute-start | bytes 196616 | tf_op jit(solution)/shard_map/ppermute | solution.py:28
  289.8 1.9 slice_bitcast_fusion.1
  291.7 0.1 copy.46
  291.8 0.2 multiply_reduce_fusion
  292.1 0.0 collective-permute-done.3
  292.1 1.3 fusion.51
  293.4 0.2 slice_negate_fusion
  293.7 0.3 fusion.53
  294.0 0.8 compare_and_fusion
  294.8 0.8 constant_dynamic-update-slice_fusion.4
  295.7 0.8 constant_dynamic-update-slice_fusion.3
  296.5 0.8 constant_dynamic-update-slice_fusion.2
  297.4 0.6 fusion.84
  297.9 1.3 fusion.83
  299.3 0.4 fusion.34
  299.6 0.1 copy.38
  299.7 0.1 collective-permute-start.9
  299.8 1.5 fusion.35
  301.3 0.1 copy.40
  301.4 0.2 collective-permute-start.10
  301.6 6.7 %collective-permute-done.9 = bf16[128,512]{1,0:T(8,128)(2,1)} collective-permute-done((bf16[128,512]{1,0:T(8,128)(2,1)S(1)}, bf16[128,512]{1,0:T(8,128)(2,1)}, u32[]{:S(2)}, u32[]{:S(2)}) %collective-permute-start.9) | collective-permute-done | bytes 131104 | tf_op jit(solution)/shard_map/ppermute | solution.py:22
  308.3 1.5 collective-permute-done.10
  309.8 1.6 maximum_bitcast_fusion
  (38 shorter events, 0.2 us)
Async XLA Ops:
  7.2 141.9 %copy-start = (bf16[1,1,384,4096]{3,2,1,0:T(8,128)(2,1)S(1)}, bf16[1,1,384,4096]{3,2,1,0:T(8,128)(2,1)}, u32[]{:S(2)}) copy-start(bf16[1,1,384,4096]{3,2,1,0:T(8,128)(2,1)} %param.16) | copy-start | bytes 9437188
  7.2 256.7 %all-gather.2.cloned.1.call-start = ((), (), s32[]{:S(2)}) async-start(), calls=%async_computation.2 | async-start | bytes 12255232 | tf_op jit(solution)/shard_map/all_gather | solution.py:108
  7.2 14.6 %collective-permute-start.2 = (s32[128]{0:T(128)}, s32[128]{0:T(128)S(1)}, u32[]{:S(2)}, u32[]{:S(2)}) collective-permute-start(s32[128]{0:T(128)} %bitcast.117), channel_id=1, source_target_pairs={{64,0},{128,64},{192,128},{0,192},{65,1},{129,65},{193,129},{1,193... | collective-permute-start | bytes 1544 | tf_op jit(solution)/shard_map/ppermute | solution.py:22
  13.0 9.0 %collective-permute-start = (bf16[64,1024]{1,0:T(8,128)(2,1)}, bf16[64,1024]{1,0:T(8,128)(2,1)S(1)}, u32[]{:S(2)}, u32[]{:S(2)}) collective-permute-start(bf16[64,1024]{1,0:T(8,128)(2,1)} %bitcast.115), channel_id=1, source_target_pairs={{64,0},{128,64},{192,128},{0,192},{65,1},{129,65},{193,129},{1,193... | collective-permute-start | bytes 393224 | tf_op jit(solution)/shard_map/ppermute | solution.py:22
  13.7 8.3 %collective-permute-start.1 = (bf16[64,256]{1,0:T(8,128)(2,1)}, bf16[64,256]{1,0:T(8,128)(2,1)S(1)}, u32[]{:S(2)}, u32[]{:S(2)}) collective-permute-start(bf16[64,256]{1,0:T(8,128)(2,1)} %bitcast.116), channel_id=1, source_target_pairs={{64,0},{128,64},{192,128},{0,192},{65,1},{129,65},{193,129},{1,193... | collective-permute-start | bytes 98312 | tf_op jit(solution)/shard_map/ppermute | solution.py:22
  39.5 106.3 %copy-start.7 = (bf16[1,1,4096,384]{3,2,1,0:T(8,128)(2,1)S(1)}, bf16[1,1,4096,384]{3,2,1,0:T(8,128)(2,1)}, u32[]{:S(2)}) copy-start(bf16[1,1,4096,384]{3,2,1,0:T(8,128)(2,1)} %param.14) | copy-start | bytes 9437188
  143.8 2.0 copy-start.2
  158.9 6.4 %copy-start.8 = (f32[1,128]{1,0:T(1,128)S(1)}, f32[1,128]{1,0:T(1,128)}, u32[]{:S(2)}) copy-start(f32[1,128]{1,0:T(1,128)} %param.20) | copy-start | bytes 1540
  158.9 8.2 %copy-start.4 = (s32[1,128,8]{1,2,0:T(8,128)S(1)}, s32[1,128,8]{1,2,0:T(8,128)}, u32[]{:S(2)}) copy-start(s32[1,128,8]{1,2,0:T(8,128)} %param.12) | copy-start | bytes 12292
  158.9 8.2 %copy-start.6 = (f32[1,128,8]{1,2,0:T(8,128)S(1)}, f32[1,128,8]{1,2,0:T(8,128)}, u32[]{:S(2)}) copy-start(f32[1,128,8]{1,2,0:T(8,128)} %param.13) | copy-start | bytes 12292
  158.9 100.4 %all-to-all-start.1 = ((bf16[64,8,4096]{2,1,0:T(8,128)(2,1)}), bf16[64,8,4096]{2,1,0:T(8,128)(2,1)}, u32[]{:S(2)}, u32[]{:S(2)}) async-start(bf16[64,8,4096]{2,1,0:T(8,128)(2,1)} %convolution_convert_fusion.1), calls=%async_computation.1 | async-start | bytes 8388608 | tf_op jit(solution)/shard_map/all_to_all | solution.py:113
  165.3 105.2 %collective-permute-start.4 = (f32[128]{0:T(128)S(1)}, f32[128]{0:T(128)S(1)}, u32[]{:S(2)}, u32[]{:S(2)}) collective-permute-start(f32[128]{0:T(128)S(1)} %bitcast.118), channel_id=1, source_target_pairs={{64,0},{128,64},{192,128},{0,192},{65,1},{129,65},{193,129},{1,193... | collective-permute-start | bytes 1544 | tf_op jit(solution)/shard_map/ppermute | solution.py:22
  165.4 126.7 %collective-permute-start.3 = (f32[128]{0:T(128)}, f32[128]{0:T(128)S(1)}, u32[]{:S(2)}, u32[]{:S(2)}) collective-permute-start(f32[128]{0:T(128)} %bitcast.16), channel_id=1, source_target_pairs={{64,0},{128,64},{192,128},{0,192},{65,1},{129,65},{193,129},{1,193... | collective-permute-start | bytes 1544 | tf_op jit(solution)/shard_map/ppermute | solution.py:22
  270.4 0.9 copy-start.3
  279.2 15.6 %collective-permute-start.5 = (bf16[128,256]{1,0:T(8,128)(2,1)S(1)}, bf16[128,256]{1,0:T(8,128)(2,1)}, u32[]{:S(2)}, u32[]{:S(2)}) collective-permute-start(bf16[128,256]{1,0:T(8,128)(2,1)S(1)} %pad_maximum_fusion.2), channel_id=1, source_target_pairs={{0,4},{1,5},{2,6},{3,7},{4,8},{5,9},{6,10},{7,11},{8,12},{9,13},{1... | collective-permute-start | bytes 196616 | tf_op jit(solution)/shard_map/ppermute | solution.py:28
  281.1 14.5 %collective-permute-start.6 = (bf16[128,256]{1,0:T(8,128)(2,1)S(1)}, bf16[128,256]{1,0:T(8,128)(2,1)}, u32[]{:S(2)}, u32[]{:S(2)}) collective-permute-start(bf16[128,256]{1,0:T(8,128)(2,1)S(1)} %pad_maximum_fusion.2), channel_id=1, source_target_pairs={{0,3},{1,4},{2,5},{3,6},{4,7},{5,8},{6,9},{7,10},{8,11},{9,12},{10... | collective-permute-start | bytes 196616 | tf_op jit(solution)/shard_map/ppermute | solution.py:28
  284.5 12.0 %collective-permute-start.7 = (bf16[128,256]{1,0:T(8,128)(2,1)S(1)}, bf16[128,256]{1,0:T(8,128)(2,1)}, u32[]{:S(2)}, u32[]{:S(2)}) collective-permute-start(bf16[128,256]{1,0:T(8,128)(2,1)S(1)} %pad_maximum_fusion.2), channel_id=1, source_target_pairs={{0,2},{1,3},{2,4},{3,5},{4,6},{5,7},{6,8},{7,9},{8,10},{9,11},{10,... | collective-permute-start | bytes 196616 | tf_op jit(solution)/shard_map/ppermute | solution.py:28
  286.4 10.9 %collective-permute-start.8 = (bf16[128,256]{1,0:T(8,128)(2,1)S(1)}, bf16[128,256]{1,0:T(8,128)(2,1)S(1)}, u32[]{:S(2)}, u32[]{:S(2)}) collective-permute-start(bf16[128,256]{1,0:T(8,128)(2,1)S(1)} %pad_maximum_fusion.2), channel_id=1, source_target_pairs={{0,1},{1,2},{2,3},{3,4},{4,5},{5,6},{6,7},{7,8},{8,9},{9,10},{10,1... | collective-permute-start | bytes 196616 | tf_op jit(solution)/shard_map/ppermute | solution.py:28
  292.1 1.6 copy-start.1
  297.4 2.2 copy-start.5
  299.7 8.6 %collective-permute-start.9 = (bf16[128,512]{1,0:T(8,128)(2,1)S(1)}, bf16[128,512]{1,0:T(8,128)(2,1)}, u32[]{:S(2)}, u32[]{:S(2)}) collective-permute-start(bf16[128,512]{1,0:T(8,128)(2,1)S(1)} %copy.38), channel_id=1, source_target_pairs={{192,0},{0,64},{64,128},{128,192},{193,1},{1,65},{65,129},{129,193... | collective-permute-start | bytes 393224 | tf_op jit(solution)/shard_map/ppermute | solution.py:22
  301.4 8.4 %collective-permute-start.10 = (bf16[128,512]{1,0:T(8,128)(2,1)S(1)}, bf16[128,512]{1,0:T(8,128)(2,1)S(1)}, u32[]{:S(2)}, u32[]{:S(2)}) collective-permute-start(bf16[128,512]{1,0:T(8,128)(2,1)S(1)} %copy.40), channel_id=1, source_target_pairs={{192,0},{0,64},{64,128},{128,192},{193,1},{1,65},{65,129},{129,193... | collective-permute-start | bytes 393224 | tf_op jit(solution)/shard_map/ppermute | solution.py:22
Sparse Core Ops, SparseCore 0:
  39.6 127.1 all-gather.1
